TPU v7x, 512 devices: a whole 4x8x8 slice. The times are simulated.
512 devices in a mesh: dir: 4 (over y_hi, core), chan: 128 (over z, y_lo, x).
Axes of the slice: x: 4, y: 8 (y_hi: 2, y_lo: 4; y = y_hi * 4 + y_lo), z: 8, core: 2. Of those that a mesh axis runs over, the one named last changes fastest.
Arguments:
- visibilities: float32 [256, 1, 2, 2, 2850], P('chan'), may hold values from -6 to 6
- model: bfloat16 [32, 256, 1, 2, 2, 2850], P('dir', 'chan'), may hold values from -4 to 4
- gains: float32 [32, 256, 2, 2, 76], P('dir', 'chan'), may hold values from -1 to 1
- weights: float32 [256], P('chan'), may hold values from 0.2 to 5
- widths: int32 [256], P('chan'), may hold values from 1 to 2
- baseline_table: int32 [2, 2850], replicated, may hold values from 0 to 75, as said below
Outputs:
- new_gains: float32 [32, 256, 2, 2, 76], P('dir', 'chan')
- residual: float32 [256, 1, 2, 2, 2850], P('chan')
Inputs may be any that keep to these rules, and one draw needn't show every extreme that they name: `baseline_table`: each column names two different stations; every unordered pair of stations appears in exactly one column.
All inputs are finite; a program needn't handle non-finite values.
Results may differ from a plain program's by a relative error of at most 0.00035.
Values sent between devices are 32-bit elements; how exact they have to be, the bound alone decides.
No kernel may reach another device: no remote copies, remote signals or barrier semaphores. Data moves between devices by JAX's collectives and lax.ppermute only.
A program may use at most 64 MiB of HBM per device.

v0:
```python
import jax
import jax.numpy as jnp
from jax import lax
from jax.sharding import PartitionSpec as P

STATIONS = 76
SPAN = 2
ITERS = 2


step_size = 0.6
epsilon = 1e-06
highest = lax.Precision.HIGHEST


def extended(cells, sides, width):
    for axis, dim in sides:
        count = lax.axis_size(axis)
        ends = count - 1
        head = lax.slice_in_dim(cells, 0, width, axis=dim)
        tail = lax.slice_in_dim(cells, cells.shape[dim] - width, cells.shape[dim], axis=dim)
        cells = jnp.concatenate(
            [
                lax.ppermute(tail, axis, [(i, (i + 1) % count) for i in range(ends)]),
                cells,
                lax.ppermute(head, axis, [((i + 1) % count, i) for i in range(ends)]),
            ],
            axis=dim,
        )
    return cells


def station_tables(baseline_table):
    column = jnp.arange(STATIONS, dtype=jnp.int32)[:, None]
    left_hot = (baseline_table[0][None, :] == column).astype(jnp.float32)
    right_hot = (baseline_table[1][None, :] == column).astype(jnp.float32)
    return (left_hot, right_hot)


def corrupt(gains, model, left_hot, right_hot):
    model = model.astype(jnp.float32)
    left_gain = jnp.matmul(gains, left_hot, precision=highest)[:, None]
    right_gain = jnp.matmul(gains, right_hot, precision=highest)[:, None]
    left_re, left_im = (left_gain[..., 0, :], left_gain[..., 1, :])
    right_re, right_im = (right_gain[..., 0, :], right_gain[..., 1, :])
    model_re, model_im = (model[..., 0, :], model[..., 1, :])
    inner_re = left_re * model_re - left_im * model_im
    inner_im = left_re * model_im + left_im * model_re
    outer_re = inner_re * right_re + inner_im * right_im
    outer_im = inner_im * right_re - inner_re * right_im
    return (jnp.stack([outer_re, outer_im], axis=-2), (left_re, left_im, right_re, right_im))


def solve(gains, model, corrupted_model, parts, residual, left_hot, right_hot):
    model = model.astype(jnp.float32)
    left_re, left_im, right_re, right_im = parts
    target = residual + corrupted_model
    target_re, target_im = (target[..., 0, :], target[..., 1, :])
    model_re, model_im = (model[..., 0, :], model[..., 1, :])
    weighted_re = target_re * model_re + target_im * model_im
    weighted_im = target_im * model_re - target_re * model_im
    left_num_re = weighted_re * right_re - weighted_im * right_im
    left_num_im = weighted_re * right_im + weighted_im * right_re
    right_num_re = weighted_re * left_re + weighted_im * left_im
    right_num_im = weighted_re * left_im - weighted_im * left_re
    power = model_re * model_re + model_im * model_im
    left_den = power * (right_re * right_re + right_im * right_im)
    right_den = power * (left_re * left_re + left_im * left_im)
    left_products = jnp.sum(jnp.stack([left_num_re, left_num_im, left_den], axis=3), axis=1)
    right_terms = jnp.sum(jnp.stack([right_num_re, right_num_im, right_den], axis=3), axis=1)
    totals = jnp.matmul(left_products, left_hot.T, precision=highest) + jnp.matmul(
        right_terms, right_hot.T, precision=highest
    )
    solved = totals[:, :, 0:2] / (totals[:, :, 2:3] + epsilon)
    return (1.0 - step_size) * gains + step_size * solved


def smooth(padded_gains, padded_weights, widths):
    count = widths.shape[0]
    half_width = widths.astype(jnp.float32) * 0.5
    numer = jnp.zeros((padded_gains.shape[0], count) + padded_gains.shape[2:], jnp.float32)
    denom = jnp.zeros((count,), jnp.float32)
    for offset in range(-SPAN, SPAN + 1):
        ratio = offset / half_width
        kernel = jnp.exp(-0.5 * ratio * ratio) * (widths >= abs(offset)).astype(jnp.float32)
        weight_here = kernel * padded_weights[SPAN + offset : SPAN + offset + count]
        numer = (
            numer
            + weight_here[None, :, None, None, None]
            * padded_gains[:, SPAN + offset : SPAN + offset + count]
        )
        denom = denom + weight_here
    return numer / denom[None, :, None, None, None]


def on_device(visibilities, model, gains, weights, widths, baseline_table):
    left_hot, right_hot = station_tables(baseline_table)
    padded_weights = extended(weights, (("chan", 0),), SPAN)
    current = gains
    residual = visibilities
    corrupt_all = jax.vmap(corrupt, in_axes=(0, 0, None, None))
    solve_all = jax.vmap(solve, in_axes=(0, 0, 0, 0, None, None, None))
    for sweep in range(ITERS):
        corrupted_model, parts = corrupt_all(current, model, left_hot, right_hot)
        partial_total = jnp.sum(corrupted_model, axis=0)
        total = lax.psum(partial_total, "dir")
        residual = visibilities - total
        stepped = solve_all(current, model, corrupted_model, parts, residual, left_hot, right_hot)
        padded_gains = extended(stepped, (("chan", 1),), SPAN)
        current = smooth(padded_gains, padded_weights, widths)
    return (current, residual)


def solution(mesh):
    placed = (
        P("chan", None, None, None, None),
        P("dir", "chan", None, None, None, None),
        P("dir", "chan", None, None, None),
        P("chan"),
        P("chan"),
        P(),
    )
    return jax.shard_map(
        on_device,
        mesh=mesh,
        in_specs=placed,
        out_specs=(P("dir", "chan", None, None, None), P("chan", None, None, None, None)),
        check_vma=False,
    )
```

profile of v0, /device:TPU:222, one launch (start us, length us, event | category | flops | bytes accessed | tf_op | source)
XLA Modules:
  0.0 184.8 jit_solution(1795756025087227704)
XLA Ops:
  7.2 0.0 all-reduce.3.cloned.1.call-start
  7.2 5.1 %collective-permute-start = (f32[2]{0:T(128)}, f32[2]{0:T(128)S(1)}, u32[]{:S(2)}, u32[]{:S(2)}) collective-permute-start(f32[2]{0:T(128)} %param.9), channel_id=1, source_target_pairs={{0,1},{1,2},{2,3},{3,4},{4,5},{5,6},{6,7},{7,8},{8,9},{9,10},{10,1... | collective-permute-start | bytes 32 | tf_op jit(solution)/shard_map/ppermute | solution.py:24
  12.3 1.9 %collective-permute-start.2 = (f32[2]{0:T(128)}, f32[2]{0:T(128)S(1)}, u32[]{:S(2)}, u32[]{:S(2)}) collective-permute-start(f32[2]{0:T(128)} %param.9), channel_id=1, source_target_pairs={{1,0},{2,1},{3,2},{4,3},{5,4},{6,5},{7,6},{8,7},{9,8},{10,9},{11,1... | collective-permute-start | bytes 32 | tf_op jit(solution)/shard_map/ppermute | solution.py:26
  14.2 0.9 slice_reduce_fusion.1
  15.1 1.3 convolution_bitcast_fusion.2
  16.5 0.5 convolution_bitcast_fusion.3
  17.0 0.4 copy-done
  17.5 0.1 copy_convert_fusion
  17.5 0.2 multiply_add_fusion.9
  17.7 0.1 multiply_subtract_fusion.8
  17.8 0.0 copy-start.10
  17.8 0.9 fusion.35
  18.7 0.0 all-reduce.3.cloned.1.call-update
  18.7 0.0 all-reduce.5.cloned.1.call-start
  18.7 5.1 %collective-permute-done.2 = f32[2]{0:T(128)S(1)} collective-permute-done((f32[2]{0:T(128)}, f32[2]{0:T(128)S(1)}, u32[]{:S(2)}, u32[]{:S(2)}) %collective-permute-start.2) | collective-permute-done | bytes 40 | tf_op jit(solution)/shard_map/ppermute | solution.py:26
  23.9 0.1 pad_maximum_fusion.7
  23.9 54.3 %all-reduce.3.cloned.1.call-done = f32[2,1,2,2,2850]{4,3,2,1,0:T(2,128)} async-done(((f32[2,1,2,2,2850]{4,3,2,1,0:T(2,128)}), f32[2,1,2,2,2850]{4,3,2,1,0:T(2,128)}) %all-reduce.3.cloned.1.call-update) | async-done | bytes 91216 | tf_op jit(solution)/shard_map/psum | solution.py:106
  78.3 0.9 subtract_bitcast_fusion
  79.2 0.1 fusion.34
  79.3 0.2 multiply_add_fusion.5
  79.5 0.2 multiply_subtract_fusion.6
  79.7 0.8 fusion
  80.5 0.8 fusion.21
  81.3 7.3 %collective-permute-start.1 = (f32[8,2,2,2,76]{4,0,3,2,1:T(8,128)S(1)}, f32[8,2,2,2,76]{4,0,3,2,1:T(8,128)S(1)}, u32[]{:S(2)}, u32[]{:S(2)}) collective-permute-start(f32[8,2,2,2,76]{4,0,3,2,1:T(8,128)S(1)} %fusion.61), channel_id=1, source_target_pairs={{0,1},{1,2},{2,3},{3,4},{4,5},{5,6},{6,7},{7,8},{8,9},{9,10},{10,1... | collective-permute-start | bytes 58376 | tf_op jit(solution)/shard_map/ppermute | solution.py:24
  88.6 1.9 %collective-permute-start.3 = (f32[8,2,2,2,76]{4,0,3,2,1:T(8,128)S(1)}, f32[8,2,2,2,76]{4,0,3,2,1:T(8,128)S(1)}, u32[]{:S(2)}, u32[]{:S(2)}) collective-permute-start(f32[8,2,2,2,76]{4,0,3,2,1:T(8,128)S(1)} %fusion.61), channel_id=1, source_target_pairs={{1,0},{2,1},{3,2},{4,3},{5,4},{6,5},{7,6},{8,7},{9,8},{10,9},{11,1... | collective-permute-start | bytes 58376 | tf_op jit(solution)/shard_map/ppermute | solution.py:26
  90.6 0.1 add_add_fusion
  90.7 9.8 %collective-permute-done.3 = f32[8,2,2,2,76]{4,0,3,2,1:T(8,128)S(1)} collective-permute-done((f32[8,2,2,2,76]{4,0,3,2,1:T(8,128)S(1)}, f32[8,2,2,2,76]{4,0,3,2,1:T(8,128)S(1)}, u32[]{:S(2)}, u32[]{:S(2)}) %collective-permute-start.3) | collective-permute-done | bytes 19488 | tf_op jit(solution)/shard_map/ppermute | solution.py:26
  100.5 0.1 fusion.56
  100.6 0.5 convolution_bitcast_fusion
  101.1 0.5 convolution_bitcast_fusion.1
  101.7 0.2 multiply_add_fusion.3
  101.8 0.1 multiply_subtract_fusion.3
  101.9 0.9 fusion.33
  102.8 0.0 all-reduce.5.cloned.1.call-update
  102.8 51.6 %all-reduce.5.cloned.1.call-done = f32[2,1,2,2,2850]{4,3,2,1,0:T(2,128)} async-done(((f32[2,1,2,2,2850]{4,3,2,1,0:T(2,128)}), f32[2,1,2,2,2850]{4,3,2,1,0:T(2,128)}) %all-reduce.5.cloned.1.call-update) | async-done | bytes 91216 | tf_op jit(solution)/shard_map/psum | solution.py:106
  154.4 0.9 sub.90
  155.4 0.0 copy-start.2
  155.4 0.1 fusion.32
  155.5 0.5 copy-done.2
  156.0 0.2 multiply_add_fusion
  156.2 0.2 multiply_subtract_fusion
  156.4 0.8 fusion.10
  157.3 0.8 fusion.20
  158.1 7.3 %collective-permute-start.4 = (f32[8,2,2,2,76]{4,0,3,2,1:T(8,128)S(1)}, f32[8,2,2,2,76]{4,0,3,2,1:T(8,128)S(1)}, u32[]{:S(2)}, u32[]{:S(2)}) collective-permute-start(f32[8,2,2,2,76]{4,0,3,2,1:T(8,128)S(1)} %fusion.52), channel_id=1, source_target_pairs={{0,1},{1,2},{2,3},{3,4},{4,5},{5,6},{6,7},{7,8},{8,9},{9,10},{10,1... | collective-permute-start | bytes 58376 | tf_op jit(solution)/shard_map/ppermute | solution.py:24
  165.4 1.9 %collective-permute-start.5 = (f32[8,2,2,2,76]{4,0,3,2,1:T(8,128)S(1)}, f32[8,2,2,2,76]{4,0,3,2,1:T(8,128)S(1)}, u32[]{:S(2)}, u32[]{:S(2)}) collective-permute-start(f32[8,2,2,2,76]{4,0,3,2,1:T(8,128)S(1)} %fusion.52), channel_id=1, source_target_pairs={{1,0},{2,1},{3,2},{4,3},{5,4},{6,5},{7,6},{8,7},{9,8},{10,9},{11,1... | collective-permute-start | bytes 58376 | tf_op jit(solution)/shard_map/ppermute | solution.py:26
  167.3 9.9 %collective-permute-done.5 = f32[8,2,2,2,76]{4,0,3,2,1:T(8,128)S(1)} collective-permute-done((f32[8,2,2,2,76]{4,0,3,2,1:T(8,128)S(1)}, f32[8,2,2,2,76]{4,0,3,2,1:T(8,128)S(1)}, u32[]{:S(2)}, u32[]{:S(2)}) %collective-permute-start.5) | collective-permute-done | bytes 19488 | tf_op jit(solution)/shard_map/ppermute | solution.py:26
  177.2 0.1 fusion.47
  177.3 0.6 copy.12
  (27 shorter events, 0.1 us)
Async XLA Ops:
  7.2 71.1 %all-reduce.3.cloned.1.call-start = ((), (), s32[]{:S(2)}) async-start(), calls=%async_computation | async-start | bytes 188416 | tf_op jit(solution)/shard_map/psum | solution.py:106
  7.2 11.5 %collective-permute-start = (f32[2]{0:T(128)}, f32[2]{0:T(128)S(1)}, u32[]{:S(2)}, u32[]{:S(2)}) collective-permute-start(f32[2]{0:T(128)} %param.9), channel_id=1, source_target_pairs={{0,1},{1,2},{2,3},{3,4},{4,5},{5,6},{6,7},{7,8},{8,9},{9,10},{10,1... | collective-permute-start | bytes 32 | tf_op jit(solution)/shard_map/ppermute | solution.py:24
  12.3 11.6 %collective-permute-start.2 = (f32[2]{0:T(128)}, f32[2]{0:T(128)S(1)}, u32[]{:S(2)}, u32[]{:S(2)}) collective-permute-start(f32[2]{0:T(128)} %param.9), channel_id=1, source_target_pairs={{1,0},{2,1},{3,2},{4,3},{5,4},{6,5},{7,6},{8,7},{9,8},{10,9},{11,1... | collective-permute-start | bytes 32 | tf_op jit(solution)/shard_map/ppermute | solution.py:26
  15.1 1.4 copy-start.3
  16.5 1.0 copy-start
  17.8 6.1 %copy-start.10 = (f32[2]{0:T(128)S(1)}, f32[2]{0:T(128)}, u32[]{:S(2)}) copy-start(f32[2]{0:T(128)} %param.9) | copy-start | bytes 28
  17.8 60.5 %copy-start.1 = (f32[2,1,2,2,2850]{4,3,2,1,0:T(2,128)S(1)}, f32[2,1,2,2,2850]{4,3,2,1,0:T(2,128)}, u32[]{:S(2)}) copy-start(f32[2,1,2,2,2850]{4,3,2,1,0:T(2,128)} %param.6) | copy-start | bytes 273604
  18.7 135.8 %all-reduce.5.cloned.1.call-start = ((), (), s32[]{:S(2)}) async-start(), calls=%async_computation.1 | async-start | bytes 188416 | tf_op jit(solution)/shard_map/psum | solution.py:106
  80.5 10.1 %copy-start.11 = (s32[2]{0:T(128)S(1)}, s32[2]{0:T(128)}, u32[]{:S(2)}) copy-start(s32[2]{0:T(128)} %param.10) | copy-start | bytes 28
  81.3 9.3 %collective-permute-start.1 = (f32[8,2,2,2,76]{4,0,3,2,1:T(8,128)S(1)}, f32[8,2,2,2,76]{4,0,3,2,1:T(8,128)S(1)}, u32[]{:S(2)}, u32[]{:S(2)}) collective-permute-start(f32[8,2,2,2,76]{4,0,3,2,1:T(8,128)S(1)} %fusion.61), channel_id=1, source_target_pairs={{0,1},{1,2},{2,3},{3,4},{4,5},{5,6},{6,7},{7,8},{8,9},{9,10},{10,1... | collective-permute-start | bytes 58376 | tf_op jit(solution)/shard_map/ppermute | solution.py:24
  88.6 11.8 %collective-permute-start.3 = (f32[8,2,2,2,76]{4,0,3,2,1:T(8,128)S(1)}, f32[8,2,2,2,76]{4,0,3,2,1:T(8,128)S(1)}, u32[]{:S(2)}, u32[]{:S(2)}) collective-permute-start(f32[8,2,2,2,76]{4,0,3,2,1:T(8,128)S(1)} %fusion.61), channel_id=1, source_target_pairs={{1,0},{2,1},{3,2},{4,3},{5,4},{6,5},{7,6},{8,7},{9,8},{10,9},{11,1... | collective-permute-start | bytes 58376 | tf_op jit(solution)/shard_map/ppermute | solution.py:26
  90.7 9.8 %copy-start.4 = (f32[2]{0:T(128)}, f32[2]{0:T(128)S(1)}, u32[]{:S(2)}) copy-start(f32[2]{0:T(128)S(1)} %get-tuple-element.15) | copy-start | bytes 28
  90.7 9.8 %copy-start.6 = (f32[2]{0:T(128)}, f32[2]{0:T(128)S(1)}, u32[]{:S(2)}) copy-start(f32[2]{0:T(128)S(1)} %get-tuple-element.16) | copy-start | bytes 28
  90.7 9.8 %copy-start.8 = (f32[2]{0:T(128)}, f32[2]{0:T(128)S(1)}, u32[]{:S(2)}) copy-start(f32[2]{0:T(128)S(1)} %get-tuple-element.17) | copy-start | bytes 28
  155.4 0.6 copy-start.2
  157.2 20.0 %copy-start.5 = (f32[2]{0:T(128)S(1)}, f32[2]{0:T(128)}, u32[]{:S(2)}) copy-start(f32[2]{0:T(128)} %copy-done.4) | copy-start | bytes 28
  157.2 20.0 %copy-start.7 = (f32[2]{0:T(128)S(1)}, f32[2]{0:T(128)}, u32[]{:S(2)}) copy-start(f32[2]{0:T(128)} %copy-done.6) | copy-start | bytes 28
  157.2 20.0 %copy-start.9 = (f32[2]{0:T(128)S(1)}, f32[2]{0:T(128)}, u32[]{:S(2)}) copy-start(f32[2]{0:T(128)} %copy-done.8) | copy-start | bytes 28
  158.1 9.2 %collective-permute-start.4 = (f32[8,2,2,2,76]{4,0,3,2,1:T(8,128)S(1)}, f32[8,2,2,2,76]{4,0,3,2,1:T(8,128)S(1)}, u32[]{:S(2)}, u32[]{:S(2)}) collective-permute-start(f32[8,2,2,2,76]{4,0,3,2,1:T(8,128)S(1)} %fusion.52), channel_id=1, source_target_pairs={{0,1},{1,2},{2,3},{3,4},{4,5},{5,6},{6,7},{7,8},{8,9},{9,10},{10,1... | collective-permute-start | bytes 58376 | tf_op jit(solution)/shard_map/ppermute | solution.py:24
  165.4 11.8 %collective-permute-start.5 = (f32[8,2,2,2,76]{4,0,3,2,1:T(8,128)S(1)}, f32[8,2,2,2,76]{4,0,3,2,1:T(8,128)S(1)}, u32[]{:S(2)}, u32[]{:S(2)}) collective-permute-start(f32[8,2,2,2,76]{4,0,3,2,1:T(8,128)S(1)} %fusion.52), channel_id=1, source_target_pairs={{1,0},{2,1},{3,2},{4,3},{5,4},{6,5},{7,6},{8,7},{9,8},{10,9},{11,1... | collective-permute-start | bytes 58376 | tf_op jit(solution)/shard_map/ppermute | solution.py:26
Sparse Core Ops, SparseCore 0:
  18.8 59.3 all-reduce.2
  102.9 51.4 all-reduce.4
where the time goes:
time: 185 us
  waiting for transfers between devices  131 us (71%)
  starting transfers between devices  25.5 us (14%)
  between operations  14.4 us (8%)
  matrix products  6.06 us (3%)
  other arithmetic  5.51 us (3%)
  local copies, waits for them, and re-layouts  2.55 us (1%)
    psum x2, waiting for transfers between devices, on_device(): total = lax.psum(partial_total, 'dir')  106 us
    ppermute x3, waiting for transfers between devices, extended(): lax.ppermute(head, axis, [((i + 1) % count, i) for i in range(ends)])  24.8 us
    ppermute x3, starting transfers between devices, extended(): lax.ppermute(tail, axis, [(i, (i + 1) % count) for i in range(ends)])  19.7 us
    ppermute x3, starting transfers between devices, extended(): lax.ppermute(head, axis, [((i + 1) % count, i) for i in range(ends)])  5.76 us
  transfers between devices with their start and end apart: 8, of which 5 were waited for; matrix products, arithmetic and copies ran while one was open for 2% of the time, Pallas kernels for 0%

commit v1 on v0

--- a/solution.py
+++ b/solution.py
@@ -28,6 +28,15 @@
             axis=dim,
         )
     return cells
+
+
+def sum_over_dir(partial):
+    count = lax.axis_size("dir")
+    swapped = [
+        lax.ppermute(partial, "dir", [(i, i ^ mask) for i in range(count)])
+        for mask in (1, 2, 3)
+    ]
+    return (partial + swapped[0]) + (swapped[1] + swapped[2])
 
 
 def station_tables(baseline_table):
@@ -103,7 +112,7 @@
     for sweep in range(ITERS):
         corrupted_model, parts = corrupt_all(current, model, left_hot, right_hot)
         partial_total = jnp.sum(corrupted_model, axis=0)
-        total = lax.psum(partial_total, "dir")
+        total = sum_over_dir(partial_total)
         residual = visibilities - total
         stepped = solve_all(current, model, corrupted_model, parts, residual, left_hot, right_hot)
         padded_gains = extended(stepped, (("chan", 1),), SPAN)

time: 185 us -> 88.2 us (0.48)
  waiting for transfers between devices: 131 us -> 33.7 us
  starting transfers between devices: 25.5 us -> 41.9 us
  between operations: 14.4 us -> 1 us
  other arithmetic: 5.51 us -> 2.44 us
    psum x2 -> x0, waiting for transfers between devices: 106 us -> none  [on_device(): total = lax.psum(partial_total, 'dir')]
    ppermute x0 -> x6, starting transfers between devices: none -> 23.1 us  [sum_over_dir(): lax.ppermute(partial, 'dir', [(i, i ^ mask) for i in range(count)])]
    ppermute x3, starting transfers between devices: 19.7 us -> 9.09 us  [extended(): lax.ppermute(tail, axis, [(i, (i + 1) % count) for i in range(ends)])]
    ppermute x0 -> x6, waiting for transfers between devices: none -> 8.46 us  [sum_over_dir(): lax.ppermute(partial, 'dir', [(i, i ^ mask) for i in range(count)])]
    ppermute x3, starting transfers between devices: 5.76 us -> 9.76 us  [extended(): lax.ppermute(head, axis, [((i + 1) % count, i) for i in range(ends)])]
  transfers between devices with their start and end apart: 8 -> 12, of which waited for: 5 -> 5; matrix products, arithmetic and copies ran while one was open for 2% -> 0% of each run, Pallas kernels for 0% -> 0%
where the time goes in v1:
time: 88.2 us; the launch traced here: 87.6 us
  starting transfers between devices  41.9 us (48%)
  waiting for transfers between devices  33.7 us (38%)
  matrix products  6.07 us (7%)
  local copies, waits for them, and re-layouts  2.52 us (3%)
  other arithmetic  2.44 us (3%)
  between operations  1 us (1%)
    ppermute x3, waiting for transfers between devices, extended(): lax.ppermute(head, axis, [((i + 1) % count, i) for i in range(ends)])  25.2 us
    ppermute x6, starting transfers between devices, sum_over_dir(): lax.ppermute(partial, 'dir', [(i, i ^ mask) for i in range(count)])  23.1 us
    ppermute x3, starting transfers between devices, extended(): lax.ppermute(head, axis, [((i + 1) % count, i) for i in range(ends)])  9.76 us
    ppermute x3, starting transfers between devices, extended(): lax.ppermute(tail, axis, [(i, (i + 1) % count) for i in range(ends)])  9.09 us
    ppermute x6, waiting for transfers between devices, sum_over_dir(): lax.ppermute(partial, 'dir', [(i, i ^ mask) for i in range(count)])  8.46 us
    dot_general x2, matrix products, corrupt(): right_gain = jnp.matmul(gains, right_hot, precision=highest)[:, None]  1.9 us
  transfers between devices with their start and end apart: 12, of which 5 were waited for; matrix products, arithmetic and copies ran while one was open for 0% of the time, Pallas kernels for 0%

profile of v1, /device:TPU:222, one launch (start us, length us, event | category | flops | bytes accessed | tf_op | source)
XLA Modules:
  0.0 87.6 jit_solution(15030354255224661081)
XLA Ops:
  0.6 0.9 slice_reduce_fusion.1
  1.5 1.3 %convolution_bitcast_fusion.2 = f32[8,2,1,2,2,2850]{5,0,4,3,1,2:T(8,128)S(1)} fusion(s32[2850]{0:T(1024)S(1)} %get-tuple-element.5, f32[8,2,2,2,76]{4,3,2,1,0:T(2,128)} %param.8), kind=kOutput, calls=%fused_computation.2 | convolution fusion | flops 166565408 | bytes 760456 | tf_op jit(solution)/shard_map/vmap()/dot_general | solution.py:52
  2.9 0.5 convolution_bitcast_fusion.3
  3.4 0.4 copy-done
  3.9 0.1 copy_convert_fusion
  3.9 0.1 multiply_add_fusion.9
  4.1 0.1 multiply_subtract_fusion.8
  4.2 0.2 fusion.35
  4.4 1.9 %collective-permute-start.1 = (f32[2,1,2,2,2850]{4,3,2,1,0:T(2,128)S(1)}, f32[2,1,2,2,2850]{4,3,2,1,0:T(2,128)S(1)}, u32[]{:S(2)}, u32[]{:S(2)}) collective-permute-start(f32[2,1,2,2,2850]{4,3,2,1,0:T(2,128)S(1)} %bitcast.58), channel_id=1, source_target_pairs={{0,128},{128,0},{256,384},{384,256},{1,129},{129,1},{257,385},{385... | collective-permute-start | bytes 273608 | tf_op jit(solution)/shard_map/ppermute | solution.py:36
  6.3 5.0 %collective-permute-start.2 = (f32[2,1,2,2,2850]{4,3,2,1,0:T(2,128)S(1)}, f32[2,1,2,2,2850]{4,3,2,1,0:T(2,128)S(1)}, u32[]{:S(2)}, u32[]{:S(2)}) collective-permute-start(f32[2,1,2,2,2850]{4,3,2,1,0:T(2,128)S(1)} %bitcast.59), channel_id=1, source_target_pairs={{0,256},{128,384},{256,0},{384,128},{1,257},{129,385},{257,1},{385... | collective-permute-start | bytes 273608 | tf_op jit(solution)/shard_map/ppermute | solution.py:36
  11.4 4.5 %collective-permute-start.3 = (f32[2,1,2,2,2850]{4,3,2,1,0:T(2,128)S(1)}, f32[2,1,2,2,2850]{4,3,2,1,0:T(2,128)S(1)}, u32[]{:S(2)}, u32[]{:S(2)}) collective-permute-start(f32[2,1,2,2,2850]{4,3,2,1,0:T(2,128)S(1)} %bitcast.60), channel_id=1, source_target_pairs={{0,384},{128,256},{256,128},{384,0},{1,385},{129,257},{257,129},{3... | collective-permute-start | bytes 273608 | tf_op jit(solution)/shard_map/ppermute | solution.py:36
  15.9 5.2 %collective-permute-start = (f32[2]{0:T(128)S(1)}, f32[2]{0:T(128)S(1)}, u32[]{:S(2)}, u32[]{:S(2)}) collective-permute-start(f32[2]{0:T(128)S(1)} %copy-done.4), channel_id=1, source_target_pairs={{0,1},{1,2},{2,3},{3,4},{4,5},{5,6},{6,7},{7,8},{8,9},{9,10},{10,1... | collective-permute-start | bytes 32 | tf_op jit(solution)/shard_map/ppermute | solution.py:24
  21.2 1.9 %collective-permute-start.5 = (f32[2]{0:T(128)S(1)}, f32[2]{0:T(128)S(1)}, u32[]{:S(2)}, u32[]{:S(2)}) collective-permute-start(f32[2]{0:T(128)S(1)} %copy-done.4), channel_id=1, source_target_pairs={{1,0},{2,1},{3,2},{4,3},{5,4},{6,5},{7,6},{8,7},{9,8},{10,9},{11,1... | collective-permute-start | bytes 32 | tf_op jit(solution)/shard_map/ppermute | solution.py:26
  23.1 9.5 %collective-permute-done.5 = f32[2]{0:T(128)S(1)} collective-permute-done((f32[2]{0:T(128)S(1)}, f32[2]{0:T(128)S(1)}, u32[]{:S(2)}, u32[]{:S(2)}) %collective-permute-start.5) | collective-permute-done | bytes 40 | tf_op jit(solution)/shard_map/ppermute | solution.py:26
  32.6 0.1 pad_maximum_fusion.7
  32.7 0.1 subtract_bitcast_fusion
  32.9 0.1 fusion.34
  33.0 0.2 multiply_add_fusion.5
  33.2 0.2 multiply_subtract_fusion.6
  33.4 0.8 fusion
  34.2 0.8 fusion.21
  35.0 1.9 %collective-permute-start.4 = (f32[8,2,2,2,76]{4,0,3,2,1:T(8,128)S(1)}, f32[8,2,2,2,76]{4,0,3,2,1:T(8,128)S(1)}, u32[]{:S(2)}, u32[]{:S(2)}) collective-permute-start(f32[8,2,2,2,76]{4,0,3,2,1:T(8,128)S(1)} %fusion.61), channel_id=1, source_target_pairs={{0,1},{1,2},{2,3},{3,4},{4,5},{5,6},{6,7},{7,8},{8,9},{9,10},{10,1... | collective-permute-start | bytes 58376 | tf_op jit(solution)/shard_map/ppermute | solution.py:24
  36.9 3.9 %collective-permute-start.6 = (f32[8,2,2,2,76]{4,0,3,2,1:T(8,128)S(1)}, f32[8,2,2,2,76]{4,0,3,2,1:T(8,128)S(1)}, u32[]{:S(2)}, u32[]{:S(2)}) collective-permute-start(f32[8,2,2,2,76]{4,0,3,2,1:T(8,128)S(1)} %fusion.61), channel_id=1, source_target_pairs={{1,0},{2,1},{3,2},{4,3},{5,4},{6,5},{7,6},{8,7},{9,8},{10,9},{11,1... | collective-permute-start | bytes 58376 | tf_op jit(solution)/shard_map/ppermute | solution.py:26
  40.8 0.1 add_add_fusion
  40.9 7.8 %collective-permute-done.6 = f32[8,2,2,2,76]{4,0,3,2,1:T(8,128)S(1)} collective-permute-done((f32[8,2,2,2,76]{4,0,3,2,1:T(8,128)S(1)}, f32[8,2,2,2,76]{4,0,3,2,1:T(8,128)S(1)}, u32[]{:S(2)}, u32[]{:S(2)}) %collective-permute-start.6) | collective-permute-done | bytes 19488 | tf_op jit(solution)/shard_map/ppermute | solution.py:26
  48.7 0.1 fusion.56
  48.8 0.5 convolution_bitcast_fusion
  49.4 0.5 convolution_bitcast_fusion.1
  49.9 0.1 multiply_add_fusion.3
  50.1 0.1 multiply_subtract_fusion.3
  50.1 0.2 fusion.33
  50.4 1.9 %collective-permute-start.7 = (f32[2,1,2,2,2850]{4,3,2,1,0:T(2,128)S(1)}, f32[2,1,2,2,2850]{4,3,2,1,0:T(2,128)S(1)}, u32[]{:S(2)}, u32[]{:S(2)}) collective-permute-start(f32[2,1,2,2,2850]{4,3,2,1,0:T(2,128)S(1)} %bitcast.61), channel_id=1, source_target_pairs={{0,128},{128,0},{256,384},{384,256},{1,129},{129,1},{257,385},{385... | collective-permute-start | bytes 273608 | tf_op jit(solution)/shard_map/ppermute | solution.py:36
  52.3 7.6 %collective-permute-start.8 = (f32[2,1,2,2,2850]{4,3,2,1,0:T(2,128)S(1)}, f32[2,1,2,2,2850]{4,3,2,1,0:T(2,128)S(1)}, u32[]{:S(2)}, u32[]{:S(2)}) collective-permute-start(f32[2,1,2,2,2850]{4,3,2,1,0:T(2,128)S(1)} %bitcast.62), channel_id=1, source_target_pairs={{0,256},{128,384},{256,0},{384,128},{1,257},{129,385},{257,1},{385... | collective-permute-start | bytes 273608 | tf_op jit(solution)/shard_map/ppermute | solution.py:36
  59.9 2.0 %collective-permute-start.9 = (f32[2,1,2,2,2850]{4,3,2,1,0:T(2,128)S(1)}, f32[2,1,2,2,2850]{4,3,2,1,0:T(2,128)S(1)}, u32[]{:S(2)}, u32[]{:S(2)}) collective-permute-start(f32[2,1,2,2,2850]{4,3,2,1,0:T(2,128)S(1)} %bitcast.63), channel_id=1, source_target_pairs={{0,384},{128,256},{256,128},{384,0},{1,385},{129,257},{257,129},{3... | collective-permute-start | bytes 273608 | tf_op jit(solution)/shard_map/ppermute | solution.py:36
  62.0 1.3 %collective-permute-done.8 = f32[2,1,2,2,2850]{4,3,2,1,0:T(2,128)S(1)} collective-permute-done((f32[2,1,2,2,2850]{4,3,2,1,0:T(2,128)S(1)}, f32[2,1,2,2,2850]{4,3,2,1,0:T(2,128)S(1)}, u32[]{:S(2)}, u32[]{:S(2)}) %collective-permute-start.8) | collective-permute-done | bytes 91232 | tf_op jit(solution)/shard_map/ppermute | solution.py:36
  63.3 7.1 %collective-permute-done.9 = f32[2,1,2,2,2850]{4,3,2,1,0:T(2,128)S(1)} collective-permute-done((f32[2,1,2,2,2850]{4,3,2,1,0:T(2,128)S(1)}, f32[2,1,2,2,2850]{4,3,2,1,0:T(2,128)S(1)}, u32[]{:S(2)}, u32[]{:S(2)}) %collective-permute-start.9) | collective-permute-done | bytes 91232 | tf_op jit(solution)/shard_map/ppermute | solution.py:36
  70.4 0.1 add_subtract_fusion
  70.6 0.1 fusion.32
  70.7 0.5 copy-done.1
  71.2 0.1 multiply_add_fusion
  71.3 0.2 multiply_subtract_fusion
  71.6 0.8 fusion.10
  72.3 0.8 fusion.20
  73.2 1.9 %collective-permute-start.10 = (f32[8,2,2,2,76]{4,0,3,2,1:T(8,128)S(1)}, f32[8,2,2,2,76]{4,0,3,2,1:T(8,128)S(1)}, u32[]{:S(2)}, u32[]{:S(2)}) collective-permute-start(f32[8,2,2,2,76]{4,0,3,2,1:T(8,128)S(1)} %fusion.52), channel_id=1, source_target_pairs={{0,1},{1,2},{2,3},{3,4},{4,5},{5,6},{6,7},{7,8},{8,9},{9,10},{10,1... | collective-permute-start | bytes 58376 | tf_op jit(solution)/shard_map/ppermute | solution.py:24
  75.1 3.9 %collective-permute-start.11 = (f32[8,2,2,2,76]{4,0,3,2,1:T(8,128)S(1)}, f32[8,2,2,2,76]{4,0,3,2,1:T(8,128)S(1)}, u32[]{:S(2)}, u32[]{:S(2)}) collective-permute-start(f32[8,2,2,2,76]{4,0,3,2,1:T(8,128)S(1)} %fusion.52), channel_id=1, source_target_pairs={{1,0},{2,1},{3,2},{4,3},{5,4},{6,5},{7,6},{8,7},{9,8},{10,9},{11,1... | collective-permute-start | bytes 58376 | tf_op jit(solution)/shard_map/ppermute | solution.py:26
  79.0 7.9 %collective-permute-done.11 = f32[8,2,2,2,76]{4,0,3,2,1:T(8,128)S(1)} collective-permute-done((f32[8,2,2,2,76]{4,0,3,2,1:T(8,128)S(1)}, f32[8,2,2,2,76]{4,0,3,2,1:T(8,128)S(1)}, u32[]{:S(2)}, u32[]{:S(2)}) %collective-permute-start.11) | collective-permute-done | bytes 19488 | tf_op jit(solution)/shard_map/ppermute | solution.py:26
  86.9 0.1 fusion.47
  87.0 0.6 copy.12
  (21 shorter events, 0.1 us)
Async XLA Ops:
  1.5 1.4 %copy-start.3 = (f32[8,2,2,2,76]{4,3,2,1,0:T(2,128)S(1)}, f32[8,2,2,2,76]{4,3,2,1,0:T(2,128)}, u32[]{:S(2)}) copy-start(f32[8,2,2,2,76]{4,3,2,1,0:T(2,128)} %param.8) | copy-start | bytes 58372
  2.9 1.0 %copy-start = (bf16[8,2,1,2,2,2850]{5,4,3,2,1,0:T(2,128)(2,1)S(1)}, bf16[8,2,1,2,2,2850]{5,4,3,2,1,0:T(2,128)(2,1)}, u32[]{:S(2)}) copy-start(bf16[8,2,1,2,2,2850]{5,4,3,2,1,0:T(2,128)(2,1)} %param.7) | copy-start | bytes 1094404
  4.1 11.8 %copy-start.4 = (f32[2]{0:T(128)S(1)}, f32[2]{0:T(128)}, u32[]{:S(2)}) copy-start(f32[2]{0:T(128)} %param.9) | copy-start | bytes 28
  4.2 28.6 %copy-start.2 = (f32[2,1,2,2,2850]{4,3,2,1,0:T(2,128)S(1)}, f32[2,1,2,2,2850]{4,3,2,1,0:T(2,128)}, u32[]{:S(2)}) copy-start(f32[2,1,2,2,2850]{4,3,2,1,0:T(2,128)} %param.6) | copy-start | bytes 273604
  4.4 28.3 %collective-permute-start.1 = (f32[2,1,2,2,2850]{4,3,2,1,0:T(2,128)S(1)}, f32[2,1,2,2,2850]{4,3,2,1,0:T(2,128)S(1)}, u32[]{:S(2)}, u32[]{:S(2)}) collective-permute-start(f32[2,1,2,2,2850]{4,3,2,1,0:T(2,128)S(1)} %bitcast.58), channel_id=1, source_target_pairs={{0,128},{128,0},{256,384},{384,256},{1,129},{129,1},{257,385},{385... | collective-permute-start | bytes 273608 | tf_op jit(solution)/shard_map/ppermute | solution.py:36
  6.3 26.4 %collective-permute-start.2 = (f32[2,1,2,2,2850]{4,3,2,1,0:T(2,128)S(1)}, f32[2,1,2,2,2850]{4,3,2,1,0:T(2,128)S(1)}, u32[]{:S(2)}, u32[]{:S(2)}) collective-permute-start(f32[2,1,2,2,2850]{4,3,2,1,0:T(2,128)S(1)} %bitcast.59), channel_id=1, source_target_pairs={{0,256},{128,384},{256,0},{384,128},{1,257},{129,385},{257,1},{385... | collective-permute-start | bytes 273608 | tf_op jit(solution)/shard_map/ppermute | solution.py:36
  11.4 21.3 %collective-permute-start.3 = (f32[2,1,2,2,2850]{4,3,2,1,0:T(2,128)S(1)}, f32[2,1,2,2,2850]{4,3,2,1,0:T(2,128)S(1)}, u32[]{:S(2)}, u32[]{:S(2)}) collective-permute-start(f32[2,1,2,2,2850]{4,3,2,1,0:T(2,128)S(1)} %bitcast.60), channel_id=1, source_target_pairs={{0,384},{128,256},{256,128},{384,0},{1,385},{129,257},{257,129},{3... | collective-permute-start | bytes 273608 | tf_op jit(solution)/shard_map/ppermute | solution.py:36
  15.9 7.2 %collective-permute-start = (f32[2]{0:T(128)S(1)}, f32[2]{0:T(128)S(1)}, u32[]{:S(2)}, u32[]{:S(2)}) collective-permute-start(f32[2]{0:T(128)S(1)} %copy-done.4), channel_id=1, source_target_pairs={{0,1},{1,2},{2,3},{3,4},{4,5},{5,6},{6,7},{7,8},{8,9},{9,10},{10,1... | collective-permute-start | bytes 32 | tf_op jit(solution)/shard_map/ppermute | solution.py:24
  21.2 11.5 %collective-permute-start.5 = (f32[2]{0:T(128)S(1)}, f32[2]{0:T(128)S(1)}, u32[]{:S(2)}, u32[]{:S(2)}) collective-permute-start(f32[2]{0:T(128)S(1)} %copy-done.4), channel_id=1, source_target_pairs={{1,0},{2,1},{3,2},{4,3},{5,4},{6,5},{7,6},{8,7},{9,8},{10,9},{11,1... | collective-permute-start | bytes 32 | tf_op jit(solution)/shard_map/ppermute | solution.py:26
  34.1 6.7 %copy-start.5 = (s32[2]{0:T(128)S(1)}, s32[2]{0:T(128)}, u32[]{:S(2)}) copy-start(s32[2]{0:T(128)} %param.10) | copy-start | bytes 28
  35.0 5.9 %collective-permute-start.4 = (f32[8,2,2,2,76]{4,0,3,2,1:T(8,128)S(1)}, f32[8,2,2,2,76]{4,0,3,2,1:T(8,128)S(1)}, u32[]{:S(2)}, u32[]{:S(2)}) collective-permute-start(f32[8,2,2,2,76]{4,0,3,2,1:T(8,128)S(1)} %fusion.61), channel_id=1, source_target_pairs={{0,1},{1,2},{2,3},{3,4},{4,5},{5,6},{6,7},{7,8},{8,9},{9,10},{10,1... | collective-permute-start | bytes 58376 | tf_op jit(solution)/shard_map/ppermute | solution.py:24
  36.9 11.8 %collective-permute-start.6 = (f32[8,2,2,2,76]{4,0,3,2,1:T(8,128)S(1)}, f32[8,2,2,2,76]{4,0,3,2,1:T(8,128)S(1)}, u32[]{:S(2)}, u32[]{:S(2)}) collective-permute-start(f32[8,2,2,2,76]{4,0,3,2,1:T(8,128)S(1)} %fusion.61), channel_id=1, source_target_pairs={{1,0},{2,1},{3,2},{4,3},{5,4},{6,5},{7,6},{8,7},{9,8},{10,9},{11,1... | collective-permute-start | bytes 58376 | tf_op jit(solution)/shard_map/ppermute | solution.py:26
  50.4 11.6 %collective-permute-start.7 = (f32[2,1,2,2,2850]{4,3,2,1,0:T(2,128)S(1)}, f32[2,1,2,2,2850]{4,3,2,1,0:T(2,128)S(1)}, u32[]{:S(2)}, u32[]{:S(2)}) collective-permute-start(f32[2,1,2,2,2850]{4,3,2,1,0:T(2,128)S(1)} %bitcast.61), channel_id=1, source_target_pairs={{0,128},{128,0},{256,384},{384,256},{1,129},{129,1},{257,385},{385... | collective-permute-start | bytes 273608 | tf_op jit(solution)/shard_map/ppermute | solution.py:36
  52.3 11.0 %collective-permute-start.8 = (f32[2,1,2,2,2850]{4,3,2,1,0:T(2,128)S(1)}, f32[2,1,2,2,2850]{4,3,2,1,0:T(2,128)S(1)}, u32[]{:S(2)}, u32[]{:S(2)}) collective-permute-start(f32[2,1,2,2,2850]{4,3,2,1,0:T(2,128)S(1)} %bitcast.62), channel_id=1, source_target_pairs={{0,256},{128,384},{256,0},{384,128},{1,257},{129,385},{257,1},{385... | collective-permute-start | bytes 273608 | tf_op jit(solution)/shard_map/ppermute | solution.py:36
  59.9 10.5 %collective-permute-start.9 = (f32[2,1,2,2,2850]{4,3,2,1,0:T(2,128)S(1)}, f32[2,1,2,2,2850]{4,3,2,1,0:T(2,128)S(1)}, u32[]{:S(2)}, u32[]{:S(2)}) collective-permute-start(f32[2,1,2,2,2850]{4,3,2,1,0:T(2,128)S(1)} %bitcast.63), channel_id=1, source_target_pairs={{0,384},{128,256},{256,128},{384,0},{1,385},{129,257},{257,129},{3... | collective-permute-start | bytes 273608 | tf_op jit(solution)/shard_map/ppermute | solution.py:36
  70.6 0.6 copy-start.1
  73.2 5.9 %collective-permute-start.10 = (f32[8,2,2,2,76]{4,0,3,2,1:T(8,128)S(1)}, f32[8,2,2,2,76]{4,0,3,2,1:T(8,128)S(1)}, u32[]{:S(2)}, u32[]{:S(2)}) collective-permute-start(f32[8,2,2,2,76]{4,0,3,2,1:T(8,128)S(1)} %fusion.52), channel_id=1, source_target_pairs={{0,1},{1,2},{2,3},{3,4},{4,5},{5,6},{6,7},{7,8},{8,9},{9,10},{10,1... | collective-permute-start | bytes 58376 | tf_op jit(solution)/shard_map/ppermute | solution.py:24
  75.1 11.8 %collective-permute-start.11 = (f32[8,2,2,2,76]{4,0,3,2,1:T(8,128)S(1)}, f32[8,2,2,2,76]{4,0,3,2,1:T(8,128)S(1)}, u32[]{:S(2)}, u32[]{:S(2)}) collective-permute-start(f32[8,2,2,2,76]{4,0,3,2,1:T(8,128)S(1)} %fusion.52), channel_id=1, source_target_pairs={{1,0},{2,1},{3,2},{4,3},{5,4},{6,5},{7,6},{8,7},{9,8},{10,9},{11,1... | collective-permute-start | bytes 58376 | tf_op jit(solution)/shard_map/ppermute | solution.py:26

commit v2 on v0

--- a/solution.py
+++ b/solution.py
@@ -28,6 +28,16 @@
             axis=dim,
         )
     return cells
+
+
+def sum_over_dir(partial):
+    count = lax.axis_size("dir")
+    total = partial
+    mask = 1
+    while mask < count:
+        total = total + lax.ppermute(total, "dir", [(i, i ^ mask) for i in range(count)])
+        mask *= 2
+    return total
 
 
 def station_tables(baseline_table):
@@ -103,7 +113,7 @@
     for sweep in range(ITERS):
         corrupted_model, parts = corrupt_all(current, model, left_hot, right_hot)
         partial_total = jnp.sum(corrupted_model, axis=0)
-        total = lax.psum(partial_total, "dir")
+        total = sum_over_dir(partial_total)
         residual = visibilities - total
         stepped = solve_all(current, model, corrupted_model, parts, residual, left_hot, right_hot)
         padded_gains = extended(stepped, (("chan", 1),), SPAN)

time: 185 us -> 83.6 us (0.45)
  the two profiles are of different devices: /device:TPU:222 before, /device:TPU:254 now
where the time goes in v2:
time: 83.6 us; the launch traced here: 83.1 us
  starting transfers between devices  36.8 us (44%)
  waiting for transfers between devices  34.3 us (41%)
  matrix products  6.07 us (7%)
  local copies, waits for them, and re-layouts  2.51 us (3%)
  other arithmetic  2.45 us (3%)
  between operations  0.98 us (1%)
    ppermute x3, waiting for transfers between devices, extended(): lax.ppermute(head, axis, [((i + 1) % count, i) for i in range(ends)])  25.1 us
    ppermute x3, starting transfers between devices, extended(): lax.ppermute(tail, axis, [(i, (i + 1) % count) for i in range(ends)])  19.4 us
    ppermute x4, starting transfers between devices, sum_over_dir(): lax.ppermute(total, 'dir', [(i, i ^ mask) for i in range(count)])  9.65 us
    ppermute x4, waiting for transfers between devices, sum_over_dir(): lax.ppermute(total, 'dir', [(i, i ^ mask) for i in range(count)])  9.14 us
    ppermute x3, starting transfers between devices, extended(): lax.ppermute(head, axis, [((i + 1) % count, i) for i in range(ends)])  7.76 us
    dot_general x2, matrix products, corrupt(): right_gain = jnp.matmul(gains, right_hot, precision=highest)[:, None]  1.89 us
  transfers between devices with their start and end apart: 10, of which 6 were waited for; matrix products, arithmetic and copies ran while one was open for 0% of the time, Pallas kernels for 0%

profile of v2, /device:TPU:254, one launch (start us, length us, event | category | flops | bytes accessed | tf_op | source)
XLA Modules:
  0.0 83.1 jit_solution(7384177848631335498)
XLA Ops:
  0.6 0.9 %slice_reduce_fusion.1 = (s32[2850]{0:T(1024)S(1)}, s32[2850]{0:T(1024)S(1)}) fusion(s32[2,2850]{1,0:T(2,128)} %param.11), kind=kLoop, calls=%fused_computation.107 | loop fusion | bytes 45600 | tf_op jit(solution)/shard_map/slice | solution.py:45
  1.5 1.3 %convolution_bitcast_fusion.2 = f32[8,2,1,2,2,2850]{5,0,4,3,1,2:T(8,128)S(1)} fusion(s32[2850]{0:T(1024)S(1)} %get-tuple-element.5, f32[8,2,2,2,76]{4,3,2,1,0:T(2,128)} %param.8), kind=kOutput, calls=%fused_computation.2 | convolution fusion | flops 166565408 | bytes 760456 | tf_op jit(solution)/shard_map/vmap()/dot_general | solution.py:53
  2.9 0.5 convolution_bitcast_fusion.3
  3.4 0.4 copy-done
  3.9 0.1 copy_convert_fusion
  3.9 0.1 multiply_add_fusion.9
  4.1 0.1 multiply_subtract_fusion.8
  4.2 0.2 fusion.35
  4.4 1.9 %collective-permute-start.1 = (f32[2,1,2,2,2850]{4,3,2,1,0:T(2,128)S(1)}, f32[2,1,2,2,2850]{4,3,2,1,0:T(2,128)S(1)}, u32[]{:S(2)}, u32[]{:S(2)}) collective-permute-start(f32[2,1,2,2,2850]{4,3,2,1,0:T(2,128)S(1)} %bitcast.58), channel_id=1, source_target_pairs={{0,128},{128,0},{256,384},{384,256},{1,129},{129,1},{257,385},{385... | collective-permute-start | bytes 273608 | tf_op jit(solution)/shard_map/ppermute | solution.py:38
  6.3 7.8 %collective-permute-start = (f32[2]{0:T(128)S(1)}, f32[2]{0:T(128)S(1)}, u32[]{:S(2)}, u32[]{:S(2)}) collective-permute-start(f32[2]{0:T(128)S(1)} %copy-done.4), channel_id=1, source_target_pairs={{0,1},{1,2},{2,3},{3,4},{4,5},{5,6},{6,7},{7,8},{8,9},{9,10},{10,1... | collective-permute-start | bytes 32 | tf_op jit(solution)/shard_map/ppermute | solution.py:24
  14.1 1.9 %collective-permute-start.4 = (f32[2]{0:T(128)S(1)}, f32[2]{0:T(128)S(1)}, u32[]{:S(2)}, u32[]{:S(2)}) collective-permute-start(f32[2]{0:T(128)S(1)} %copy-done.4), channel_id=1, source_target_pairs={{1,0},{2,1},{3,2},{4,3},{5,4},{6,5},{7,6},{8,7},{9,8},{10,9},{11,1... | collective-permute-start | bytes 32 | tf_op jit(solution)/shard_map/ppermute | solution.py:26
  16.0 0.1 bitcast_add_fusion.1
  16.1 2.0 %collective-permute-start.2 = (f32[2,1,2,2,2850]{4,3,2,1,0:T(2,128)S(1)}, f32[2,1,2,2,2850]{4,3,2,1,0:T(2,128)S(1)}, u32[]{:S(2)}, u32[]{:S(2)}) collective-permute-start(f32[2,1,2,2,2850]{4,3,2,1,0:T(2,128)S(1)} %bitcast_add_fusion.1), channel_id=1, source_target_pairs={{0,256},{128,384},{256,0},{384,128},{1,257},{129,385},{257,1},{385... | collective-permute-start | bytes 273608 | tf_op jit(solution)/shard_map/ppermute | solution.py:38
  18.1 7.4 %collective-permute-done.4 = f32[2]{0:T(128)S(1)} collective-permute-done((f32[2]{0:T(128)S(1)}, f32[2]{0:T(128)S(1)}, u32[]{:S(2)}, u32[]{:S(2)}) %collective-permute-start.4) | collective-permute-done | bytes 40 | tf_op jit(solution)/shard_map/ppermute | solution.py:26
  25.6 0.1 pad_maximum_fusion.7
  25.6 1.1 %collective-permute-done.2 = f32[2,1,2,2,2850]{4,3,2,1,0:T(2,128)S(1)} collective-permute-done((f32[2,1,2,2,2850]{4,3,2,1,0:T(2,128)S(1)}, f32[2,1,2,2,2850]{4,3,2,1,0:T(2,128)S(1)}, u32[]{:S(2)}, u32[]{:S(2)}) %collective-permute-start.2) | collective-permute-done | bytes 91232 | tf_op jit(solution)/shard_map/ppermute | solution.py:38
  26.7 0.1 subtract_bitcast_fusion
  26.8 0.1 fusion.34
  26.9 0.2 multiply_add_fusion.5
  27.1 0.2 multiply_subtract_fusion.6
  27.3 0.8 fusion
  28.1 0.8 fusion.21
  28.9 9.7 %collective-permute-start.3 = (f32[8,2,2,2,76]{4,0,3,2,1:T(8,128)S(1)}, f32[8,2,2,2,76]{4,0,3,2,1:T(8,128)S(1)}, u32[]{:S(2)}, u32[]{:S(2)}) collective-permute-start(f32[8,2,2,2,76]{4,0,3,2,1:T(8,128)S(1)} %fusion.61), channel_id=1, source_target_pairs={{0,1},{1,2},{2,3},{3,4},{4,5},{5,6},{6,7},{7,8},{8,9},{9,10},{10,1... | collective-permute-start | bytes 58376 | tf_op jit(solution)/shard_map/ppermute | solution.py:24
  38.6 1.9 %collective-permute-start.5 = (f32[8,2,2,2,76]{4,0,3,2,1:T(8,128)S(1)}, f32[8,2,2,2,76]{4,0,3,2,1:T(8,128)S(1)}, u32[]{:S(2)}, u32[]{:S(2)}) collective-permute-start(f32[8,2,2,2,76]{4,0,3,2,1:T(8,128)S(1)} %fusion.61), channel_id=1, source_target_pairs={{1,0},{2,1},{3,2},{4,3},{5,4},{6,5},{7,6},{8,7},{9,8},{10,9},{11,1... | collective-permute-start | bytes 58376 | tf_op jit(solution)/shard_map/ppermute | solution.py:26
  40.6 0.1 add_add_fusion
  40.6 9.8 %collective-permute-done.5 = f32[8,2,2,2,76]{4,0,3,2,1:T(8,128)S(1)} collective-permute-done((f32[8,2,2,2,76]{4,0,3,2,1:T(8,128)S(1)}, f32[8,2,2,2,76]{4,0,3,2,1:T(8,128)S(1)}, u32[]{:S(2)}, u32[]{:S(2)}) %collective-permute-start.5) | collective-permute-done | bytes 19488 | tf_op jit(solution)/shard_map/ppermute | solution.py:26
  50.5 0.1 fusion.56
  50.6 0.5 convolution_bitcast_fusion
  51.1 0.5 convolution_bitcast_fusion.1
  51.7 0.1 multiply_add_fusion.3
  51.8 0.1 multiply_subtract_fusion.3
  51.9 0.2 fusion.33
  52.1 1.9 %collective-permute-start.6 = (f32[2,1,2,2,2850]{4,3,2,1,0:T(2,128)S(1)}, f32[2,1,2,2,2850]{4,3,2,1,0:T(2,128)S(1)}, u32[]{:S(2)}, u32[]{:S(2)}) collective-permute-start(f32[2,1,2,2,2850]{4,3,2,1,0:T(2,128)S(1)} %bitcast.59), channel_id=1, source_target_pairs={{0,128},{128,0},{256,384},{384,256},{1,129},{129,1},{257,385},{385... | collective-permute-start | bytes 273608 | tf_op jit(solution)/shard_map/ppermute | solution.py:38
  54.0 1.3 %collective-permute-done.6 = f32[2,1,2,2,2850]{4,3,2,1,0:T(2,128)S(1)} collective-permute-done((f32[2,1,2,2,2850]{4,3,2,1,0:T(2,128)S(1)}, f32[2,1,2,2,2850]{4,3,2,1,0:T(2,128)S(1)}, u32[]{:S(2)}, u32[]{:S(2)}) %collective-permute-start.6) | collective-permute-done | bytes 91232 | tf_op jit(solution)/shard_map/ppermute | solution.py:38
  55.3 3.8 %collective-permute-start.7 = (f32[2,1,2,2,2850]{4,3,2,1,0:T(2,128)S(1)}, f32[2,1,2,2,2850]{4,3,2,1,0:T(2,128)S(1)}, u32[]{:S(2)}, u32[]{:S(2)}) collective-permute-start(f32[2,1,2,2,2850]{4,3,2,1,0:T(2,128)S(1)} %bitcast_add_fusion), channel_id=1, source_target_pairs={{0,256},{128,384},{256,0},{384,128},{1,257},{129,385},{257,1},{385... | collective-permute-start | bytes 273608 | tf_op jit(solution)/shard_map/ppermute | solution.py:38
  59.1 6.8 %collective-permute-done.7 = f32[2,1,2,2,2850]{4,3,2,1,0:T(2,128)S(1)} collective-permute-done((f32[2,1,2,2,2850]{4,3,2,1,0:T(2,128)S(1)}, f32[2,1,2,2,2850]{4,3,2,1,0:T(2,128)S(1)}, u32[]{:S(2)}, u32[]{:S(2)}) %collective-permute-start.7) | collective-permute-done | bytes 91232 | tf_op jit(solution)/shard_map/ppermute | solution.py:38
  65.9 0.1 add_subtract_fusion
  66.0 0.1 fusion.32
  66.1 0.5 copy-done.2
  66.6 0.1 multiply_add_fusion
  66.8 0.2 multiply_subtract_fusion
  67.0 0.8 fusion.10
  67.8 0.8 fusion.20
  68.6 1.9 %collective-permute-start.8 = (f32[8,2,2,2,76]{4,0,3,2,1:T(8,128)S(1)}, f32[8,2,2,2,76]{4,0,3,2,1:T(8,128)S(1)}, u32[]{:S(2)}, u32[]{:S(2)}) collective-permute-start(f32[8,2,2,2,76]{4,0,3,2,1:T(8,128)S(1)} %fusion.52), channel_id=1, source_target_pairs={{0,1},{1,2},{2,3},{3,4},{4,5},{5,6},{6,7},{7,8},{8,9},{9,10},{10,1... | collective-permute-start | bytes 58376 | tf_op jit(solution)/shard_map/ppermute | solution.py:24
  70.5 3.9 %collective-permute-start.9 = (f32[8,2,2,2,76]{4,0,3,2,1:T(8,128)S(1)}, f32[8,2,2,2,76]{4,0,3,2,1:T(8,128)S(1)}, u32[]{:S(2)}, u32[]{:S(2)}) collective-permute-start(f32[8,2,2,2,76]{4,0,3,2,1:T(8,128)S(1)} %fusion.52), channel_id=1, source_target_pairs={{1,0},{2,1},{3,2},{4,3},{5,4},{6,5},{7,6},{8,7},{9,8},{10,9},{11,1... | collective-permute-start | bytes 58376 | tf_op jit(solution)/shard_map/ppermute | solution.py:26
  74.5 7.9 %collective-permute-done.9 = f32[8,2,2,2,76]{4,0,3,2,1:T(8,128)S(1)} collective-permute-done((f32[8,2,2,2,76]{4,0,3,2,1:T(8,128)S(1)}, f32[8,2,2,2,76]{4,0,3,2,1:T(8,128)S(1)}, u32[]{:S(2)}, u32[]{:S(2)}) %collective-permute-start.9) | collective-permute-done | bytes 19488 | tf_op jit(solution)/shard_map/ppermute | solution.py:26
  82.3 0.1 fusion.47
  82.4 0.6 copy.12
  (19 shorter events, 0.1 us)
Async XLA Ops:
  1.5 1.4 %copy-start.3 = (f32[8,2,2,2,76]{4,3,2,1,0:T(2,128)S(1)}, f32[8,2,2,2,76]{4,3,2,1,0:T(2,128)}, u32[]{:S(2)}) copy-start(f32[8,2,2,2,76]{4,3,2,1,0:T(2,128)} %param.8) | copy-start | bytes 58372
  2.9 1.0 %copy-start = (bf16[8,2,1,2,2,2850]{5,4,3,2,1,0:T(2,128)(2,1)S(1)}, bf16[8,2,1,2,2,2850]{5,4,3,2,1,0:T(2,128)(2,1)}, u32[]{:S(2)}) copy-start(bf16[8,2,1,2,2,2850]{5,4,3,2,1,0:T(2,128)(2,1)} %param.7) | copy-start | bytes 1094404
  4.1 2.2 %copy-start.4 = (f32[2]{0:T(128)S(1)}, f32[2]{0:T(128)}, u32[]{:S(2)}) copy-start(f32[2]{0:T(128)} %param.9) | copy-start | bytes 28
  4.2 22.6 %copy-start.1 = (f32[2,1,2,2,2850]{4,3,2,1,0:T(2,128)S(1)}, f32[2,1,2,2,2850]{4,3,2,1,0:T(2,128)}, u32[]{:S(2)}) copy-start(f32[2,1,2,2,2850]{4,3,2,1,0:T(2,128)} %param.6) | copy-start | bytes 273604
  4.4 11.6 %collective-permute-start.1 = (f32[2,1,2,2,2850]{4,3,2,1,0:T(2,128)S(1)}, f32[2,1,2,2,2850]{4,3,2,1,0:T(2,128)S(1)}, u32[]{:S(2)}, u32[]{:S(2)}) collective-permute-start(f32[2,1,2,2,2850]{4,3,2,1,0:T(2,128)S(1)} %bitcast.58), channel_id=1, source_target_pairs={{0,128},{128,0},{256,384},{384,256},{1,129},{129,1},{257,385},{385... | collective-permute-start | bytes 273608 | tf_op jit(solution)/shard_map/ppermute | solution.py:38
  6.3 11.8 %collective-permute-start = (f32[2]{0:T(128)S(1)}, f32[2]{0:T(128)S(1)}, u32[]{:S(2)}, u32[]{:S(2)}) collective-permute-start(f32[2]{0:T(128)S(1)} %copy-done.4), channel_id=1, source_target_pairs={{0,1},{1,2},{2,3},{3,4},{4,5},{5,6},{6,7},{7,8},{8,9},{9,10},{10,1... | collective-permute-start | bytes 32 | tf_op jit(solution)/shard_map/ppermute | solution.py:24
  14.1 11.5 %collective-permute-start.4 = (f32[2]{0:T(128)S(1)}, f32[2]{0:T(128)S(1)}, u32[]{:S(2)}, u32[]{:S(2)}) collective-permute-start(f32[2]{0:T(128)S(1)} %copy-done.4), channel_id=1, source_target_pairs={{1,0},{2,1},{3,2},{4,3},{5,4},{6,5},{7,6},{8,7},{9,8},{10,9},{11,1... | collective-permute-start | bytes 32 | tf_op jit(solution)/shard_map/ppermute | solution.py:26
  16.1 10.6 %collective-permute-start.2 = (f32[2,1,2,2,2850]{4,3,2,1,0:T(2,128)S(1)}, f32[2,1,2,2,2850]{4,3,2,1,0:T(2,128)S(1)}, u32[]{:S(2)}, u32[]{:S(2)}) collective-permute-start(f32[2,1,2,2,2850]{4,3,2,1,0:T(2,128)S(1)} %bitcast_add_fusion.1), channel_id=1, source_target_pairs={{0,256},{128,384},{256,0},{384,128},{1,257},{129,385},{257,1},{385... | collective-permute-start | bytes 273608 | tf_op jit(solution)/shard_map/ppermute | solution.py:38
  28.1 12.4 %copy-start.5 = (s32[2]{0:T(128)S(1)}, s32[2]{0:T(128)}, u32[]{:S(2)}) copy-start(s32[2]{0:T(128)} %param.10) | copy-start | bytes 28
  28.9 11.7 %collective-permute-start.3 = (f32[8,2,2,2,76]{4,0,3,2,1:T(8,128)S(1)}, f32[8,2,2,2,76]{4,0,3,2,1:T(8,128)S(1)}, u32[]{:S(2)}, u32[]{:S(2)}) collective-permute-start(f32[8,2,2,2,76]{4,0,3,2,1:T(8,128)S(1)} %fusion.61), channel_id=1, source_target_pairs={{0,1},{1,2},{2,3},{3,4},{4,5},{5,6},{6,7},{7,8},{8,9},{9,10},{10,1... | collective-permute-start | bytes 58376 | tf_op jit(solution)/shard_map/ppermute | solution.py:24
  38.6 11.8 %collective-permute-start.5 = (f32[8,2,2,2,76]{4,0,3,2,1:T(8,128)S(1)}, f32[8,2,2,2,76]{4,0,3,2,1:T(8,128)S(1)}, u32[]{:S(2)}, u32[]{:S(2)}) collective-permute-start(f32[8,2,2,2,76]{4,0,3,2,1:T(8,128)S(1)} %fusion.61), channel_id=1, source_target_pairs={{1,0},{2,1},{3,2},{4,3},{5,4},{6,5},{7,6},{8,7},{9,8},{10,9},{11,1... | collective-permute-start | bytes 58376 | tf_op jit(solution)/shard_map/ppermute | solution.py:26
  52.1 3.2 %collective-permute-start.6 = (f32[2,1,2,2,2850]{4,3,2,1,0:T(2,128)S(1)}, f32[2,1,2,2,2850]{4,3,2,1,0:T(2,128)S(1)}, u32[]{:S(2)}, u32[]{:S(2)}) collective-permute-start(f32[2,1,2,2,2850]{4,3,2,1,0:T(2,128)S(1)} %bitcast.59), channel_id=1, source_target_pairs={{0,128},{128,0},{256,384},{384,256},{1,129},{129,1},{257,385},{385... | collective-permute-start | bytes 273608 | tf_op jit(solution)/shard_map/ppermute | solution.py:38
  55.3 10.6 %collective-permute-start.7 = (f32[2,1,2,2,2850]{4,3,2,1,0:T(2,128)S(1)}, f32[2,1,2,2,2850]{4,3,2,1,0:T(2,128)S(1)}, u32[]{:S(2)}, u32[]{:S(2)}) collective-permute-start(f32[2,1,2,2,2850]{4,3,2,1,0:T(2,128)S(1)} %bitcast_add_fusion), channel_id=1, source_target_pairs={{0,256},{128,384},{256,0},{384,128},{1,257},{129,385},{257,1},{385... | collective-permute-start | bytes 273608 | tf_op jit(solution)/shard_map/ppermute | solution.py:38
  66.0 0.6 copy-start.2
  68.6 5.9 %collective-permute-start.8 = (f32[8,2,2,2,76]{4,0,3,2,1:T(8,128)S(1)}, f32[8,2,2,2,76]{4,0,3,2,1:T(8,128)S(1)}, u32[]{:S(2)}, u32[]{:S(2)}) collective-permute-start(f32[8,2,2,2,76]{4,0,3,2,1:T(8,128)S(1)} %fusion.52), channel_id=1, source_target_pairs={{0,1},{1,2},{2,3},{3,4},{4,5},{5,6},{6,7},{7,8},{8,9},{9,10},{10,1... | collective-permute-start | bytes 58376 | tf_op jit(solution)/shard_map/ppermute | solution.py:24
  70.5 11.8 %collective-permute-start.9 = (f32[8,2,2,2,76]{4,0,3,2,1:T(8,128)S(1)}, f32[8,2,2,2,76]{4,0,3,2,1:T(8,128)S(1)}, u32[]{:S(2)}, u32[]{:S(2)}) collective-permute-start(f32[8,2,2,2,76]{4,0,3,2,1:T(8,128)S(1)} %fusion.52), channel_id=1, source_target_pairs={{1,0},{2,1},{3,2},{4,3},{5,4},{6,5},{7,6},{8,7},{9,8},{10,9},{11,1... | collective-permute-start | bytes 58376 | tf_op jit(solution)/shard_map/ppermute | solution.py:26

commit v3 on v2

--- a/solution.py
+++ b/solution.py
@@ -13,21 +13,31 @@
 highest = lax.Precision.HIGHEST
 
 
-def extended(cells, sides, width):
-    for axis, dim in sides:
-        count = lax.axis_size(axis)
-        ends = count - 1
-        head = lax.slice_in_dim(cells, 0, width, axis=dim)
-        tail = lax.slice_in_dim(cells, cells.shape[dim] - width, cells.shape[dim], axis=dim)
-        cells = jnp.concatenate(
-            [
-                lax.ppermute(tail, axis, [(i, (i + 1) % count) for i in range(ends)]),
-                cells,
-                lax.ppermute(head, axis, [((i + 1) % count, i) for i in range(ends)]),
-            ],
-            axis=dim,
-        )
-    return cells
+def extended(items, axis, width):
+    count = lax.axis_size(axis)
+    ends = count - 1
+
+    def edge(cells, dim, first):
+        size = cells.shape[dim]
+        start = 0 if first else size - width
+        return lax.slice_in_dim(cells, start, start + width, axis=dim)
+
+    def send(pieces, pairs):
+        flat = jnp.concatenate([piece.reshape(-1) for piece in pieces])
+        arrived = lax.ppermute(flat, axis, pairs)
+        out = []
+        offset = 0
+        for piece in pieces:
+            out.append(arrived[offset : offset + piece.size].reshape(piece.shape))
+            offset += piece.size
+        return out
+
+    from_left = send([edge(c, d, False) for c, d in items], [(i, i + 1) for i in range(ends)])
+    from_right = send([edge(c, d, True) for c, d in items], [(i + 1, i) for i in range(ends)])
+    return [
+        jnp.concatenate([left, cells, right], axis=dim)
+        for (cells, dim), left, right in zip(items, from_left, from_right)
+    ]
 
 
 def sum_over_dir(partial):
@@ -105,7 +115,7 @@
 
 def on_device(visibilities, model, gains, weights, widths, baseline_table):
     left_hot, right_hot = station_tables(baseline_table)
-    padded_weights = extended(weights, (("chan", 0),), SPAN)
+    padded_weights = None
     current = gains
     residual = visibilities
     corrupt_all = jax.vmap(corrupt, in_axes=(0, 0, None, None))
@@ -116,7 +126,10 @@
         total = sum_over_dir(partial_total)
         residual = visibilities - total
         stepped = solve_all(current, model, corrupted_model, parts, residual, left_hot, right_hot)
-        padded_gains = extended(stepped, (("chan", 1),), SPAN)
+        if padded_weights is None:
+            padded_gains, padded_weights = extended(((stepped, 1), (weights, 0)), "chan", SPAN)
+        else:
+            (padded_gains,) = extended(((stepped, 1),), "chan", SPAN)
         current = smooth(padded_gains, padded_weights, widths)
     return (current, residual)
 

time: 83.6 us -> 75.7 us (0.906)
  starting transfers between devices: 36.8 us -> 26 us
  waiting for transfers between devices: 34.3 us -> 36.3 us
    ppermute x6 -> x4, starting transfers between devices: 27.1 us -> 15.5 us  [send(): arrived = lax.ppermute(flat, axis, pairs)]
    ppermute x4, waiting for transfers between devices: 9.14 us -> 19 us  [sum_over_dir(): lax.ppermute(total, 'dir', [(i, i ^ mask) for i in range(count)])]
    ppermute x6 -> x4, waiting for transfers between devices: 25.1 us -> 17.2 us  [send(): arrived = lax.ppermute(flat, axis, pairs)]
  transfers between devices with their start and end apart: 10 -> 8, of which waited for: 6 -> 6; matrix products, arithmetic and copies ran while one was open for 0% -> 0% of each run, Pallas kernels for 0% -> 0%
where the time goes in v3:
time: 75.7 us; the launch traced here: 75.2 us
  waiting for transfers between devices  36.3 us (48%)
  starting transfers between devices  26 us (34%)
  matrix products  6.06 us (8%)
  local copies, waits for them, and re-layouts  3.28 us (4%)
  other arithmetic  2.57 us (3%)
  between operations  1.05 us (1%)
    ppermute x4, waiting for transfers between devices, sum_over_dir(): lax.ppermute(total, 'dir', [(i, i ^ mask) for i in range(count)])  19 us
    ppermute x4, waiting for transfers between devices, send(): arrived = lax.ppermute(flat, axis, pairs)  17.2 us
    ppermute x4, starting transfers between devices, send(): arrived = lax.ppermute(flat, axis, pairs)  15.5 us
    ppermute x4, starting transfers between devices, sum_over_dir(): lax.ppermute(total, 'dir', [(i, i ^ mask) for i in range(count)])  10.5 us
    dot_general x2, matrix products, corrupt(): right_gain = jnp.matmul(gains, right_hot, precision=highest)[:, None]  1.89 us
    unnamed x14, local copies, waits for them, and re-layouts  1.65 us
    dot_general x2, matrix products, solve(): jnp.matmul(right_terms, right_hot.T, precision=highest)  1.55 us
    dot_general x2, matrix products, solve(): jnp.matmul(left_products, left_hot.T, precision=highest)  1.55 us
  transfers between devices with their start and end apart: 8, of which 6 were waited for; matrix products, arithmetic and copies ran while one was open for 0% of the time, Pallas kernels for 0%

profile of v3, /device:TPU:254, one launch (start us, length us, event | category | flops | bytes accessed | tf_op | source)
XLA Modules:
  0.0 75.2 jit_solution(4935942887699064606)
XLA Ops:
  0.6 0.9 %slice_reduce_fusion.1 = (s32[2850]{0:T(1024)S(1)}, s32[2850]{0:T(1024)S(1)}) fusion(s32[2,2850]{1,0:T(2,128)} %param.11), kind=kLoop, calls=%fused_computation.107 | loop fusion | bytes 45600 | tf_op jit(solution)/shard_map/slice | solution.py:55
  1.5 1.3 %convolution_bitcast_fusion.2 = f32[8,2,1,2,2,2850]{5,0,4,3,1,2:T(8,128)S(1)} fusion(s32[2850]{0:T(1024)S(1)} %get-tuple-element.7, f32[8,2,2,2,76]{4,3,2,1,0:T(2,128)} %param.8), kind=kOutput, calls=%fused_computation.2 | convolution fusion | flops 166565408 | bytes 760456 | tf_op jit(solution)/shard_map/vmap()/dot_general | solution.py:63
  2.9 0.5 convolution_bitcast_fusion.3
  3.4 0.4 copy-done
  3.9 0.1 multiply_add_fusion.9
  4.1 0.1 multiply_subtract_fusion.8
  4.2 0.2 fusion.35
  4.4 1.9 %collective-permute-start = (f32[2,1,2,2,2850]{4,3,2,1,0:T(2,128)S(1)}, f32[2,1,2,2,2850]{4,3,2,1,0:T(2,128)S(1)}, u32[]{:S(2)}, u32[]{:S(2)}) collective-permute-start(f32[2,1,2,2,2850]{4,3,2,1,0:T(2,128)S(1)} %bitcast.60), channel_id=1, source_target_pairs={{0,128},{128,0},{256,384},{384,256},{1,129},{129,1},{257,385},{385... | collective-permute-start | bytes 273608 | tf_op jit(solution)/shard_map/ppermute | solution.py:48
  6.3 1.3 %collective-permute-done = f32[2,1,2,2,2850]{4,3,2,1,0:T(2,128)S(1)} collective-permute-done((f32[2,1,2,2,2850]{4,3,2,1,0:T(2,128)S(1)}, f32[2,1,2,2,2850]{4,3,2,1,0:T(2,128)S(1)}, u32[]{:S(2)}, u32[]{:S(2)}) %collective-permute-start) | collective-permute-done | bytes 91232 | tf_op jit(solution)/shard_map/ppermute | solution.py:48
  7.6 4.7 %collective-permute-start.1 = (f32[2,1,2,2,2850]{4,3,2,1,0:T(2,128)S(1)}, f32[2,1,2,2,2850]{4,3,2,1,0:T(2,128)S(1)}, u32[]{:S(2)}, u32[]{:S(2)}) collective-permute-start(f32[2,1,2,2,2850]{4,3,2,1,0:T(2,128)S(1)} %bitcast_add_fusion.1), channel_id=1, source_target_pairs={{0,256},{128,384},{256,0},{384,128},{1,257},{129,385},{257,1},{385... | collective-permute-start | bytes 273608 | tf_op jit(solution)/shard_map/ppermute | solution.py:48
  12.4 7.9 %collective-permute-done.1 = f32[2,1,2,2,2850]{4,3,2,1,0:T(2,128)S(1)} collective-permute-done((f32[2,1,2,2,2850]{4,3,2,1,0:T(2,128)S(1)}, f32[2,1,2,2,2850]{4,3,2,1,0:T(2,128)S(1)}, u32[]{:S(2)}, u32[]{:S(2)}) %collective-permute-start.1) | collective-permute-done | bytes 91232 | tf_op jit(solution)/shard_map/ppermute | solution.py:48
  20.3 0.1 fusion.34
  20.4 0.2 multiply_add_fusion.5
  20.6 0.2 multiply_subtract_fusion.6
  20.8 0.8 %fusion = f32[8,2,2,3,76]{4,0,3,2,1:T(8,128)S(1)} fusion(f32[8,2,1,2,1,2850]{5,0,4,3,1,2:T(8,128)S(1)} %get-tuple-element.40, f32[8,2,1,2,1,2850]{5,0,4,3,1,2:T(8,128)S(1)} %get-tuple-element.31, f32[8,2,1,2,1,2850]{5,0,4,3,1,2:T(8,128)S(1)} %get-tuple-element.30, s32[2850]{0:T(1024)S(1)} %get-tuple-element.6), kind=kOutput, calls=%fused_computation.5 | convolution fusion | flops 250287008 | bytes 1134984 | tf_op jit(solution)/shard_map/vmap()/dot_general | solution.py:91
  21.6 0.8 %fusion.21 = f32[8,2,2,3,76]{4,0,3,2,1:T(8,128)S(1)} fusion(f32[8,2,2,3,76]{4,0,3,2,1:T(8,128)S(1)} %fusion, f32[8,2,1,2,1,2850]{5,0,4,3,1,2:T(8,128)S(1)} %get-tuple-element.32, f32[8,2,1,2,1,2850]{5,0,4,3,1,2:T(8,128)S(1)} %get-tuple-element.39, f32[8,2,1,2,1,2850]{5,0,4,3,1,2:T(8,128)S(1)} %get-tuple-element.20, s32[2850]{0:T(1024)S(1)} %get-tuple-element.7), kind=kOutput, calls=%fused_computation.29 | convolution fusion | flops 250294304 | bytes 1164168 | tf_op jit(solution)/shard_map/vmap()/dot_general | solution.py:91
  22.5 0.1 reshape.379
  22.6 7.7 %collective-permute-start.2 = (f32[4866]{0:T(1024)S(1)}, f32[4866]{0:T(1024)S(1)}, u32[]{:S(2)}, u32[]{:S(2)}) collective-permute-start(f32[4866]{0:T(1024)S(1)} %constant_dynamic-update-slice_fusion), channel_id=1, source_target_pairs={{0,1},{1,2},{2,3},{3,4},{4,5},{5,6},{6,7},{7,8},{8,9},{9,10},{10,1... | collective-permute-start | bytes 58400 | tf_op jit(solution)/shard_map/ppermute | solution.py:27
  30.4 1.9 %collective-permute-start.3 = (f32[4866]{0:T(1024)S(1)}, f32[4866]{0:T(1024)S(1)}, u32[]{:S(2)}, u32[]{:S(2)}) collective-permute-start(f32[4866]{0:T(1024)S(1)} %constant_dynamic-update-slice_fusion), channel_id=1, source_target_pairs={{1,0},{2,1},{3,2},{4,3},{5,4},{6,5},{7,6},{8,7},{9,8},{10,9},{11,1... | collective-permute-start | bytes 58400 | tf_op jit(solution)/shard_map/ppermute | solution.py:27
  32.3 0.1 reshape.380
  32.5 9.6 %collective-permute-done.3 = f32[4866]{0:T(1024)S(1)} collective-permute-done((f32[4866]{0:T(1024)S(1)}, f32[4866]{0:T(1024)S(1)}, u32[]{:S(2)}, u32[]{:S(2)}) %collective-permute-start.3) | collective-permute-done | bytes 19496 | tf_op jit(solution)/shard_map/ppermute | solution.py:27
  42.1 0.1 reshape.381
  42.2 0.1 pad_maximum_fusion.7
  42.3 0.1 add_add_fusion
  42.4 0.1 fusion.56
  42.5 0.5 convolution_bitcast_fusion
  43.0 0.5 convolution_bitcast_fusion.1
  43.6 0.2 multiply_add_fusion.3
  43.8 0.1 multiply_subtract_fusion.3
  43.8 0.2 fusion.33
  44.1 1.9 %collective-permute-start.4 = (f32[2,1,2,2,2850]{4,3,2,1,0:T(2,128)S(1)}, f32[2,1,2,2,2850]{4,3,2,1,0:T(2,128)S(1)}, u32[]{:S(2)}, u32[]{:S(2)}) collective-permute-start(f32[2,1,2,2,2850]{4,3,2,1,0:T(2,128)S(1)} %bitcast.61), channel_id=1, source_target_pairs={{0,128},{128,0},{256,384},{384,256},{1,129},{129,1},{257,385},{385... | collective-permute-start | bytes 273608 | tf_op jit(solution)/shard_map/ppermute | solution.py:48
  46.0 1.3 %collective-permute-done.4 = f32[2,1,2,2,2850]{4,3,2,1,0:T(2,128)S(1)} collective-permute-done((f32[2,1,2,2,2850]{4,3,2,1,0:T(2,128)S(1)}, f32[2,1,2,2,2850]{4,3,2,1,0:T(2,128)S(1)}, u32[]{:S(2)}, u32[]{:S(2)}) %collective-permute-start.4) | collective-permute-done | bytes 91232 | tf_op jit(solution)/shard_map/ppermute | solution.py:48
  47.3 1.9 %collective-permute-start.5 = (f32[2,1,2,2,2850]{4,3,2,1,0:T(2,128)S(1)}, f32[2,1,2,2,2850]{4,3,2,1,0:T(2,128)S(1)}, u32[]{:S(2)}, u32[]{:S(2)}) collective-permute-start(f32[2,1,2,2,2850]{4,3,2,1,0:T(2,128)S(1)} %bitcast_add_fusion), channel_id=1, source_target_pairs={{0,256},{128,384},{256,0},{384,128},{1,257},{129,385},{257,1},{385... | collective-permute-start | bytes 273608 | tf_op jit(solution)/shard_map/ppermute | solution.py:48
  49.2 8.6 %collective-permute-done.5 = f32[2,1,2,2,2850]{4,3,2,1,0:T(2,128)S(1)} collective-permute-done((f32[2,1,2,2,2850]{4,3,2,1,0:T(2,128)S(1)}, f32[2,1,2,2,2850]{4,3,2,1,0:T(2,128)S(1)}, u32[]{:S(2)}, u32[]{:S(2)}) %collective-permute-start.5) | collective-permute-done | bytes 91232 | tf_op jit(solution)/shard_map/ppermute | solution.py:48
  58.0 0.1 fusion.32
  58.1 0.5 copy-done.2
  58.6 0.2 multiply_add_fusion
  58.8 0.2 multiply_subtract_fusion
  59.0 0.8 %fusion.10 = f32[8,2,2,3,76]{4,0,3,2,1:T(8,128)S(1)} fusion(f32[8,2,1,2,1,2850]{5,0,4,3,1,2:T(8,128)S(1)} %get-tuple-element.38, f32[8,2,1,2,1,2850]{5,0,4,3,1,2:T(8,128)S(1)} %get-tuple-element.36, f32[8,2,1,2,1,2850]{5,0,4,3,1,2:T(8,128)S(1)} %get-tuple-element.37, s32[2850]{0:T(1024)S(1)} %get-tuple-element.6), kind=kOutput, calls=%fused_computation.17 | convolution fusion | flops 250287008 | bytes 1134984 | tf_op jit(solution)/shard_map/vmap()/dot_general | solution.py:91
  59.8 0.8 %fusion.20 = f32[8,2,2,3,76]{4,0,3,2,1:T(8,128)S(1)} fusion(f32[8,2,2,3,76]{4,0,3,2,1:T(8,128)S(1)} %fusion.10, f32[8,2,1,2,1,2850]{5,0,4,3,1,2:T(8,128)S(1)} %get-tuple-element.35, f32[8,2,1,2,1,2850]{5,0,4,3,1,2:T(8,128)S(1)} %get-tuple-element.34, f32[8,2,1,2,1,2850]{5,0,4,3,1,2:T(8,128)S(1)} %get-tuple-element.8, s32[2850]{0:T(1024)S(1)} %get-tuple-element.7), kind=kOutput, calls=%fused_computation.28 | convolution fusion | flops 250294304 | bytes 1164168 | tf_op jit(solution)/shard_map/vmap()/dot_general | solution.py:91
  60.6 0.1 reshape.382
  60.7 1.9 %collective-permute-start.6 = (f32[4864]{0:T(1024)S(1)}, f32[4864]{0:T(1024)S(1)}, u32[]{:S(2)}, u32[]{:S(2)}) collective-permute-start(f32[4864]{0:T(1024)S(1)} %reshape.382), channel_id=1, source_target_pairs={{0,1},{1,2},{2,3},{3,4},{4,5},{5,6},{6,7},{7,8},{8,9},{9,10},{10,1... | collective-permute-start | bytes 58376 | tf_op jit(solution)/shard_map/ppermute | solution.py:27
  62.7 3.9 %collective-permute-start.7 = (f32[4864]{0:T(1024)S(1)}, f32[4864]{0:T(1024)S(1)}, u32[]{:S(2)}, u32[]{:S(2)}) collective-permute-start(f32[4864]{0:T(1024)S(1)} %reshape.382), channel_id=1, source_target_pairs={{1,0},{2,1},{3,2},{4,3},{5,4},{6,5},{7,6},{8,7},{9,8},{10,9},{11,1... | collective-permute-start | bytes 58376 | tf_op jit(solution)/shard_map/ppermute | solution.py:27
  66.6 0.1 reshape.383
  66.7 7.6 %collective-permute-done.7 = f32[4864]{0:T(1024)S(1)} collective-permute-done((f32[4864]{0:T(1024)S(1)}, f32[4864]{0:T(1024)S(1)}, u32[]{:S(2)}, u32[]{:S(2)}) %collective-permute-start.7) | collective-permute-done | bytes 19488 | tf_op jit(solution)/shard_map/ppermute | solution.py:27
  74.4 0.1 reshape.384
  74.5 0.1 fusion.47
  74.6 0.6 copy.27
  (32 shorter events, 0.5 us)
Async XLA Ops:
  1.5 1.4 %copy-start.3 = (f32[8,2,2,2,76]{4,3,2,1,0:T(2,128)S(1)}, f32[8,2,2,2,76]{4,3,2,1,0:T(2,128)}, u32[]{:S(2)}) copy-start(f32[8,2,2,2,76]{4,3,2,1,0:T(2,128)} %param.8) | copy-start | bytes 58372
  2.9 1.0 %copy-start = (bf16[8,2,1,2,2,2850]{5,4,3,2,1,0:T(2,128)(2,1)S(1)}, bf16[8,2,1,2,2,2850]{5,4,3,2,1,0:T(2,128)(2,1)}, u32[]{:S(2)}) copy-start(bf16[8,2,1,2,2,2850]{5,4,3,2,1,0:T(2,128)(2,1)} %param.7) | copy-start | bytes 1094404
  4.2 16.1 %copy-start.1 = (f32[2,1,2,2,2850]{4,3,2,1,0:T(2,128)S(1)}, f32[2,1,2,2,2850]{4,3,2,1,0:T(2,128)}, u32[]{:S(2)}) copy-start(f32[2,1,2,2,2850]{4,3,2,1,0:T(2,128)} %param.6) | copy-start | bytes 273604
  4.4 3.2 %collective-permute-start = (f32[2,1,2,2,2850]{4,3,2,1,0:T(2,128)S(1)}, f32[2,1,2,2,2850]{4,3,2,1,0:T(2,128)S(1)}, u32[]{:S(2)}, u32[]{:S(2)}) collective-permute-start(f32[2,1,2,2,2850]{4,3,2,1,0:T(2,128)S(1)} %bitcast.60), channel_id=1, source_target_pairs={{0,128},{128,0},{256,384},{384,256},{1,129},{129,1},{257,385},{385... | collective-permute-start | bytes 273608 | tf_op jit(solution)/shard_map/ppermute | solution.py:48
  7.6 12.6 %collective-permute-start.1 = (f32[2,1,2,2,2850]{4,3,2,1,0:T(2,128)S(1)}, f32[2,1,2,2,2850]{4,3,2,1,0:T(2,128)S(1)}, u32[]{:S(2)}, u32[]{:S(2)}) collective-permute-start(f32[2,1,2,2,2850]{4,3,2,1,0:T(2,128)S(1)} %bitcast_add_fusion.1), channel_id=1, source_target_pairs={{0,256},{128,384},{256,0},{384,128},{1,257},{129,385},{257,1},{385... | collective-permute-start | bytes 273608 | tf_op jit(solution)/shard_map/ppermute | solution.py:48
  21.6 1.0 %copy-start.4 = (f32[2]{0:T(128)S(1)}, f32[2]{0:T(128)}, u32[]{:S(2)}) copy-start(f32[2]{0:T(128)} %param.9) | copy-start | bytes 28
  21.6 20.7 %copy-start.5 = (s32[2]{0:T(128)S(1)}, s32[2]{0:T(128)}, u32[]{:S(2)}) copy-start(s32[2]{0:T(128)} %param.10) | copy-start | bytes 28
  22.6 9.7 %collective-permute-start.2 = (f32[4866]{0:T(1024)S(1)}, f32[4866]{0:T(1024)S(1)}, u32[]{:S(2)}, u32[]{:S(2)}) collective-permute-start(f32[4866]{0:T(1024)S(1)} %constant_dynamic-update-slice_fusion), channel_id=1, source_target_pairs={{0,1},{1,2},{2,3},{3,4},{4,5},{5,6},{6,7},{7,8},{8,9},{9,10},{10,1... | collective-permute-start | bytes 58400 | tf_op jit(solution)/shard_map/ppermute | solution.py:27
  30.4 11.7 %collective-permute-start.3 = (f32[4866]{0:T(1024)S(1)}, f32[4866]{0:T(1024)S(1)}, u32[]{:S(2)}, u32[]{:S(2)}) collective-permute-start(f32[4866]{0:T(1024)S(1)} %constant_dynamic-update-slice_fusion), channel_id=1, source_target_pairs={{1,0},{2,1},{3,2},{4,3},{5,4},{6,5},{7,6},{8,7},{9,8},{10,9},{11,1... | collective-permute-start | bytes 58400 | tf_op jit(solution)/shard_map/ppermute | solution.py:27
  44.1 3.2 %collective-permute-start.4 = (f32[2,1,2,2,2850]{4,3,2,1,0:T(2,128)S(1)}, f32[2,1,2,2,2850]{4,3,2,1,0:T(2,128)S(1)}, u32[]{:S(2)}, u32[]{:S(2)}) collective-permute-start(f32[2,1,2,2,2850]{4,3,2,1,0:T(2,128)S(1)} %bitcast.61), channel_id=1, source_target_pairs={{0,128},{128,0},{256,384},{384,256},{1,129},{129,1},{257,385},{385... | collective-permute-start | bytes 273608 | tf_op jit(solution)/shard_map/ppermute | solution.py:48
  47.3 10.6 %collective-permute-start.5 = (f32[2,1,2,2,2850]{4,3,2,1,0:T(2,128)S(1)}, f32[2,1,2,2,2850]{4,3,2,1,0:T(2,128)S(1)}, u32[]{:S(2)}, u32[]{:S(2)}) collective-permute-start(f32[2,1,2,2,2850]{4,3,2,1,0:T(2,128)S(1)} %bitcast_add_fusion), channel_id=1, source_target_pairs={{0,256},{128,384},{256,0},{384,128},{1,257},{129,385},{257,1},{385... | collective-permute-start | bytes 273608 | tf_op jit(solution)/shard_map/ppermute | solution.py:48
  57.9 0.6 copy-start.2
  60.7 5.9 %collective-permute-start.6 = (f32[4864]{0:T(1024)S(1)}, f32[4864]{0:T(1024)S(1)}, u32[]{:S(2)}, u32[]{:S(2)}) collective-permute-start(f32[4864]{0:T(1024)S(1)} %reshape.382), channel_id=1, source_target_pairs={{0,1},{1,2},{2,3},{3,4},{4,5},{5,6},{6,7},{7,8},{8,9},{9,10},{10,1... | collective-permute-start | bytes 58376 | tf_op jit(solution)/shard_map/ppermute | solution.py:27
  62.7 11.7 %collective-permute-start.7 = (f32[4864]{0:T(1024)S(1)}, f32[4864]{0:T(1024)S(1)}, u32[]{:S(2)}, u32[]{:S(2)}) collective-permute-start(f32[4864]{0:T(1024)S(1)} %reshape.382), channel_id=1, source_target_pairs={{1,0},{2,1},{3,2},{4,3},{5,4},{6,5},{7,6},{8,7},{9,8},{10,9},{11,1... | collective-permute-start | bytes 58376 | tf_op jit(solution)/shard_map/ppermute | solution.py:27

commit v4 on v3

--- a/solution.py
+++ b/solution.py
@@ -42,12 +42,23 @@
 
 def sum_over_dir(partial):
     count = lax.axis_size("dir")
-    total = partial
-    mask = 1
-    while mask < count:
-        total = total + lax.ppermute(total, "dir", [(i, i ^ mask) for i in range(count)])
-        mask *= 2
-    return total
+    assert count == 4
+    core = lax.axis_index("dir") % 2
+    cores = [(i, i ^ 1) for i in range(count)]
+    chips = [(i, i ^ 2) for i in range(count)]
+    half = partial.shape[0] // 2
+    low, high = partial[:half], partial[half:]
+    first = core == 0
+    keep = jnp.where(first, low, high)
+    give = jnp.where(first, high, low)
+    mine = keep + lax.ppermute(give, "dir", cores)
+    owned = mine + lax.ppermute(mine, "dir", chips)
+    other = lax.ppermute(owned, "dir", cores)
+    return jnp.where(
+        first,
+        jnp.concatenate([owned, other], axis=0),
+        jnp.concatenate([other, owned], axis=0),
+    )
 
 
 def station_tables(baseline_table):

time: 75.7 us -> 78.9 us (1.042)
  starting transfers between devices: 26 us -> 30 us
  waiting for transfers between devices: 36.3 us -> 35.1 us
    ppermute x4 -> x6, starting transfers between devices: 10.5 us -> 14.3 us  [the longest x2 6.63 us: sum_over_dir(): owned = mine + lax.ppermute(mine, 'dir', chips)]
    unnamed x14 -> x12, local copies, waits for them, and re-layouts: 1.65 us -> 1.11 us
    ppermute x4 -> x6, waiting for transfers between devices: 19 us -> 18.6 us  [the longest x2 13.8 us: sum_over_dir(): owned = mine + lax.ppermute(mine, 'dir', chips)]
  transfers between devices with their start and end apart: 8 -> 10, of which waited for: 6 -> 8; matrix products, arithmetic and copies ran while one was open for 0% -> 1% of each run, Pallas kernels for 0% -> 0%
where the time goes in v4:
time: 78.9 us; the launch traced here: 78.4 us
  waiting for transfers between devices  35.1 us (44%)
  starting transfers between devices  30 us (38%)
  matrix products  6.08 us (8%)
  other arithmetic  3.35 us (4%)
  local copies, waits for them, and re-layouts  2.75 us (3%)
  between operations  1.09 us (1%)
    ppermute x4, waiting for transfers between devices, send(): arrived = lax.ppermute(flat, axis, pairs)  16.5 us
    ppermute x4, starting transfers between devices, send(): arrived = lax.ppermute(flat, axis, pairs)  15.7 us
    ppermute x2, waiting for transfers between devices, sum_over_dir(): owned = mine + lax.ppermute(mine, 'dir', chips)  13.8 us
    ppermute x2, starting transfers between devices, sum_over_dir(): owned = mine + lax.ppermute(mine, 'dir', chips)  6.63 us
    ppermute x2, starting transfers between devices, sum_over_dir(): mine = keep + lax.ppermute(give, 'dir', cores)  3.84 us
    ppermute x2, starting transfers between devices, sum_over_dir(): other = lax.ppermute(owned, 'dir', cores)  3.84 us
    ppermute x2, waiting for transfers between devices, sum_over_dir(): mine = keep + lax.ppermute(give, 'dir', cores)  2.39 us
    ppermute x2, waiting for transfers between devices, sum_over_dir(): other = lax.ppermute(owned, 'dir', cores)  2.38 us
  transfers between devices with their start and end apart: 10, of which 8 were waited for; matrix products, arithmetic and copies ran while one was open for 1% of the time, Pallas kernels for 0%

profile of v4, /device:TPU:254, one launch (start us, length us, event | category | flops | bytes accessed | tf_op | source)
XLA Modules:
  0.0 78.4 jit_solution(17549454349461591083)
XLA Ops:
  0.6 0.9 %slice_reduce_fusion.1 = (s32[2850]{0:T(1024)S(1)}, s32[2850]{0:T(1024)S(1)}) fusion(s32[2,2850]{1,0:T(2,128)} %param.11), kind=kLoop, calls=%fused_computation.114 | loop fusion | bytes 45600 | tf_op jit(solution)/shard_map/slice | solution.py:66
  1.5 1.4 %convolution_bitcast_fusion.2 = f32[8,2,1,2,2,2850]{5,0,4,3,1,2:T(8,128)S(1)} fusion(s32[2850]{0:T(1024)S(1)} %get-tuple-element.7, f32[8,2,2,2,76]{4,3,2,1,0:T(2,128)} %param.8), kind=kOutput, calls=%fused_computation.2 | convolution fusion | flops 166565408 | bytes 760456 | tf_op jit(solution)/shard_map/vmap()/dot_general | solution.py:74
  2.9 0.5 convolution_bitcast_fusion.3
  3.5 0.4 copy-done.1
  4.0 0.1 multiply_add_fusion.9
  4.1 0.1 multiply_subtract_fusion.8
  4.2 0.2 fusion.35
  4.5 1.9 %collective-permute-start = (f32[1,1,2,2,2850]{4,3,2,1,0:T(2,128)S(1)}, f32[1,1,2,2,2850]{4,3,2,1,0:T(2,128)S(1)}, u32[]{:S(2)}, u32[]{:S(2)}) collective-permute-start(f32[1,1,2,2,2850]{4,3,2,1,0:T(2,128)S(1)} %select_bitcast_fusion.1), channel_id=1, source_target_pairs={{0,128},{128,0},{256,384},{384,256},{1,129},{129,1},{257,385},{385... | collective-permute-start | bytes 136808 | tf_op jit(solution)/shard_map/ppermute | solution.py:54
  6.4 1.2 %collective-permute-done = f32[1,1,2,2,2850]{4,3,2,1,0:T(2,128)S(1)} collective-permute-done((f32[1,1,2,2,2850]{4,3,2,1,0:T(2,128)S(1)}, f32[1,1,2,2,2850]{4,3,2,1,0:T(2,128)S(1)}, u32[]{:S(2)}, u32[]{:S(2)}) %collective-permute-start) | collective-permute-done | bytes 45632 | tf_op jit(solution)/shard_map/ppermute | solution.py:54
  7.6 4.7 %collective-permute-start.1 = (f32[1,1,2,2,2850]{4,3,2,1,0:T(2,128)S(1)}, f32[1,1,2,2,2850]{4,3,2,1,0:T(2,128)S(1)}, u32[]{:S(2)}, u32[]{:S(2)}) collective-permute-start(f32[1,1,2,2,2850]{4,3,2,1,0:T(2,128)S(1)} %bitcast_add_fusion.1), channel_id=1, source_target_pairs={{0,256},{128,384},{256,0},{384,128},{1,257},{129,385},{257,1},{385... | collective-permute-start | bytes 136808 | tf_op jit(solution)/shard_map/ppermute | solution.py:55
  12.3 5.9 %collective-permute-done.1 = f32[1,1,2,2,2850]{4,3,2,1,0:T(2,128)S(1)} collective-permute-done((f32[1,1,2,2,2850]{4,3,2,1,0:T(2,128)S(1)}, f32[1,1,2,2,2850]{4,3,2,1,0:T(2,128)S(1)}, u32[]{:S(2)}, u32[]{:S(2)}) %collective-permute-start.1) | collective-permute-done | bytes 45632 | tf_op jit(solution)/shard_map/ppermute | solution.py:55
  18.2 1.9 %collective-permute-start.2 = (f32[1,1,2,2,2850]{4,3,2,1,0:T(2,128)S(1)}, f32[1,1,2,2,2850]{4,3,2,1,0:T(2,128)S(1)}, u32[]{:S(2)}, u32[]{:S(2)}) collective-permute-start(f32[1,1,2,2,2850]{4,3,2,1,0:T(2,128)S(1)} %add.228), channel_id=1, source_target_pairs={{0,128},{128,0},{256,384},{384,256},{1,129},{129,1},{257,385},{385... | collective-permute-start | bytes 136808 | tf_op jit(solution)/shard_map/ppermute | solution.py:56
  20.2 1.2 %collective-permute-done.2 = f32[1,1,2,2,2850]{4,3,2,1,0:T(2,128)S(1)} collective-permute-done((f32[1,1,2,2,2850]{4,3,2,1,0:T(2,128)S(1)}, f32[1,1,2,2,2850]{4,3,2,1,0:T(2,128)S(1)}, u32[]{:S(2)}, u32[]{:S(2)}) %collective-permute-start.2) | collective-permute-done | bytes 45632 | tf_op jit(solution)/shard_map/ppermute | solution.py:56
  21.5 0.2 multiply_add_fusion.5
  21.7 0.2 multiply_subtract_fusion.6
  21.9 0.8 fusion
  22.7 0.8 fusion.21
  23.6 0.1 reshape.555
  23.7 8.0 %collective-permute-start.3 = (f32[4866]{0:T(1024)S(1)}, f32[4866]{0:T(1024)S(1)}, u32[]{:S(2)}, u32[]{:S(2)}) collective-permute-start(f32[4866]{0:T(1024)S(1)} %constant_dynamic-update-slice_fusion), channel_id=1, source_target_pairs={{0,1},{1,2},{2,3},{3,4},{4,5},{5,6},{6,7},{7,8},{8,9},{9,10},{10,1... | collective-permute-start | bytes 58400 | tf_op jit(solution)/shard_map/ppermute | solution.py:27
  31.7 1.9 %collective-permute-start.4 = (f32[4866]{0:T(1024)S(1)}, f32[4866]{0:T(1024)S(1)}, u32[]{:S(2)}, u32[]{:S(2)}) collective-permute-start(f32[4866]{0:T(1024)S(1)} %constant_dynamic-update-slice_fusion), channel_id=1, source_target_pairs={{1,0},{2,1},{3,2},{4,3},{5,4},{6,5},{7,6},{8,7},{9,8},{10,9},{11,1... | collective-permute-start | bytes 58400 | tf_op jit(solution)/shard_map/ppermute | solution.py:27
  33.6 0.1 reshape.556
  33.8 9.6 %collective-permute-done.4 = f32[4866]{0:T(1024)S(1)} collective-permute-done((f32[4866]{0:T(1024)S(1)}, f32[4866]{0:T(1024)S(1)}, u32[]{:S(2)}, u32[]{:S(2)}) %collective-permute-start.4) | collective-permute-done | bytes 19496 | tf_op jit(solution)/shard_map/ppermute | solution.py:27
  43.4 0.1 reshape.557
  43.7 0.1 fusion.59
  43.8 0.5 convolution_bitcast_fusion
  44.4 0.5 convolution_bitcast_fusion.1
  44.9 0.2 multiply_add_fusion.3
  45.2 0.2 fusion.33
  45.4 1.9 %collective-permute-start.5 = (f32[1,1,2,2,2850]{4,3,2,1,0:T(2,128)S(1)}, f32[1,1,2,2,2850]{4,3,2,1,0:T(2,128)S(1)}, u32[]{:S(2)}, u32[]{:S(2)}) collective-permute-start(f32[1,1,2,2,2850]{4,3,2,1,0:T(2,128)S(1)} %select_bitcast_fusion), channel_id=1, source_target_pairs={{0,128},{128,0},{256,384},{384,256},{1,129},{129,1},{257,385},{385... | collective-permute-start | bytes 136808 | tf_op jit(solution)/shard_map/ppermute | solution.py:54
  47.4 1.2 %collective-permute-done.5 = f32[1,1,2,2,2850]{4,3,2,1,0:T(2,128)S(1)} collective-permute-done((f32[1,1,2,2,2850]{4,3,2,1,0:T(2,128)S(1)}, f32[1,1,2,2,2850]{4,3,2,1,0:T(2,128)S(1)}, u32[]{:S(2)}, u32[]{:S(2)}) %collective-permute-start.5) | collective-permute-done | bytes 45632 | tf_op jit(solution)/shard_map/ppermute | solution.py:54
  48.6 1.9 %collective-permute-start.6 = (f32[1,1,2,2,2850]{4,3,2,1,0:T(2,128)S(1)}, f32[1,1,2,2,2850]{4,3,2,1,0:T(2,128)S(1)}, u32[]{:S(2)}, u32[]{:S(2)}) collective-permute-start(f32[1,1,2,2,2850]{4,3,2,1,0:T(2,128)S(1)} %bitcast_add_fusion), channel_id=1, source_target_pairs={{0,256},{128,384},{256,0},{384,128},{1,257},{129,385},{257,1},{385... | collective-permute-start | bytes 136808 | tf_op jit(solution)/shard_map/ppermute | solution.py:55
  50.5 7.9 %collective-permute-done.6 = f32[1,1,2,2,2850]{4,3,2,1,0:T(2,128)S(1)} collective-permute-done((f32[1,1,2,2,2850]{4,3,2,1,0:T(2,128)S(1)}, f32[1,1,2,2,2850]{4,3,2,1,0:T(2,128)S(1)}, u32[]{:S(2)}, u32[]{:S(2)}) %collective-permute-start.6) | collective-permute-done | bytes 45632 | tf_op jit(solution)/shard_map/ppermute | solution.py:55
  58.5 1.9 %collective-permute-start.7 = (f32[1,1,2,2,2850]{4,3,2,1,0:T(2,128)S(1)}, f32[1,1,2,2,2850]{4,3,2,1,0:T(2,128)S(1)}, u32[]{:S(2)}, u32[]{:S(2)}) collective-permute-start(f32[1,1,2,2,2850]{4,3,2,1,0:T(2,128)S(1)} %add.252), channel_id=1, source_target_pairs={{0,128},{128,0},{256,384},{384,256},{1,129},{129,1},{257,385},{385... | collective-permute-start | bytes 136808 | tf_op jit(solution)/shard_map/ppermute | solution.py:56
  60.4 1.2 %collective-permute-done.7 = f32[1,1,2,2,2850]{4,3,2,1,0:T(2,128)S(1)} collective-permute-done((f32[1,1,2,2,2850]{4,3,2,1,0:T(2,128)S(1)}, f32[1,1,2,2,2850]{4,3,2,1,0:T(2,128)S(1)}, u32[]{:S(2)}, u32[]{:S(2)}) %collective-permute-start.7) | collective-permute-done | bytes 45632 | tf_op jit(solution)/shard_map/ppermute | solution.py:56
  61.7 0.1 fusion.32
  61.8 0.2 multiply_add_fusion
  61.9 0.2 multiply_subtract_fusion
  62.2 0.8 fusion.10
  63.0 0.8 fusion.20
  63.8 0.1 reshape.558
  63.9 1.9 %collective-permute-start.8 = (f32[4864]{0:T(1024)S(1)}, f32[4864]{0:T(1024)S(1)}, u32[]{:S(2)}, u32[]{:S(2)}) collective-permute-start(f32[4864]{0:T(1024)S(1)} %reshape.558), channel_id=1, source_target_pairs={{0,1},{1,2},{2,3},{3,4},{4,5},{5,6},{6,7},{7,8},{8,9},{9,10},{10,1... | collective-permute-start | bytes 58376 | tf_op jit(solution)/shard_map/ppermute | solution.py:27
  65.8 3.9 %collective-permute-start.9 = (f32[4864]{0:T(1024)S(1)}, f32[4864]{0:T(1024)S(1)}, u32[]{:S(2)}, u32[]{:S(2)}) collective-permute-start(f32[4864]{0:T(1024)S(1)} %reshape.558), channel_id=1, source_target_pairs={{1,0},{2,1},{3,2},{4,3},{5,4},{6,5},{7,6},{8,7},{9,8},{10,9},{11,1... | collective-permute-start | bytes 58376 | tf_op jit(solution)/shard_map/ppermute | solution.py:27
  69.8 0.7 fusion.46
  70.5 0.1 reshape.559
  70.6 6.9 %collective-permute-done.9 = f32[4864]{0:T(1024)S(1)} collective-permute-done((f32[4864]{0:T(1024)S(1)}, f32[4864]{0:T(1024)S(1)}, u32[]{:S(2)}, u32[]{:S(2)}) %collective-permute-start.9) | collective-permute-done | bytes 19488 | tf_op jit(solution)/shard_map/ppermute | solution.py:27
  77.5 0.1 reshape.560
  77.7 0.1 fusion.50
  77.8 0.6 copy.27
  (39 shorter events, 0.8 us)
Async XLA Ops:
  1.5 1.4 %copy-start.2 = (f32[8,2,2,2,76]{4,3,2,1,0:T(2,128)S(1)}, f32[8,2,2,2,76]{4,3,2,1,0:T(2,128)}, u32[]{:S(2)}) copy-start(f32[8,2,2,2,76]{4,3,2,1,0:T(2,128)} %param.8) | copy-start | bytes 58372
  2.9 1.0 %copy-start.1 = (bf16[8,2,1,2,2,2850]{5,4,3,2,1,0:T(2,128)(2,1)S(1)}, bf16[8,2,1,2,2,2850]{5,4,3,2,1,0:T(2,128)(2,1)}, u32[]{:S(2)}) copy-start(bf16[8,2,1,2,2,2850]{5,4,3,2,1,0:T(2,128)(2,1)} %param.7) | copy-start | bytes 1094404
  4.2 17.2 %copy-start = (f32[2,1,2,2,2850]{4,3,2,1,0:T(2,128)S(1)}, f32[2,1,2,2,2850]{4,3,2,1,0:T(2,128)}, u32[]{:S(2)}) copy-start(f32[2,1,2,2,2850]{4,3,2,1,0:T(2,128)} %param.6) | copy-start | bytes 273604
  4.5 3.1 %collective-permute-start = (f32[1,1,2,2,2850]{4,3,2,1,0:T(2,128)S(1)}, f32[1,1,2,2,2850]{4,3,2,1,0:T(2,128)S(1)}, u32[]{:S(2)}, u32[]{:S(2)}) collective-permute-start(f32[1,1,2,2,2850]{4,3,2,1,0:T(2,128)S(1)} %select_bitcast_fusion.1), channel_id=1, source_target_pairs={{0,128},{128,0},{256,384},{384,256},{1,129},{129,1},{257,385},{385... | collective-permute-start | bytes 136808 | tf_op jit(solution)/shard_map/ppermute | solution.py:54
  7.6 10.6 %collective-permute-start.1 = (f32[1,1,2,2,2850]{4,3,2,1,0:T(2,128)S(1)}, f32[1,1,2,2,2850]{4,3,2,1,0:T(2,128)S(1)}, u32[]{:S(2)}, u32[]{:S(2)}) collective-permute-start(f32[1,1,2,2,2850]{4,3,2,1,0:T(2,128)S(1)} %bitcast_add_fusion.1), channel_id=1, source_target_pairs={{0,256},{128,384},{256,0},{384,128},{1,257},{129,385},{257,1},{385... | collective-permute-start | bytes 136808 | tf_op jit(solution)/shard_map/ppermute | solution.py:55
  18.2 3.1 %collective-permute-start.2 = (f32[1,1,2,2,2850]{4,3,2,1,0:T(2,128)S(1)}, f32[1,1,2,2,2850]{4,3,2,1,0:T(2,128)S(1)}, u32[]{:S(2)}, u32[]{:S(2)}) collective-permute-start(f32[1,1,2,2,2850]{4,3,2,1,0:T(2,128)S(1)} %add.228), channel_id=1, source_target_pairs={{0,128},{128,0},{256,384},{384,256},{1,129},{129,1},{257,385},{385... | collective-permute-start | bytes 136808 | tf_op jit(solution)/shard_map/ppermute | solution.py:56
  22.7 1.0 %copy-start.3 = (f32[2]{0:T(128)S(1)}, f32[2]{0:T(128)}, u32[]{:S(2)}) copy-start(f32[2]{0:T(128)} %param.9) | copy-start | bytes 28
  22.7 20.9 %copy-start.4 = (s32[2]{0:T(128)S(1)}, s32[2]{0:T(128)}, u32[]{:S(2)}) copy-start(s32[2]{0:T(128)} %param.10) | copy-start | bytes 28
  23.7 9.9 %collective-permute-start.3 = (f32[4866]{0:T(1024)S(1)}, f32[4866]{0:T(1024)S(1)}, u32[]{:S(2)}, u32[]{:S(2)}) collective-permute-start(f32[4866]{0:T(1024)S(1)} %constant_dynamic-update-slice_fusion), channel_id=1, source_target_pairs={{0,1},{1,2},{2,3},{3,4},{4,5},{5,6},{6,7},{7,8},{8,9},{9,10},{10,1... | collective-permute-start | bytes 58400 | tf_op jit(solution)/shard_map/ppermute | solution.py:27
  31.7 11.7 %collective-permute-start.4 = (f32[4866]{0:T(1024)S(1)}, f32[4866]{0:T(1024)S(1)}, u32[]{:S(2)}, u32[]{:S(2)}) collective-permute-start(f32[4866]{0:T(1024)S(1)} %constant_dynamic-update-slice_fusion), channel_id=1, source_target_pairs={{1,0},{2,1},{3,2},{4,3},{5,4},{6,5},{7,6},{8,7},{9,8},{10,9},{11,1... | collective-permute-start | bytes 58400 | tf_op jit(solution)/shard_map/ppermute | solution.py:27
  45.4 3.1 %collective-permute-start.5 = (f32[1,1,2,2,2850]{4,3,2,1,0:T(2,128)S(1)}, f32[1,1,2,2,2850]{4,3,2,1,0:T(2,128)S(1)}, u32[]{:S(2)}, u32[]{:S(2)}) collective-permute-start(f32[1,1,2,2,2850]{4,3,2,1,0:T(2,128)S(1)} %select_bitcast_fusion), channel_id=1, source_target_pairs={{0,128},{128,0},{256,384},{384,256},{1,129},{129,1},{257,385},{385... | collective-permute-start | bytes 136808 | tf_op jit(solution)/shard_map/ppermute | solution.py:54
  48.6 9.9 %collective-permute-start.6 = (f32[1,1,2,2,2850]{4,3,2,1,0:T(2,128)S(1)}, f32[1,1,2,2,2850]{4,3,2,1,0:T(2,128)S(1)}, u32[]{:S(2)}, u32[]{:S(2)}) collective-permute-start(f32[1,1,2,2,2850]{4,3,2,1,0:T(2,128)S(1)} %bitcast_add_fusion), channel_id=1, source_target_pairs={{0,256},{128,384},{256,0},{384,128},{1,257},{129,385},{257,1},{385... | collective-permute-start | bytes 136808 | tf_op jit(solution)/shard_map/ppermute | solution.py:55
  58.5 3.1 %collective-permute-start.7 = (f32[1,1,2,2,2850]{4,3,2,1,0:T(2,128)S(1)}, f32[1,1,2,2,2850]{4,3,2,1,0:T(2,128)S(1)}, u32[]{:S(2)}, u32[]{:S(2)}) collective-permute-start(f32[1,1,2,2,2850]{4,3,2,1,0:T(2,128)S(1)} %add.252), channel_id=1, source_target_pairs={{0,128},{128,0},{256,384},{384,256},{1,129},{129,1},{257,385},{385... | collective-permute-start | bytes 136808 | tf_op jit(solution)/shard_map/ppermute | solution.py:56
  63.9 6.6 %collective-permute-start.8 = (f32[4864]{0:T(1024)S(1)}, f32[4864]{0:T(1024)S(1)}, u32[]{:S(2)}, u32[]{:S(2)}) collective-permute-start(f32[4864]{0:T(1024)S(1)} %reshape.558), channel_id=1, source_target_pairs={{0,1},{1,2},{2,3},{3,4},{4,5},{5,6},{6,7},{7,8},{8,9},{9,10},{10,1... | collective-permute-start | bytes 58376 | tf_op jit(solution)/shard_map/ppermute | solution.py:27
  65.8 11.7 %collective-permute-start.9 = (f32[4864]{0:T(1024)S(1)}, f32[4864]{0:T(1024)S(1)}, u32[]{:S(2)}, u32[]{:S(2)}) collective-permute-start(f32[4864]{0:T(1024)S(1)} %reshape.558), channel_id=1, source_target_pairs={{1,0},{2,1},{3,2},{4,3},{5,4},{6,5},{7,6},{8,7},{9,8},{10,9},{11,1... | collective-permute-start | bytes 58376 | tf_op jit(solution)/shard_map/ppermute | solution.py:27

commit v5 on v3

--- a/solution.py
+++ b/solution.py
@@ -42,12 +42,9 @@
 
 def sum_over_dir(partial):
     count = lax.axis_size("dir")
-    total = partial
-    mask = 1
-    while mask < count:
-        total = total + lax.ppermute(total, "dir", [(i, i ^ mask) for i in range(count)])
-        mask *= 2
-    return total
+    spread = jnp.broadcast_to(partial[None], (count,) + partial.shape)
+    parts = lax.all_to_all(spread, "dir", 0, 0)
+    return (parts[0] + parts[1]) + (parts[2] + parts[3])
 
 
 def station_tables(baseline_table):

time: 75.7 us -> 79.7 us (1.053)
  blocking collectives: 0 us -> 15.4 us
  waiting for transfers between devices: 36.3 us -> 24.9 us
  local copies, waits for them, and re-layouts: 3.28 us -> 4.21 us
  starting transfers between devices: 26 us -> 25.1 us
    ppermute x4 -> x0, waiting for transfers between devices: 19 us -> none  [sum_over_dir(): lax.ppermute(total, 'dir', [(i, i ^ mask) for i in range(count)])]
    all_to_all x0 -> x1, blocking collectives: none -> 15.4 us  [sum_over_dir(): parts = lax.all_to_all(spread, 'dir', 0, 0)]
    ppermute x4 -> x0, starting transfers between devices: 10.5 us -> none  [sum_over_dir(): lax.ppermute(total, 'dir', [(i, i ^ mask) for i in range(count)])]
    all_to_all x0 -> x1, starting transfers between devices: none -> 7.2 us  [sum_over_dir(): parts = lax.all_to_all(spread, 'dir', 0, 0)]
    all_to_all x0 -> x1, waiting for transfers between devices: none -> 5.7 us  [sum_over_dir(): parts = lax.all_to_all(spread, 'dir', 0, 0)]
    ppermute x4, starting transfers between devices: 15.5 us -> 17.9 us  [send(): arrived = lax.ppermute(flat, axis, pairs)]
    ppermute x4, waiting for transfers between devices: 17.2 us -> 19.2 us  [send(): arrived = lax.ppermute(flat, axis, pairs)]
    broadcast_in_dim x0 -> x2, local copies, waits for them, and re-layouts: none -> 0.93 us  [sum_over_dir(): spread = jnp.broadcast_to(partial[None], (count,) + partial.shape)]
  transfers between devices with their start and end apart: 8 -> 5, of which waited for: 6 -> 3; matrix products, arithmetic and copies ran while one was open for 0% -> 0% of each run, Pallas kernels for 0% -> 0%
where the time goes in v5:
time: 79.7 us; the launch traced here: 79.2 us
  starting transfers between devices  25.1 us (31%)
  waiting for transfers between devices  24.9 us (31%)
  blocking collectives  15.4 us (19%)
  matrix products  6.07 us (8%)
  local copies, waits for them, and re-layouts  4.21 us (5%)
  other arithmetic  2.55 us (3%)
  between operations  1.03 us (1%)
    ppermute x4, waiting for transfers between devices, send(): arrived = lax.ppermute(flat, axis, pairs)  19.2 us
    ppermute x4, starting transfers between devices, send(): arrived = lax.ppermute(flat, axis, pairs)  17.9 us
    all_to_all x1, blocking collectives, sum_over_dir(): parts = lax.all_to_all(spread, 'dir', 0, 0)  15.4 us
    all_to_all x1, starting transfers between devices, sum_over_dir(): parts = lax.all_to_all(spread, 'dir', 0, 0)  7.2 us
    all_to_all x1, waiting for transfers between devices, sum_over_dir(): parts = lax.all_to_all(spread, 'dir', 0, 0)  5.7 us
    dot_general x2, matrix products, corrupt(): right_gain = jnp.matmul(gains, right_hot, precision=highest)[:, None]  1.89 us
    unnamed x16, local copies, waits for them, and re-layouts  1.65 us
  transfers between devices with their start and end apart: 5, of which 3 were waited for; matrix products, arithmetic and copies ran while one was open for 0% of the time, Pallas kernels for 0%

profile of v5, /device:TPU:254, one launch (start us, length us, event | category | flops | bytes accessed | tf_op | source)
XLA Modules:
  0.0 79.2 jit_solution(685344215560342080)
XLA Ops:
  0.6 0.9 %slice_reduce_fusion.1 = (s32[2850]{0:T(1024)S(1)}, s32[2850]{0:T(1024)S(1)}) fusion(s32[2,2850]{1,0:T(2,128)} %param.11), kind=kLoop, calls=%fused_computation.116 | loop fusion | bytes 45600 | tf_op jit(solution)/shard_map/slice | solution.py:52
  1.5 1.3 %convolution_bitcast_fusion.2 = f32[8,2,1,2,2,2850]{5,0,4,3,1,2:T(8,128)S(1)} fusion(s32[2850]{0:T(1024)S(1)} %get-tuple-element.7, f32[8,2,2,2,76]{4,3,2,1,0:T(2,128)} %param.8), kind=kOutput, calls=%fused_computation.2 | convolution fusion | flops 166565408 | bytes 760456 | tf_op jit(solution)/shard_map/vmap()/dot_general | solution.py:60
  2.9 0.5 convolution_bitcast_fusion.3
  3.4 0.4 copy-done
  3.9 0.1 copy_convert_fusion
  3.9 0.1 multiply_add_fusion.9
  4.1 0.1 multiply_subtract_fusion.8
  4.2 0.2 fusion.35
  4.4 0.8 %broadcast_in_dim.14 = f32[4,2,1,2,2,2850]{5,4,3,1,2,0:T(2,128)} broadcast(f32[2,2,2,2850]{3,2,1,0:T(2,128)S(1)} %fusion.35), dimensions={1,3,4,5} | broadcast | bytes 456000 | tf_op jit(solution)/shard_map/broadcast_in_dim | solution.py:45
  5.2 7.2 %all-to-all-start = ((f32[4,2,1,2,2,2850]{5,4,3,1,2,0:T(2,128)}), f32[4,2,1,2,2,2850]{5,4,3,1,2,0:T(2,128)S(1)}, u32[]{:S(2)}, u32[]{:S(2)}) async-start(f32[4,2,1,2,2,2850]{5,4,3,1,2,0:T(2,128)} %broadcast_in_dim.14), calls=%async_computation | async-start | bytes 753664 | tf_op jit(solution)/shard_map/all_to_all | solution.py:46
  12.4 5.7 %all-to-all-done = f32[4,2,1,2,2,2850]{5,4,3,1,2,0:T(2,128)S(1)} async-done(((f32[4,2,1,2,2,2850]{5,4,3,1,2,0:T(2,128)}), f32[4,2,1,2,2,2850]{5,4,3,1,2,0:T(2,128)S(1)}, u32[]{:S(2)}, u32[]{:S(2)}) %all-to-all-start) | async-done | bytes 364832 | tf_op jit(solution)/shard_map/all_to_all | solution.py:46
  18.1 0.1 fusion.50
  18.2 0.1 fusion.34
  18.3 0.2 multiply_add_fusion.5
  18.6 0.2 multiply_subtract_fusion.6
  18.8 0.8 fusion
  19.6 0.8 fusion.21
  20.4 0.1 reshape.481
  20.6 9.5 %collective-permute-start = (f32[4866]{0:T(1024)S(1)}, f32[4866]{0:T(1024)S(1)}, u32[]{:S(2)}, u32[]{:S(2)}) collective-permute-start(f32[4866]{0:T(1024)S(1)} %constant_dynamic-update-slice_fusion), channel_id=1, source_target_pairs={{0,1},{1,2},{2,3},{3,4},{4,5},{5,6},{6,7},{7,8},{8,9},{9,10},{10,1... | collective-permute-start | bytes 58400 | tf_op jit(solution)/shard_map/ppermute | solution.py:27
  30.1 1.9 %collective-permute-start.1 = (f32[4866]{0:T(1024)S(1)}, f32[4866]{0:T(1024)S(1)}, u32[]{:S(2)}, u32[]{:S(2)}) collective-permute-start(f32[4866]{0:T(1024)S(1)} %constant_dynamic-update-slice_fusion), channel_id=1, source_target_pairs={{1,0},{2,1},{3,2},{4,3},{5,4},{6,5},{7,6},{8,7},{9,8},{10,9},{11,1... | collective-permute-start | bytes 58400 | tf_op jit(solution)/shard_map/ppermute | solution.py:27
  32.0 0.1 reshape.482
  32.1 9.6 %collective-permute-done.1 = f32[4866]{0:T(1024)S(1)} collective-permute-done((f32[4866]{0:T(1024)S(1)}, f32[4866]{0:T(1024)S(1)}, u32[]{:S(2)}, u32[]{:S(2)}) %collective-permute-start.1) | collective-permute-done | bytes 19496 | tf_op jit(solution)/shard_map/ppermute | solution.py:27
  41.8 0.1 reshape.483
  41.9 0.1 pad_maximum_fusion.7
  42.0 0.1 add_add_fusion
  42.1 0.1 fusion.63
  42.2 0.5 convolution_bitcast_fusion
  42.7 0.5 convolution_bitcast_fusion.1
  43.3 0.2 multiply_add_fusion.3
  43.4 0.1 multiply_subtract_fusion.3
  43.5 0.2 fusion.33
  43.8 0.1 broadcast_in_dim.17
  43.9 15.4 %all_to_all.10 = f32[4,2,1,2,2,2850]{5,4,3,1,2,0:T(2,128)S(1)} all-to-all(f32[4,2,1,2,2,2850]{5,4,3,1,2,0:T(2,128)S(1)} %broadcast_in_dim.17), channel_id=1, replica_groups=mesh['dir'=4,'chan'=128] {'dir'}, dimensions={0} | all-to-all | bytes 729600 | tf_op jit(solution)/shard_map/all_to_all | solution.py:46
  59.2 0.1 fusion.46
  59.3 0.1 fusion.32
  59.4 0.5 copy-done.1
  60.0 0.2 multiply_add_fusion
  60.1 0.2 multiply_subtract_fusion
  60.4 0.8 fusion.10
  61.2 0.8 fusion.20
  62.0 0.1 reshape.484
  62.1 4.5 %collective-permute-start.2 = (f32[4864]{0:T(1024)S(1)}, f32[4864]{0:T(1024)S(1)}, u32[]{:S(2)}, u32[]{:S(2)}) collective-permute-start(f32[4864]{0:T(1024)S(1)} %reshape.484), channel_id=1, source_target_pairs={{0,1},{1,2},{2,3},{3,4},{4,5},{5,6},{6,7},{7,8},{8,9},{9,10},{10,1... | collective-permute-start | bytes 58376 | tf_op jit(solution)/shard_map/ppermute | solution.py:27
  66.7 1.9 %collective-permute-start.3 = (f32[4864]{0:T(1024)S(1)}, f32[4864]{0:T(1024)S(1)}, u32[]{:S(2)}, u32[]{:S(2)}) collective-permute-start(f32[4864]{0:T(1024)S(1)} %reshape.484), channel_id=1, source_target_pairs={{1,0},{2,1},{3,2},{4,3},{5,4},{6,5},{7,6},{8,7},{9,8},{10,9},{11,1... | collective-permute-start | bytes 58376 | tf_op jit(solution)/shard_map/ppermute | solution.py:27
  68.6 0.1 reshape.485
  68.7 9.6 %collective-permute-done.3 = f32[4864]{0:T(1024)S(1)} collective-permute-done((f32[4864]{0:T(1024)S(1)}, f32[4864]{0:T(1024)S(1)}, u32[]{:S(2)}, u32[]{:S(2)}) %collective-permute-start.3) | collective-permute-done | bytes 19488 | tf_op jit(solution)/shard_map/ppermute | solution.py:27
  78.4 0.1 reshape.486
  78.5 0.1 fusion.54
  78.6 0.6 copy.27
  (29 shorter events, 0.2 us)
Async XLA Ops:
  1.5 1.4 %copy-start.3 = (f32[8,2,2,2,76]{4,3,2,1,0:T(2,128)S(1)}, f32[8,2,2,2,76]{4,3,2,1,0:T(2,128)}, u32[]{:S(2)}) copy-start(f32[8,2,2,2,76]{4,3,2,1,0:T(2,128)} %param.8) | copy-start | bytes 58372
  2.9 1.0 %copy-start = (bf16[8,2,1,2,2,2850]{5,4,3,2,1,0:T(2,128)(2,1)S(1)}, bf16[8,2,1,2,2,2850]{5,4,3,2,1,0:T(2,128)(2,1)}, u32[]{:S(2)}) copy-start(bf16[8,2,1,2,2,2850]{5,4,3,2,1,0:T(2,128)(2,1)} %param.7) | copy-start | bytes 1094404
  4.4 13.7 %copy-start.2 = (f32[2,1,2,2,2850]{4,3,2,1,0:T(2,128)S(1)}, f32[2,1,2,2,2850]{4,3,2,1,0:T(2,128)}, u32[]{:S(2)}) copy-start(f32[2,1,2,2,2850]{4,3,2,1,0:T(2,128)} %param.6) | copy-start | bytes 273604
  5.2 12.9 %all-to-all-start = ((f32[4,2,1,2,2,2850]{5,4,3,1,2,0:T(2,128)}), f32[4,2,1,2,2,2850]{5,4,3,1,2,0:T(2,128)S(1)}, u32[]{:S(2)}, u32[]{:S(2)}) async-start(f32[4,2,1,2,2,2850]{5,4,3,1,2,0:T(2,128)} %broadcast_in_dim.14), calls=%async_computation | async-start | bytes 753664 | tf_op jit(solution)/shard_map/all_to_all | solution.py:46
  19.5 1.0 %copy-start.6 = (f32[4866]{0:T(1024)S(1)}, f32[4866]{0:T(1024)}, u32[]{:S(2)}) copy-start(f32[4866]{0:T(1024)} %custom-call) | copy-start | bytes 58396
  19.6 1.0 %copy-start.4 = (f32[2]{0:T(128)S(1)}, f32[2]{0:T(128)}, u32[]{:S(2)}) copy-start(f32[2]{0:T(128)} %param.9) | copy-start | bytes 28
  19.6 22.4 %copy-start.5 = (s32[2]{0:T(128)S(1)}, s32[2]{0:T(128)}, u32[]{:S(2)}) copy-start(s32[2]{0:T(128)} %param.10) | copy-start | bytes 28
  20.6 11.4 %collective-permute-start = (f32[4866]{0:T(1024)S(1)}, f32[4866]{0:T(1024)S(1)}, u32[]{:S(2)}, u32[]{:S(2)}) collective-permute-start(f32[4866]{0:T(1024)S(1)} %constant_dynamic-update-slice_fusion), channel_id=1, source_target_pairs={{0,1},{1,2},{2,3},{3,4},{4,5},{5,6},{6,7},{7,8},{8,9},{9,10},{10,1... | collective-permute-start | bytes 58400 | tf_op jit(solution)/shard_map/ppermute | solution.py:27
  30.1 11.7 %collective-permute-start.1 = (f32[4866]{0:T(1024)S(1)}, f32[4866]{0:T(1024)S(1)}, u32[]{:S(2)}, u32[]{:S(2)}) collective-permute-start(f32[4866]{0:T(1024)S(1)} %constant_dynamic-update-slice_fusion), channel_id=1, source_target_pairs={{1,0},{2,1},{3,2},{4,3},{5,4},{6,5},{7,6},{8,7},{9,8},{10,9},{11,1... | collective-permute-start | bytes 58400 | tf_op jit(solution)/shard_map/ppermute | solution.py:27
  59.3 0.6 copy-start.1
  62.1 6.5 %collective-permute-start.2 = (f32[4864]{0:T(1024)S(1)}, f32[4864]{0:T(1024)S(1)}, u32[]{:S(2)}, u32[]{:S(2)}) collective-permute-start(f32[4864]{0:T(1024)S(1)} %reshape.484), channel_id=1, source_target_pairs={{0,1},{1,2},{2,3},{3,4},{4,5},{5,6},{6,7},{7,8},{8,9},{9,10},{10,1... | collective-permute-start | bytes 58376 | tf_op jit(solution)/shard_map/ppermute | solution.py:27
  66.7 11.7 %collective-permute-start.3 = (f32[4864]{0:T(1024)S(1)}, f32[4864]{0:T(1024)S(1)}, u32[]{:S(2)}, u32[]{:S(2)}) collective-permute-start(f32[4864]{0:T(1024)S(1)} %reshape.484), channel_id=1, source_target_pairs={{1,0},{2,1},{3,2},{4,3},{5,4},{6,5},{7,6},{8,7},{9,8},{10,9},{11,1... | collective-permute-start | bytes 58376 | tf_op jit(solution)/shard_map/ppermute | solution.py:27

commit v6 on v3

--- a/solution.py
+++ b/solution.py
@@ -50,6 +50,16 @@
     return total
 
 
+def table_dot(values, table):
+    high = lax.reduce_precision(values, exponent_bits=8, mantissa_bits=7)
+    rest = values - high
+    middle = lax.reduce_precision(rest, exponent_bits=8, mantissa_bits=7)
+    low = rest - middle
+    parts = jnp.stack([high, middle, low]).astype(jnp.bfloat16)
+    out = jnp.matmul(parts, table.astype(jnp.bfloat16), preferred_element_type=jnp.float32)
+    return (out[0] + out[1]) + out[2]
+
+
 def station_tables(baseline_table):
     column = jnp.arange(STATIONS, dtype=jnp.int32)[:, None]
     left_hot = (baseline_table[0][None, :] == column).astype(jnp.float32)
@@ -59,8 +69,8 @@
 
 def corrupt(gains, model, left_hot, right_hot):
     model = model.astype(jnp.float32)
-    left_gain = jnp.matmul(gains, left_hot, precision=highest)[:, None]
-    right_gain = jnp.matmul(gains, right_hot, precision=highest)[:, None]
+    left_gain = table_dot(gains, left_hot)[:, None]
+    right_gain = table_dot(gains, right_hot)[:, None]
     left_re, left_im = (left_gain[..., 0, :], left_gain[..., 1, :])
     right_re, right_im = (right_gain[..., 0, :], right_gain[..., 1, :])
     model_re, model_im = (model[..., 0, :], model[..., 1, :])
@@ -88,9 +98,7 @@
     right_den = power * (left_re * left_re + left_im * left_im)
     left_products = jnp.sum(jnp.stack([left_num_re, left_num_im, left_den], axis=3), axis=1)
     right_terms = jnp.sum(jnp.stack([right_num_re, right_num_im, right_den], axis=3), axis=1)
-    totals = jnp.matmul(left_products, left_hot.T, precision=highest) + jnp.matmul(
-        right_terms, right_hot.T, precision=highest
-    )
+    totals = table_dot(left_products, left_hot.T) + table_dot(right_terms, right_hot.T)
     solved = totals[:, :, 0:2] / (totals[:, :, 2:3] + epsilon)
     return (1.0 - step_size) * gains + step_size * solved
 

time: 75.7 us -> 76.2 us (level)
  other arithmetic: 2.57 us -> 4.73 us
  matrix products: 6.06 us -> 4.26 us
    dot_general x8, matrix products: 6.06 us -> 4.26 us  [table_dot(): jnp.matmul(parts, table.astype(jnp.bfloat16), preferred_element_type=jnp....]
    another operation x0 -> x7, other arithmetic: none -> 1.79 us
where the time goes in v6:
time: 76.2 us; the launch traced here: 75.6 us
  waiting for transfers between devices  36.3 us (48%)
  starting transfers between devices  26 us (34%)
  other arithmetic  4.73 us (6%)
  matrix products  4.26 us (6%)
  local copies, waits for them, and re-layouts  3.25 us (4%)
  between operations  1.13 us (1%)
    ppermute x4, waiting for transfers between devices, sum_over_dir(): lax.ppermute(total, 'dir', [(i, i ^ mask) for i in range(count)])  19 us
    ppermute x4, waiting for transfers between devices, send(): arrived = lax.ppermute(flat, axis, pairs)  17.2 us
    ppermute x4, starting transfers between devices, send(): arrived = lax.ppermute(flat, axis, pairs)  15.5 us
    ppermute x4, starting transfers between devices, sum_over_dir(): lax.ppermute(total, 'dir', [(i, i ^ mask) for i in range(count)])  10.5 us
    dot_general x8, matrix products, table_dot(): jnp.matmul(parts, table.astype(jnp.bfloat16), preferred_element_type=jnp....  4.26 us
    unnamed x14, local copies, waits for them, and re-layouts  1.62 us
  transfers between devices with their start and end apart: 8, of which 6 were waited for; matrix products, arithmetic and copies ran while one was open for 0% of the time, Pallas kernels for 0%

profile of v6, /device:TPU:254, one launch (start us, length us, event | category | flops | bytes accessed | tf_op | source)
XLA Modules:
  0.0 75.6 jit_solution(8379604902109501934)
XLA Ops:
  0.6 0.9 %slice_reduce_fusion = (s32[2850]{0:T(1024)S(1)}, s32[2850]{0:T(1024)S(1)}) fusion(s32[2,2850]{1,0:T(2,128)} %param.11), kind=kLoop, calls=%fused_computation.176 | loop fusion | bytes 45600 | tf_op jit(solution)/shard_map/slice | solution.py:66
  1.5 0.8 %fusion.86 = (bf16[1,8,2,2,2,76]{5,1,4,3,2,0:T(8,128)(2,1)S(1)}, bf16[1,8,2,2,2,76]{5,1,4,3,2,0:T(8,128)(2,1)S(1)}, bf16[1,8,2,2,2,76]{5,1,4,3,2,0:T(8,128)(2,1)S(1)}) fusion(f32[8,2,2,2,76]{4,3,2,1,0:T(2,128)} %param.8), kind=kLoop, calls=%fused_computation.168 | loop fusion | flops 34048 | bytes 48640 | tf_op jit(solution)/shard_map/vmap()/stack | solution.py:58
  2.3 0.4 fusion.39
  2.7 0.4 fusion.44
  3.2 0.5 copy-done
  3.8 0.2 fusion.30
  4.0 0.1 multiply_add_fusion.9
  4.2 0.2 fusion.35
  4.5 1.9 %collective-permute-start = (f32[2,1,2,2,2850]{4,3,2,1,0:T(2,128)S(1)}, f32[2,1,2,2,2850]{4,3,2,1,0:T(2,128)S(1)}, u32[]{:S(2)}, u32[]{:S(2)}) collective-permute-start(f32[2,1,2,2,2850]{4,3,2,1,0:T(2,128)S(1)} %bitcast.94), channel_id=1, source_target_pairs={{0,128},{128,0},{256,384},{384,256},{1,129},{129,1},{257,385},{385... | collective-permute-start | bytes 273608 | tf_op jit(solution)/shard_map/ppermute | solution.py:48
  6.4 1.3 %collective-permute-done = f32[2,1,2,2,2850]{4,3,2,1,0:T(2,128)S(1)} collective-permute-done((f32[2,1,2,2,2850]{4,3,2,1,0:T(2,128)S(1)}, f32[2,1,2,2,2850]{4,3,2,1,0:T(2,128)S(1)}, u32[]{:S(2)}, u32[]{:S(2)}) %collective-permute-start) | collective-permute-done | bytes 91232 | tf_op jit(solution)/shard_map/ppermute | solution.py:48
  7.7 4.7 %collective-permute-start.1 = (f32[2,1,2,2,2850]{4,3,2,1,0:T(2,128)S(1)}, f32[2,1,2,2,2850]{4,3,2,1,0:T(2,128)S(1)}, u32[]{:S(2)}, u32[]{:S(2)}) collective-permute-start(f32[2,1,2,2,2850]{4,3,2,1,0:T(2,128)S(1)} %bitcast_add_fusion.1), channel_id=1, source_target_pairs={{0,256},{128,384},{256,0},{384,128},{1,257},{129,385},{257,1},{385... | collective-permute-start | bytes 273608 | tf_op jit(solution)/shard_map/ppermute | solution.py:48
  12.4 7.9 %collective-permute-done.1 = f32[2,1,2,2,2850]{4,3,2,1,0:T(2,128)S(1)} collective-permute-done((f32[2,1,2,2,2850]{4,3,2,1,0:T(2,128)S(1)}, f32[2,1,2,2,2850]{4,3,2,1,0:T(2,128)S(1)}, u32[]{:S(2)}, u32[]{:S(2)}) %collective-permute-start.1) | collective-permute-done | bytes 91232 | tf_op jit(solution)/shard_map/ppermute | solution.py:48
  20.4 0.2 multiply_subtract_fusion.6
  20.7 0.2 multiply_add_fusion.5
  20.9 0.2 reduce-precision_convert_fusion.7
  21.1 0.6 fusion
  21.7 0.2 reduce-precision_convert_fusion.5
  22.0 0.6 fusion.6
  22.8 0.1 reshape.649
  22.9 7.7 %collective-permute-start.2 = (f32[4866]{0:T(1024)S(1)}, f32[4866]{0:T(1024)S(1)}, u32[]{:S(2)}, u32[]{:S(2)}) collective-permute-start(f32[4866]{0:T(1024)S(1)} %constant_dynamic-update-slice_fusion), channel_id=1, source_target_pairs={{0,1},{1,2},{2,3},{3,4},{4,5},{5,6},{6,7},{7,8},{8,9},{9,10},{10,1... | collective-permute-start | bytes 58400 | tf_op jit(solution)/shard_map/ppermute | solution.py:27
  30.7 1.9 %collective-permute-start.3 = (f32[4866]{0:T(1024)S(1)}, f32[4866]{0:T(1024)S(1)}, u32[]{:S(2)}, u32[]{:S(2)}) collective-permute-start(f32[4866]{0:T(1024)S(1)} %constant_dynamic-update-slice_fusion), channel_id=1, source_target_pairs={{1,0},{2,1},{3,2},{4,3},{5,4},{6,5},{7,6},{8,7},{9,8},{10,9},{11,1... | collective-permute-start | bytes 58400 | tf_op jit(solution)/shard_map/ppermute | solution.py:27
  32.6 0.1 reshape.650
  32.8 9.6 %collective-permute-done.3 = f32[4866]{0:T(1024)S(1)} collective-permute-done((f32[4866]{0:T(1024)S(1)}, f32[4866]{0:T(1024)S(1)}, u32[]{:S(2)}, u32[]{:S(2)}) %collective-permute-start.3) | collective-permute-done | bytes 19496 | tf_op jit(solution)/shard_map/ppermute | solution.py:27
  42.4 0.1 reshape.651
  42.8 0.4 fusion.37
  43.3 0.4 fusion.42
  43.7 0.1 fusion.29
  43.8 0.1 fusion.28
  43.9 0.2 multiply_add_fusion.3
  44.2 0.2 fusion.33
  44.4 1.9 %collective-permute-start.4 = (f32[2,1,2,2,2850]{4,3,2,1,0:T(2,128)S(1)}, f32[2,1,2,2,2850]{4,3,2,1,0:T(2,128)S(1)}, u32[]{:S(2)}, u32[]{:S(2)}) collective-permute-start(f32[2,1,2,2,2850]{4,3,2,1,0:T(2,128)S(1)} %bitcast.95), channel_id=1, source_target_pairs={{0,128},{128,0},{256,384},{384,256},{1,129},{129,1},{257,385},{385... | collective-permute-start | bytes 273608 | tf_op jit(solution)/shard_map/ppermute | solution.py:48
  46.4 1.3 %collective-permute-done.4 = f32[2,1,2,2,2850]{4,3,2,1,0:T(2,128)S(1)} collective-permute-done((f32[2,1,2,2,2850]{4,3,2,1,0:T(2,128)S(1)}, f32[2,1,2,2,2850]{4,3,2,1,0:T(2,128)S(1)}, u32[]{:S(2)}, u32[]{:S(2)}) %collective-permute-start.4) | collective-permute-done | bytes 91232 | tf_op jit(solution)/shard_map/ppermute | solution.py:48
  47.7 1.9 %collective-permute-start.5 = (f32[2,1,2,2,2850]{4,3,2,1,0:T(2,128)S(1)}, f32[2,1,2,2,2850]{4,3,2,1,0:T(2,128)S(1)}, u32[]{:S(2)}, u32[]{:S(2)}) collective-permute-start(f32[2,1,2,2,2850]{4,3,2,1,0:T(2,128)S(1)} %bitcast_add_fusion), channel_id=1, source_target_pairs={{0,256},{128,384},{256,0},{384,128},{1,257},{129,385},{257,1},{385... | collective-permute-start | bytes 273608 | tf_op jit(solution)/shard_map/ppermute | solution.py:48
  49.6 8.6 %collective-permute-done.5 = f32[2,1,2,2,2850]{4,3,2,1,0:T(2,128)S(1)} collective-permute-done((f32[2,1,2,2,2850]{4,3,2,1,0:T(2,128)S(1)}, f32[2,1,2,2,2850]{4,3,2,1,0:T(2,128)S(1)}, u32[]{:S(2)}, u32[]{:S(2)}) %collective-permute-start.5) | collective-permute-done | bytes 91232 | tf_op jit(solution)/shard_map/ppermute | solution.py:48
  58.4 0.2 multiply_subtract_fusion.1
  58.6 0.4 copy-done.2
  59.0 0.2 multiply_add_fusion.1
  59.2 0.2 reduce-precision_convert_fusion.3
  59.4 0.6 fusion.12
  60.1 0.2 reduce-precision_convert_fusion.1
  60.3 0.6 fusion.18
  61.0 0.1 reshape.652
  61.1 1.9 %collective-permute-start.6 = (f32[4864]{0:T(1024)S(1)}, f32[4864]{0:T(1024)S(1)}, u32[]{:S(2)}, u32[]{:S(2)}) collective-permute-start(f32[4864]{0:T(1024)S(1)} %reshape.652), channel_id=1, source_target_pairs={{0,1},{1,2},{2,3},{3,4},{4,5},{5,6},{6,7},{7,8},{8,9},{9,10},{10,1... | collective-permute-start | bytes 58376 | tf_op jit(solution)/shard_map/ppermute | solution.py:27
  63.1 3.9 %collective-permute-start.7 = (f32[4864]{0:T(1024)S(1)}, f32[4864]{0:T(1024)S(1)}, u32[]{:S(2)}, u32[]{:S(2)}) collective-permute-start(f32[4864]{0:T(1024)S(1)} %reshape.652), channel_id=1, source_target_pairs={{1,0},{2,1},{3,2},{4,3},{5,4},{6,5},{7,6},{8,7},{9,8},{10,9},{11,1... | collective-permute-start | bytes 58376 | tf_op jit(solution)/shard_map/ppermute | solution.py:27
  67.0 0.1 reshape.653
  67.1 7.6 %collective-permute-done.7 = f32[4864]{0:T(1024)S(1)} collective-permute-done((f32[4864]{0:T(1024)S(1)}, f32[4864]{0:T(1024)S(1)}, u32[]{:S(2)}, u32[]{:S(2)}) %collective-permute-start.7) | collective-permute-done | bytes 19488 | tf_op jit(solution)/shard_map/ppermute | solution.py:27
  74.8 0.1 reshape.654
  75.0 0.6 copy.27
  (43 shorter events, 1.2 us)
Async XLA Ops:
  2.7 1.0 %copy-start = (bf16[8,2,1,2,2,2850]{5,4,3,2,1,0:T(2,128)(2,1)S(1)}, bf16[8,2,1,2,2,2850]{5,4,3,2,1,0:T(2,128)(2,1)}, u32[]{:S(2)}) copy-start(bf16[8,2,1,2,2,2850]{5,4,3,2,1,0:T(2,128)(2,1)} %param.7) | copy-start | bytes 1094404
  4.1 16.2 %copy-start.1 = (f32[2,1,2,2,2850]{4,3,2,1,0:T(2,128)S(1)}, f32[2,1,2,2,2850]{4,3,2,1,0:T(2,128)}, u32[]{:S(2)}) copy-start(f32[2,1,2,2,2850]{4,3,2,1,0:T(2,128)} %param.6) | copy-start | bytes 273604
  4.5 3.2 %collective-permute-start = (f32[2,1,2,2,2850]{4,3,2,1,0:T(2,128)S(1)}, f32[2,1,2,2,2850]{4,3,2,1,0:T(2,128)S(1)}, u32[]{:S(2)}, u32[]{:S(2)}) collective-permute-start(f32[2,1,2,2,2850]{4,3,2,1,0:T(2,128)S(1)} %bitcast.94), channel_id=1, source_target_pairs={{0,128},{128,0},{256,384},{384,256},{1,129},{129,1},{257,385},{385... | collective-permute-start | bytes 273608 | tf_op jit(solution)/shard_map/ppermute | solution.py:48
  7.7 12.6 %collective-permute-start.1 = (f32[2,1,2,2,2850]{4,3,2,1,0:T(2,128)S(1)}, f32[2,1,2,2,2850]{4,3,2,1,0:T(2,128)S(1)}, u32[]{:S(2)}, u32[]{:S(2)}) collective-permute-start(f32[2,1,2,2,2850]{4,3,2,1,0:T(2,128)S(1)} %bitcast_add_fusion.1), channel_id=1, source_target_pairs={{0,256},{128,384},{256,0},{384,128},{1,257},{129,385},{257,1},{385... | collective-permute-start | bytes 273608 | tf_op jit(solution)/shard_map/ppermute | solution.py:48
  22.0 0.8 %copy-start.3 = (f32[8,2,2,2,76]{4,3,2,1,0:T(2,128)S(1)}, f32[8,2,2,2,76]{4,3,2,1,0:T(2,128)}, u32[]{:S(2)}) copy-start(f32[8,2,2,2,76]{4,3,2,1,0:T(2,128)} %param.8) | copy-start | bytes 58372
  22.0 0.9 %copy-start.4 = (f32[2]{0:T(128)S(1)}, f32[2]{0:T(128)}, u32[]{:S(2)}) copy-start(f32[2]{0:T(128)} %param.9) | copy-start | bytes 28
  22.0 20.6 %copy-start.5 = (s32[2]{0:T(128)S(1)}, s32[2]{0:T(128)}, u32[]{:S(2)}) copy-start(s32[2]{0:T(128)} %param.10) | copy-start | bytes 28
  22.9 9.7 %collective-permute-start.2 = (f32[4866]{0:T(1024)S(1)}, f32[4866]{0:T(1024)S(1)}, u32[]{:S(2)}, u32[]{:S(2)}) collective-permute-start(f32[4866]{0:T(1024)S(1)} %constant_dynamic-update-slice_fusion), channel_id=1, source_target_pairs={{0,1},{1,2},{2,3},{3,4},{4,5},{5,6},{6,7},{7,8},{8,9},{9,10},{10,1... | collective-permute-start | bytes 58400 | tf_op jit(solution)/shard_map/ppermute | solution.py:27
  30.7 11.7 %collective-permute-start.3 = (f32[4866]{0:T(1024)S(1)}, f32[4866]{0:T(1024)S(1)}, u32[]{:S(2)}, u32[]{:S(2)}) collective-permute-start(f32[4866]{0:T(1024)S(1)} %constant_dynamic-update-slice_fusion), channel_id=1, source_target_pairs={{1,0},{2,1},{3,2},{4,3},{5,4},{6,5},{7,6},{8,7},{9,8},{10,9},{11,1... | collective-permute-start | bytes 58400 | tf_op jit(solution)/shard_map/ppermute | solution.py:27
  44.4 3.2 %collective-permute-start.4 = (f32[2,1,2,2,2850]{4,3,2,1,0:T(2,128)S(1)}, f32[2,1,2,2,2850]{4,3,2,1,0:T(2,128)S(1)}, u32[]{:S(2)}, u32[]{:S(2)}) collective-permute-start(f32[2,1,2,2,2850]{4,3,2,1,0:T(2,128)S(1)} %bitcast.95), channel_id=1, source_target_pairs={{0,128},{128,0},{256,384},{384,256},{1,129},{129,1},{257,385},{385... | collective-permute-start | bytes 273608 | tf_op jit(solution)/shard_map/ppermute | solution.py:48
  47.7 10.6 %collective-permute-start.5 = (f32[2,1,2,2,2850]{4,3,2,1,0:T(2,128)S(1)}, f32[2,1,2,2,2850]{4,3,2,1,0:T(2,128)S(1)}, u32[]{:S(2)}, u32[]{:S(2)}) collective-permute-start(f32[2,1,2,2,2850]{4,3,2,1,0:T(2,128)S(1)} %bitcast_add_fusion), channel_id=1, source_target_pairs={{0,256},{128,384},{256,0},{384,128},{1,257},{129,385},{257,1},{385... | collective-permute-start | bytes 273608 | tf_op jit(solution)/shard_map/ppermute | solution.py:48
  58.3 0.6 copy-start.2
  61.1 5.9 %collective-permute-start.6 = (f32[4864]{0:T(1024)S(1)}, f32[4864]{0:T(1024)S(1)}, u32[]{:S(2)}, u32[]{:S(2)}) collective-permute-start(f32[4864]{0:T(1024)S(1)} %reshape.652), channel_id=1, source_target_pairs={{0,1},{1,2},{2,3},{3,4},{4,5},{5,6},{6,7},{7,8},{8,9},{9,10},{10,1... | collective-permute-start | bytes 58376 | tf_op jit(solution)/shard_map/ppermute | solution.py:27
  63.1 11.7 %collective-permute-start.7 = (f32[4864]{0:T(1024)S(1)}, f32[4864]{0:T(1024)S(1)}, u32[]{:S(2)}, u32[]{:S(2)}) collective-permute-start(f32[4864]{0:T(1024)S(1)} %reshape.652), channel_id=1, source_target_pairs={{1,0},{2,1},{3,2},{4,3},{5,4},{6,5},{7,6},{8,7},{9,8},{10,9},{11,1... | collective-permute-start | bytes 58376 | tf_op jit(solution)/shard_map/ppermute | solution.py:27

commit v7 on v3

--- a/solution.py
+++ b/solution.py
@@ -59,8 +59,10 @@
 
 def corrupt(gains, model, left_hot, right_hot):
     model = model.astype(jnp.float32)
-    left_gain = jnp.matmul(gains, left_hot, precision=highest)[:, None]
-    right_gain = jnp.matmul(gains, right_hot, precision=highest)[:, None]
+    count = left_hot.shape[1]
+    both = jnp.matmul(gains, jnp.concatenate([left_hot, right_hot], axis=1), precision=highest)
+    left_gain = both[..., :count][:, None]
+    right_gain = both[..., count:][:, None]
     left_re, left_im = (left_gain[..., 0, :], left_gain[..., 1, :])
     right_re, right_im = (right_gain[..., 0, :], right_gain[..., 1, :])
     model_re, model_im = (model[..., 0, :], model[..., 1, :])
@@ -88,8 +90,10 @@
     right_den = power * (left_re * left_re + left_im * left_im)
     left_products = jnp.sum(jnp.stack([left_num_re, left_num_im, left_den], axis=3), axis=1)
     right_terms = jnp.sum(jnp.stack([right_num_re, right_num_im, right_den], axis=3), axis=1)
-    totals = jnp.matmul(left_products, left_hot.T, precision=highest) + jnp.matmul(
-        right_terms, right_hot.T, precision=highest
+    totals = jnp.matmul(
+        jnp.concatenate([left_products, right_terms], axis=-1),
+        jnp.concatenate([left_hot.T, right_hot.T], axis=0),
+        precision=highest,
     )
     solved = totals[:, :, 0:2] / (totals[:, :, 2:3] + epsilon)
     return (1.0 - step_size) * gains + step_size * solved

time: 75.7 us -> 79.3 us (1.048)
  other arithmetic: 2.57 us -> 5.76 us
  local copies, waits for them, and re-layouts: 3.28 us -> 4.87 us
    eq x0 -> x2, other arithmetic: none -> 1.27 us  [station_tables(): right_hot = (baseline_table[1][None, :] == column).astype(jnp.float32)]
    unnamed x14 -> x18, local copies, waits for them, and re-layouts: 1.65 us -> 2.72 us
    add x3, other arithmetic: 0.24 us -> 1.21 us  [solve(): target = residual + corrupted_model]
    dot_general x8 -> x4, matrix products: 6.06 us -> 5.52 us  [the longest x2 2.92 us: solve(): jnp.matmul(jnp.concatenate([left_products, right_terms], axis=-1), jnp.co...]
  transfers between devices with their start and end apart: 8 -> 8, of which waited for: 6 -> 6; matrix products, arithmetic and copies ran while one was open for 0% -> 2% of each run, Pallas kernels for 0% -> 0%
where the time goes in v7:
time: 79.3 us; the launch traced here: 78.8 us
  waiting for transfers between devices  35.6 us (45%)
  starting transfers between devices  26 us (33%)
  other arithmetic  5.76 us (7%)
  matrix products  5.52 us (7%)
  local copies, waits for them, and re-layouts  4.87 us (6%)
  between operations  1.07 us (1%)
    ppermute x4, waiting for transfers between devices, sum_over_dir(): lax.ppermute(total, 'dir', [(i, i ^ mask) for i in range(count)])  18.3 us
    ppermute x4, waiting for transfers between devices, send(): arrived = lax.ppermute(flat, axis, pairs)  17.2 us
    ppermute x4, starting transfers between devices, send(): arrived = lax.ppermute(flat, axis, pairs)  15.5 us
    ppermute x4, starting transfers between devices, sum_over_dir(): lax.ppermute(total, 'dir', [(i, i ^ mask) for i in range(count)])  10.5 us
    dot_general x2, matrix products, solve(): jnp.matmul(jnp.concatenate([left_products, right_terms], axis=-1), jnp.co...  2.92 us
    unnamed x18, local copies, waits for them, and re-layouts  2.72 us
    dot_general x2, matrix products, corrupt(): jnp.matmul(gains, jnp.concatenate([left_hot, right_hot], axis=1), precisi...  2.61 us
  transfers between devices with their start and end apart: 8, of which 6 were waited for; matrix products, arithmetic and copies ran while one was open for 2% of the time, Pallas kernels for 0%

profile of v7, /device:TPU:254, one launch (start us, length us, event | category | flops | bytes accessed | tf_op | source)
XLA Modules:
  0.0 78.8 jit_solution(4610499584462280973)
XLA Ops:
  0.6 0.9 %slice_reduce_fusion.1 = (s32[2850]{0:T(1024)S(1)}, s32[2850]{0:T(1024)S(1)}) fusion(s32[2,2850]{1,0:T(2,128)} %param.11), kind=kLoop, calls=%fused_computation.88 | loop fusion | bytes 45600 | tf_op jit(solution)/shard_map/slice | solution.py:55
  1.5 0.2 iota_compare_fusion.2
  1.8 1.7 %convolution_bitcast_fusion = f32[8,2,2,2,5700]{4,0,3,2,1:T(8,128)S(1)} fusion(pred[76,2850]{1,0:T(8,128)(4,1)S(1)} %get-tuple-element.49, pred[76,2850]{1,0:T(8,128)(4,1)S(1)} %get-tuple-element.50, f32[8,2,2,2,76]{4,3,2,1,0:T(2,128)} %param.8), kind=kOutput, calls=%fused_computation | convolution fusion | flops 333130816 | bytes 1911856 | tf_op jit(solution)/shard_map/vmap()/dot_general | solution.py:63
  3.5 0.3 slice_bitcast_fusion.3
  3.7 0.7 copy-done
  4.5 0.1 multiply_add_fusion.9
  4.6 0.1 multiply_subtract_fusion.8
  4.7 0.2 fusion.11
  5.0 1.9 %collective-permute-start = (f32[2,1,2,2,2850]{4,3,2,1,0:T(2,128)S(1)}, f32[2,1,2,2,2850]{4,3,2,1,0:T(2,128)S(1)}, u32[]{:S(2)}, u32[]{:S(2)}) collective-permute-start(f32[2,1,2,2,2850]{4,3,2,1,0:T(2,128)S(1)} %bitcast.45), channel_id=1, source_target_pairs={{0,128},{128,0},{256,384},{384,256},{1,129},{129,1},{257,385},{385... | collective-permute-start | bytes 273608 | tf_op jit(solution)/shard_map/ppermute | solution.py:48
  6.9 1.3 %collective-permute-done = f32[2,1,2,2,2850]{4,3,2,1,0:T(2,128)S(1)} collective-permute-done((f32[2,1,2,2,2850]{4,3,2,1,0:T(2,128)S(1)}, f32[2,1,2,2,2850]{4,3,2,1,0:T(2,128)S(1)}, u32[]{:S(2)}, u32[]{:S(2)}) %collective-permute-start) | collective-permute-done | bytes 91232 | tf_op jit(solution)/shard_map/ppermute | solution.py:48
  8.2 0.7 bitcast_add_fusion.1
  8.8 4.7 %collective-permute-start.1 = (f32[2,1,2,2,2850]{4,3,2,1,0:T(2,128)}, f32[2,1,2,2,2850]{4,3,2,1,0:T(2,128)}, u32[]{:S(2)}, u32[]{:S(2)}) collective-permute-start(f32[2,1,2,2,2850]{4,3,2,1,0:T(2,128)} %bitcast_add_fusion.1), channel_id=1, source_target_pairs={{0,256},{128,384},{256,0},{384,128},{1,257},{129,385},{257,1},{385... | collective-permute-start | bytes 273608 | tf_op jit(solution)/shard_map/ppermute | solution.py:48
  13.6 1.0 %iota_compare_fusion = (pred[2850,76]{0,1:T(8,128)(4,1)}, pred[2850,76]{0,1:T(8,128)(4,1)}) fusion(s32[2850]{0:T(1024)S(1)} %get-tuple-element.7, s32[2850]{0:T(1024)S(1)} %get-tuple-element.6), kind=kLoop, calls=%fused_computation.15 | loop fusion | flops 433200 | bytes 456000 | tf_op jit(solution)/shard_map/eq | solution.py:56
  14.6 7.2 %collective-permute-done.1 = f32[2,1,2,2,2850]{4,3,2,1,0:T(2,128)} collective-permute-done((f32[2,1,2,2,2850]{4,3,2,1,0:T(2,128)}, f32[2,1,2,2,2850]{4,3,2,1,0:T(2,128)}, u32[]{:S(2)}, u32[]{:S(2)}) %collective-permute-start.1) | collective-permute-done | bytes 91232 | tf_op jit(solution)/shard_map/ppermute | solution.py:48
  21.7 1.0 %subtract_bitcast_fusion = f32[2,2,2,2850]{3,2,1,0:T(2,128)S(1)} fusion(f32[2,1,2,2,2850]{4,3,2,1,0:T(2,128)} %param.6, f32[2,1,2,2,2850]{4,3,2,1,0:T(2,128)} %bitcast_add_fusion.1, f32[2,1,2,2,2850]{4,3,2,1,0:T(2,128)} %collective-permute-done.1), kind=kLoop, calls=%fused_computation.57 | loop fusion | flops 45600 | bytes 364800 | tf_op jit(solution)/shard_map/vmap()/add | solution.py:79
  22.9 0.2 multiply_subtract_fusion.6
  23.1 0.2 multiply_add_fusion.5
  23.5 0.8 %copy-done.3 = pred[2850,76]{0,1:T(8,128)(4,1)S(1)} copy-done((pred[2850,76]{0,1:T(8,128)(4,1)S(1)}, pred[2850,76]{0,1:T(8,128)(4,1)}, u32[]{:S(2)}) %copy-start.3) | copy-done | bytes 216624
  24.3 0.1 copy-done.4
  24.5 1.5 %fusion = f32[8,2,2,3,76]{4,0,3,2,1:T(8,128)S(1)} fusion(f32[8,2,2,3,2850]{4,0,3,2,1:T(8,128)S(1)} %maximum_bitcast_fusion.1, f32[8,2,2,3,2850]{4,0,3,2,1:T(8,128)S(1)} %maximum_bitcast_fusion, pred[2850,76]{0,1:T(8,128)(4,1)S(1)} %copy-done.3, pred[2850,76]{0,1:T(8,128)(4,1)S(1)} %copy-done.4), kind=kOutput, calls=%fused_computation.1 | convolution fusion | flops 500026816 | bytes 2651184 | tf_op jit(solution)/shard_map/vmap()/dot_general | solution.py:93
  26.0 0.1 reshape.379
  26.1 7.7 %collective-permute-start.2 = (f32[4866]{0:T(1024)S(1)}, f32[4866]{0:T(1024)S(1)}, u32[]{:S(2)}, u32[]{:S(2)}) collective-permute-start(f32[4866]{0:T(1024)S(1)} %constant_dynamic-update-slice_fusion), channel_id=1, source_target_pairs={{0,1},{1,2},{2,3},{3,4},{4,5},{5,6},{6,7},{7,8},{8,9},{9,10},{10,1... | collective-permute-start | bytes 58400 | tf_op jit(solution)/shard_map/ppermute | solution.py:27
  33.9 1.9 %collective-permute-start.3 = (f32[4866]{0:T(1024)S(1)}, f32[4866]{0:T(1024)S(1)}, u32[]{:S(2)}, u32[]{:S(2)}) collective-permute-start(f32[4866]{0:T(1024)S(1)} %constant_dynamic-update-slice_fusion), channel_id=1, source_target_pairs={{1,0},{2,1},{3,2},{4,3},{5,4},{6,5},{7,6},{8,7},{9,8},{10,9},{11,1... | collective-permute-start | bytes 58400 | tf_op jit(solution)/shard_map/ppermute | solution.py:27
  35.8 0.1 reshape.380
  36.0 9.6 %collective-permute-done.3 = f32[4866]{0:T(1024)S(1)} collective-permute-done((f32[4866]{0:T(1024)S(1)}, f32[4866]{0:T(1024)S(1)}, u32[]{:S(2)}, u32[]{:S(2)}) %collective-permute-start.3) | collective-permute-done | bytes 19496 | tf_op jit(solution)/shard_map/ppermute | solution.py:27
  45.6 0.1 reshape.381
  45.9 0.1 fusion.25
  46.0 0.9 %fusion.12 = f32[8,2,2,2,5700]{4,0,3,2,1:T(8,128)S(1)} fusion(f32[8,2,2,2,76]{4,0,3,2,1:T(8,128)S(1)} %fusion.25, pred[76,2850]{1,0:T(8,128)(4,1)S(1)} %get-tuple-element.49, pred[76,2850]{1,0:T(8,128)(4,1)S(1)} %get-tuple-element.50), kind=kOutput, calls=%fused_computation.29 | convolution fusion | flops 333130816 | bytes 1911856 | tf_op jit(solution)/shard_map/vmap()/dot_general | solution.py:63
  46.9 0.3 slice_bitcast_fusion
  47.2 0.2 multiply_add_fusion.3
  47.4 0.2 fusion.9
  47.7 1.9 %collective-permute-start.4 = (f32[2,1,2,2,2850]{4,3,2,1,0:T(2,128)S(1)}, f32[2,1,2,2,2850]{4,3,2,1,0:T(2,128)S(1)}, u32[]{:S(2)}, u32[]{:S(2)}) collective-permute-start(f32[2,1,2,2,2850]{4,3,2,1,0:T(2,128)S(1)} %bitcast.46), channel_id=1, source_target_pairs={{0,128},{128,0},{256,384},{384,256},{1,129},{129,1},{257,385},{385... | collective-permute-start | bytes 273608 | tf_op jit(solution)/shard_map/ppermute | solution.py:48
  49.6 1.3 %collective-permute-done.4 = f32[2,1,2,2,2850]{4,3,2,1,0:T(2,128)S(1)} collective-permute-done((f32[2,1,2,2,2850]{4,3,2,1,0:T(2,128)S(1)}, f32[2,1,2,2,2850]{4,3,2,1,0:T(2,128)S(1)}, u32[]{:S(2)}, u32[]{:S(2)}) %collective-permute-start.4) | collective-permute-done | bytes 91232 | tf_op jit(solution)/shard_map/ppermute | solution.py:48
  50.9 1.9 %collective-permute-start.5 = (f32[2,1,2,2,2850]{4,3,2,1,0:T(2,128)S(1)}, f32[2,1,2,2,2850]{4,3,2,1,0:T(2,128)S(1)}, u32[]{:S(2)}, u32[]{:S(2)}) collective-permute-start(f32[2,1,2,2,2850]{4,3,2,1,0:T(2,128)S(1)} %bitcast_add_fusion), channel_id=1, source_target_pairs={{0,256},{128,384},{256,0},{384,128},{1,257},{129,385},{257,1},{385... | collective-permute-start | bytes 273608 | tf_op jit(solution)/shard_map/ppermute | solution.py:48
  52.8 8.6 %collective-permute-done.5 = f32[2,1,2,2,2850]{4,3,2,1,0:T(2,128)S(1)} collective-permute-done((f32[2,1,2,2,2850]{4,3,2,1,0:T(2,128)S(1)}, f32[2,1,2,2,2850]{4,3,2,1,0:T(2,128)S(1)}, u32[]{:S(2)}, u32[]{:S(2)}) %collective-permute-start.5) | collective-permute-done | bytes 91232 | tf_op jit(solution)/shard_map/ppermute | solution.py:48
  61.7 0.2 multiply_subtract_fusion.1
  61.8 0.4 copy-done.2
  62.2 0.2 multiply_add_fusion.1
  62.5 0.1 maximum_bitcast_fusion.2
  62.6 1.5 %fusion.4 = f32[8,2,2,3,76]{4,0,3,2,1:T(8,128)S(1)} fusion(f32[8,2,2,3,2850]{4,0,3,2,1:T(8,128)S(1)} %maximum_bitcast_fusion.3, f32[8,2,2,3,2850]{4,0,3,2,1:T(8,128)S(1)} %maximum_bitcast_fusion.2, pred[2850,76]{0,1:T(8,128)(4,1)S(1)} %copy-done.3, pred[2850,76]{0,1:T(8,128)(4,1)S(1)} %copy-done.4), kind=kOutput, calls=%fused_computation.5 | convolution fusion | flops 500026816 | bytes 2651184 | tf_op jit(solution)/shard_map/vmap()/dot_general | solution.py:93
  64.2 0.1 reshape.382
  64.3 1.9 %collective-permute-start.6 = (f32[4864]{0:T(1024)S(1)}, f32[4864]{0:T(1024)S(1)}, u32[]{:S(2)}, u32[]{:S(2)}) collective-permute-start(f32[4864]{0:T(1024)S(1)} %reshape.382), channel_id=1, source_target_pairs={{0,1},{1,2},{2,3},{3,4},{4,5},{5,6},{6,7},{7,8},{8,9},{9,10},{10,1... | collective-permute-start | bytes 58376 | tf_op jit(solution)/shard_map/ppermute | solution.py:27
  66.2 3.9 %collective-permute-start.7 = (f32[4864]{0:T(1024)S(1)}, f32[4864]{0:T(1024)S(1)}, u32[]{:S(2)}, u32[]{:S(2)}) collective-permute-start(f32[4864]{0:T(1024)S(1)} %reshape.382), channel_id=1, source_target_pairs={{1,0},{2,1},{3,2},{4,3},{5,4},{6,5},{7,6},{8,7},{9,8},{10,9},{11,1... | collective-permute-start | bytes 58376 | tf_op jit(solution)/shard_map/ppermute | solution.py:27
  70.1 0.1 reshape.383
  70.3 7.6 %collective-permute-done.7 = f32[4864]{0:T(1024)S(1)} collective-permute-done((f32[4864]{0:T(1024)S(1)}, f32[4864]{0:T(1024)S(1)}, u32[]{:S(2)}, u32[]{:S(2)}) %collective-permute-start.7) | collective-permute-done | bytes 19488 | tf_op jit(solution)/shard_map/ppermute | solution.py:27
  77.9 0.1 reshape.384
  78.0 0.1 fusion.16
  78.1 0.6 copy.25
  (40 shorter events, 0.9 us)
Async XLA Ops:
  3.5 1.0 %copy-start = (bf16[8,2,1,2,2,2850]{5,4,3,2,1,0:T(2,128)(2,1)S(1)}, bf16[8,2,1,2,2,2850]{5,4,3,2,1,0:T(2,128)(2,1)}, u32[]{:S(2)}) copy-start(bf16[8,2,1,2,2,2850]{5,4,3,2,1,0:T(2,128)(2,1)} %param.7) | copy-start | bytes 1094404
  5.0 3.2 %collective-permute-start = (f32[2,1,2,2,2850]{4,3,2,1,0:T(2,128)S(1)}, f32[2,1,2,2,2850]{4,3,2,1,0:T(2,128)S(1)}, u32[]{:S(2)}, u32[]{:S(2)}) collective-permute-start(f32[2,1,2,2,2850]{4,3,2,1,0:T(2,128)S(1)} %bitcast.45), channel_id=1, source_target_pairs={{0,128},{128,0},{256,384},{384,256},{1,129},{129,1},{257,385},{385... | collective-permute-start | bytes 273608 | tf_op jit(solution)/shard_map/ppermute | solution.py:48
  8.8 12.9 %collective-permute-start.1 = (f32[2,1,2,2,2850]{4,3,2,1,0:T(2,128)}, f32[2,1,2,2,2850]{4,3,2,1,0:T(2,128)}, u32[]{:S(2)}, u32[]{:S(2)}) collective-permute-start(f32[2,1,2,2,2850]{4,3,2,1,0:T(2,128)} %bitcast_add_fusion.1), channel_id=1, source_target_pairs={{0,256},{128,384},{256,0},{384,128},{1,257},{129,385},{257,1},{385... | collective-permute-start | bytes 273608 | tf_op jit(solution)/shard_map/ppermute | solution.py:48
  23.4 0.9 %copy-start.3 = (pred[2850,76]{0,1:T(8,128)(4,1)S(1)}, pred[2850,76]{0,1:T(8,128)(4,1)}, u32[]{:S(2)}) copy-start(pred[2850,76]{0,1:T(8,128)(4,1)} %get-tuple-element.47) | copy-start | bytes 649804
  23.4 1.0 %copy-start.4 = (pred[2850,76]{0,1:T(8,128)(4,1)S(1)}, pred[2850,76]{0,1:T(8,128)(4,1)}, u32[]{:S(2)}) copy-start(pred[2850,76]{0,1:T(8,128)(4,1)} %get-tuple-element.48) | copy-start | bytes 649804
  24.4 1.5 %copy-start.5 = (f32[8,2,2,2,76]{4,3,2,1,0:T(2,128)S(1)}, f32[8,2,2,2,76]{4,3,2,1,0:T(2,128)}, u32[]{:S(2)}) copy-start(f32[8,2,2,2,76]{4,3,2,1,0:T(2,128)} %param.8) | copy-start | bytes 58372
  24.5 1.7 %copy-start.6 = (f32[2]{0:T(128)S(1)}, f32[2]{0:T(128)}, u32[]{:S(2)}) copy-start(f32[2]{0:T(128)} %param.9) | copy-start | bytes 28
  24.5 21.4 %copy-start.7 = (s32[2]{0:T(128)S(1)}, s32[2]{0:T(128)}, u32[]{:S(2)}) copy-start(s32[2]{0:T(128)} %param.10) | copy-start | bytes 28
  26.1 9.7 %collective-permute-start.2 = (f32[4866]{0:T(1024)S(1)}, f32[4866]{0:T(1024)S(1)}, u32[]{:S(2)}, u32[]{:S(2)}) collective-permute-start(f32[4866]{0:T(1024)S(1)} %constant_dynamic-update-slice_fusion), channel_id=1, source_target_pairs={{0,1},{1,2},{2,3},{3,4},{4,5},{5,6},{6,7},{7,8},{8,9},{9,10},{10,1... | collective-permute-start | bytes 58400 | tf_op jit(solution)/shard_map/ppermute | solution.py:27
  33.9 11.7 %collective-permute-start.3 = (f32[4866]{0:T(1024)S(1)}, f32[4866]{0:T(1024)S(1)}, u32[]{:S(2)}, u32[]{:S(2)}) collective-permute-start(f32[4866]{0:T(1024)S(1)} %constant_dynamic-update-slice_fusion), channel_id=1, source_target_pairs={{1,0},{2,1},{3,2},{4,3},{5,4},{6,5},{7,6},{8,7},{9,8},{10,9},{11,1... | collective-permute-start | bytes 58400 | tf_op jit(solution)/shard_map/ppermute | solution.py:27
  47.4 14.1 %copy-start.1 = (f32[2,1,2,2,2850]{4,3,2,1,0:T(2,128)S(1)}, f32[2,1,2,2,2850]{4,3,2,1,0:T(2,128)}, u32[]{:S(2)}) copy-start(f32[2,1,2,2,2850]{4,3,2,1,0:T(2,128)} %param.6) | copy-start | bytes 273604
  47.7 3.2 %collective-permute-start.4 = (f32[2,1,2,2,2850]{4,3,2,1,0:T(2,128)S(1)}, f32[2,1,2,2,2850]{4,3,2,1,0:T(2,128)S(1)}, u32[]{:S(2)}, u32[]{:S(2)}) collective-permute-start(f32[2,1,2,2,2850]{4,3,2,1,0:T(2,128)S(1)} %bitcast.46), channel_id=1, source_target_pairs={{0,128},{128,0},{256,384},{384,256},{1,129},{129,1},{257,385},{385... | collective-permute-start | bytes 273608 | tf_op jit(solution)/shard_map/ppermute | solution.py:48
  50.9 10.6 %collective-permute-start.5 = (f32[2,1,2,2,2850]{4,3,2,1,0:T(2,128)S(1)}, f32[2,1,2,2,2850]{4,3,2,1,0:T(2,128)S(1)}, u32[]{:S(2)}, u32[]{:S(2)}) collective-permute-start(f32[2,1,2,2,2850]{4,3,2,1,0:T(2,128)S(1)} %bitcast_add_fusion), channel_id=1, source_target_pairs={{0,256},{128,384},{256,0},{384,128},{1,257},{129,385},{257,1},{385... | collective-permute-start | bytes 273608 | tf_op jit(solution)/shard_map/ppermute | solution.py:48
  61.6 0.6 copy-start.2
  64.3 5.9 %collective-permute-start.6 = (f32[4864]{0:T(1024)S(1)}, f32[4864]{0:T(1024)S(1)}, u32[]{:S(2)}, u32[]{:S(2)}) collective-permute-start(f32[4864]{0:T(1024)S(1)} %reshape.382), channel_id=1, source_target_pairs={{0,1},{1,2},{2,3},{3,4},{4,5},{5,6},{6,7},{7,8},{8,9},{9,10},{10,1... | collective-permute-start | bytes 58376 | tf_op jit(solution)/shard_map/ppermute | solution.py:27
  66.2 11.7 %collective-permute-start.7 = (f32[4864]{0:T(1024)S(1)}, f32[4864]{0:T(1024)S(1)}, u32[]{:S(2)}, u32[]{:S(2)}) collective-permute-start(f32[4864]{0:T(1024)S(1)} %reshape.382), channel_id=1, source_target_pairs={{1,0},{2,1},{3,2},{4,3},{5,4},{6,5},{7,6},{8,7},{9,8},{10,9},{11,1... | collective-permute-start | bytes 58376 | tf_op jit(solution)/shard_map/ppermute | solution.py:27

commit v8 on v3

--- a/solution.py
+++ b/solution.py
@@ -52,9 +52,8 @@
 
 def station_tables(baseline_table):
     column = jnp.arange(STATIONS, dtype=jnp.int32)[:, None]
-    left_hot = (baseline_table[0][None, :] == column).astype(jnp.float32)
-    right_hot = (baseline_table[1][None, :] == column).astype(jnp.float32)
-    return (left_hot, right_hot)
+    hot = (baseline_table[:, None, :] == column[None]).astype(jnp.float32)
+    return (hot[0], hot[1])
 
 
 def corrupt(gains, model, left_hot, right_hot):

time: 75.7 us -> 77.4 us (1.022)
  other arithmetic: 2.57 us -> 5.23 us
  local copies, waits for them, and re-layouts: 3.28 us -> 2.46 us
    eq x0 -> x1, other arithmetic: none -> 1 us  [station_tables(): hot = (baseline_table[:, None, :] == column[None]).astype(jnp.float32)]
    add x3, other arithmetic: 0.24 us -> 1.23 us  [solve(): target = residual + corrupted_model]
    slice x1 -> x0, local copies, waits for them, and re-layouts: 0.87 us -> none  [station_tables(): left_hot = (baseline_table[0][None, :] == column).astype(jnp.float32)]
where the time goes in v8:
time: 77.4 us; the launch traced here: 76.9 us
  waiting for transfers between devices  36.6 us (47%)
  starting transfers between devices  26 us (34%)
  matrix products  5.6 us (7%)
  other arithmetic  5.23 us (7%)
  local copies, waits for them, and re-layouts  2.46 us (3%)
  between operations  1.05 us (1%)
    ppermute x4, waiting for transfers between devices, sum_over_dir(): lax.ppermute(total, 'dir', [(i, i ^ mask) for i in range(count)])  19.3 us
    ppermute x4, waiting for transfers between devices, send(): arrived = lax.ppermute(flat, axis, pairs)  17.2 us
    ppermute x4, starting transfers between devices, send(): arrived = lax.ppermute(flat, axis, pairs)  15.5 us
    ppermute x4, starting transfers between devices, sum_over_dir(): lax.ppermute(total, 'dir', [(i, i ^ mask) for i in range(count)])  10.5 us
    dot_general x2, matrix products, corrupt(): right_gain = jnp.matmul(gains, right_hot, precision=highest)[:, None]  1.76 us
    unnamed x14, local copies, waits for them, and re-layouts  1.69 us
  transfers between devices with their start and end apart: 8, of which 6 were waited for; matrix products, arithmetic and copies ran while one was open for 0% of the time, Pallas kernels for 0%

profile of v8, /device:TPU:254, one launch (start us, length us, event | category | flops | bytes accessed | tf_op | source)
XLA Modules:
  0.0 76.9 jit_solution(4186012352857076535)
XLA Ops:
  0.6 1.0 %iota_compare_fusion = pred[2,76,2850]{2,1,0:T(8,128)(4,1)S(1)} fusion(s32[2,2850]{1,0:T(2,128)} %param.11), kind=kLoop, calls=%fused_computation.4 | loop fusion | flops 433200 | bytes 456000 | tf_op jit(solution)/shard_map/eq | solution.py:55
  1.6 1.3 %convolution_bitcast_fusion.2 = f32[8,2,1,2,2,2850]{5,0,4,3,1,2:T(8,128)S(1)} fusion(f32[8,2,2,2,76]{4,3,2,1,0:T(2,128)} %param.8, pred[2,76,2850]{2,1,0:T(8,128)(4,1)S(1)} %iota_compare_fusion), kind=kOutput, calls=%fused_computation.2 | convolution fusion | flops 166348800 | bytes 984576 | tf_op jit(solution)/shard_map/vmap()/dot_general | solution.py:62
  3.0 0.5 convolution_bitcast_fusion.3
  3.5 0.5 copy-done
  4.0 0.1 multiply_add_fusion.9
  4.1 0.1 multiply_subtract_fusion.8
  4.2 0.2 fusion.25
  4.5 1.9 %collective-permute-start = (f32[2,1,2,2,2850]{4,3,2,1,0:T(2,128)S(1)}, f32[2,1,2,2,2850]{4,3,2,1,0:T(2,128)S(1)}, u32[]{:S(2)}, u32[]{:S(2)}) collective-permute-start(f32[2,1,2,2,2850]{4,3,2,1,0:T(2,128)S(1)} %bitcast.64), channel_id=1, source_target_pairs={{0,128},{128,0},{256,384},{384,256},{1,129},{129,1},{257,385},{385... | collective-permute-start | bytes 273608 | tf_op jit(solution)/shard_map/ppermute | solution.py:48
  6.4 1.3 %collective-permute-done = f32[2,1,2,2,2850]{4,3,2,1,0:T(2,128)S(1)} collective-permute-done((f32[2,1,2,2,2850]{4,3,2,1,0:T(2,128)S(1)}, f32[2,1,2,2,2850]{4,3,2,1,0:T(2,128)S(1)}, u32[]{:S(2)}, u32[]{:S(2)}) %collective-permute-start) | collective-permute-done | bytes 91232 | tf_op jit(solution)/shard_map/ppermute | solution.py:48
  7.7 0.7 bitcast_add_fusion.1
  8.4 4.7 %collective-permute-start.1 = (f32[2,1,2,2,2850]{4,3,2,1,0:T(2,128)}, f32[2,1,2,2,2850]{4,3,2,1,0:T(2,128)}, u32[]{:S(2)}, u32[]{:S(2)}) collective-permute-start(f32[2,1,2,2,2850]{4,3,2,1,0:T(2,128)} %bitcast_add_fusion.1), channel_id=1, source_target_pairs={{0,256},{128,384},{256,0},{384,128},{1,257},{129,385},{257,1},{385... | collective-permute-start | bytes 273608 | tf_op jit(solution)/shard_map/ppermute | solution.py:48
  13.1 8.2 %collective-permute-done.1 = f32[2,1,2,2,2850]{4,3,2,1,0:T(2,128)} collective-permute-done((f32[2,1,2,2,2850]{4,3,2,1,0:T(2,128)}, f32[2,1,2,2,2850]{4,3,2,1,0:T(2,128)}, u32[]{:S(2)}, u32[]{:S(2)}) %collective-permute-start.1) | collective-permute-done | bytes 91232 | tf_op jit(solution)/shard_map/ppermute | solution.py:48
  21.2 1.0 %subtract_bitcast_fusion = f32[2,2,2,2850]{3,2,1,0:T(2,128)S(1)} fusion(f32[2,1,2,2,2850]{4,3,2,1,0:T(2,128)} %param.6, f32[2,1,2,2,2850]{4,3,2,1,0:T(2,128)} %bitcast_add_fusion.1, f32[2,1,2,2,2850]{4,3,2,1,0:T(2,128)} %collective-permute-done.1), kind=kLoop, calls=%fused_computation.66 | loop fusion | flops 45600 | bytes 364800 | tf_op jit(solution)/shard_map/vmap()/add | solution.py:76
  22.3 0.1 fusion.24
  22.4 0.2 multiply_add_fusion.5
  22.6 0.2 multiply_subtract_fusion.6
  22.8 0.7 fusion
  23.6 0.7 fusion.21
  24.4 0.1 reshape.380
  24.5 7.7 %collective-permute-start.2 = (f32[4866]{0:T(1024)S(1)}, f32[4866]{0:T(1024)S(1)}, u32[]{:S(2)}, u32[]{:S(2)}) collective-permute-start(f32[4866]{0:T(1024)S(1)} %constant_dynamic-update-slice_fusion), channel_id=1, source_target_pairs={{0,1},{1,2},{2,3},{3,4},{4,5},{5,6},{6,7},{7,8},{8,9},{9,10},{10,1... | collective-permute-start | bytes 58400 | tf_op jit(solution)/shard_map/ppermute | solution.py:27
  32.3 1.9 %collective-permute-start.3 = (f32[4866]{0:T(1024)S(1)}, f32[4866]{0:T(1024)S(1)}, u32[]{:S(2)}, u32[]{:S(2)}) collective-permute-start(f32[4866]{0:T(1024)S(1)} %constant_dynamic-update-slice_fusion), channel_id=1, source_target_pairs={{1,0},{2,1},{3,2},{4,3},{5,4},{6,5},{7,6},{8,7},{9,8},{10,9},{11,1... | collective-permute-start | bytes 58400 | tf_op jit(solution)/shard_map/ppermute | solution.py:27
  34.2 0.1 reshape.381
  34.3 9.6 %collective-permute-done.3 = f32[4866]{0:T(1024)S(1)} collective-permute-done((f32[4866]{0:T(1024)S(1)}, f32[4866]{0:T(1024)S(1)}, u32[]{:S(2)}, u32[]{:S(2)}) %collective-permute-start.3) | collective-permute-done | bytes 19496 | tf_op jit(solution)/shard_map/ppermute | solution.py:27
  44.0 0.1 reshape.382
  44.1 0.1 pad_maximum_fusion.7
  44.3 0.1 fusion.38
  44.4 0.5 convolution_bitcast_fusion
  44.9 0.5 convolution_bitcast_fusion.1
  45.3 0.2 multiply_add_fusion.3
  45.6 0.2 fusion.23
  45.8 1.9 %collective-permute-start.4 = (f32[2,1,2,2,2850]{4,3,2,1,0:T(2,128)S(1)}, f32[2,1,2,2,2850]{4,3,2,1,0:T(2,128)S(1)}, u32[]{:S(2)}, u32[]{:S(2)}) collective-permute-start(f32[2,1,2,2,2850]{4,3,2,1,0:T(2,128)S(1)} %bitcast.65), channel_id=1, source_target_pairs={{0,128},{128,0},{256,384},{384,256},{1,129},{129,1},{257,385},{385... | collective-permute-start | bytes 273608 | tf_op jit(solution)/shard_map/ppermute | solution.py:48
  47.7 1.3 %collective-permute-done.4 = f32[2,1,2,2,2850]{4,3,2,1,0:T(2,128)S(1)} collective-permute-done((f32[2,1,2,2,2850]{4,3,2,1,0:T(2,128)S(1)}, f32[2,1,2,2,2850]{4,3,2,1,0:T(2,128)S(1)}, u32[]{:S(2)}, u32[]{:S(2)}) %collective-permute-start.4) | collective-permute-done | bytes 91232 | tf_op jit(solution)/shard_map/ppermute | solution.py:48
  49.1 1.9 %collective-permute-start.5 = (f32[2,1,2,2,2850]{4,3,2,1,0:T(2,128)S(1)}, f32[2,1,2,2,2850]{4,3,2,1,0:T(2,128)S(1)}, u32[]{:S(2)}, u32[]{:S(2)}) collective-permute-start(f32[2,1,2,2,2850]{4,3,2,1,0:T(2,128)S(1)} %bitcast_add_fusion), channel_id=1, source_target_pairs={{0,256},{128,384},{256,0},{384,128},{1,257},{129,385},{257,1},{385... | collective-permute-start | bytes 273608 | tf_op jit(solution)/shard_map/ppermute | solution.py:48
  51.0 8.6 %collective-permute-done.5 = f32[2,1,2,2,2850]{4,3,2,1,0:T(2,128)S(1)} collective-permute-done((f32[2,1,2,2,2850]{4,3,2,1,0:T(2,128)S(1)}, f32[2,1,2,2,2850]{4,3,2,1,0:T(2,128)S(1)}, u32[]{:S(2)}, u32[]{:S(2)}) %collective-permute-start.5) | collective-permute-done | bytes 91232 | tf_op jit(solution)/shard_map/ppermute | solution.py:48
  59.7 0.1 fusion.22
  59.8 0.5 copy-done.2
  60.3 0.2 multiply_add_fusion
  60.5 0.2 multiply_subtract_fusion
  60.8 0.7 fusion.10
  61.5 0.7 fusion.20
  62.3 0.1 reshape.383
  62.4 1.9 %collective-permute-start.6 = (f32[4864]{0:T(1024)S(1)}, f32[4864]{0:T(1024)S(1)}, u32[]{:S(2)}, u32[]{:S(2)}) collective-permute-start(f32[4864]{0:T(1024)S(1)} %reshape.383), channel_id=1, source_target_pairs={{0,1},{1,2},{2,3},{3,4},{4,5},{5,6},{6,7},{7,8},{8,9},{9,10},{10,1... | collective-permute-start | bytes 58376 | tf_op jit(solution)/shard_map/ppermute | solution.py:27
  64.3 3.9 %collective-permute-start.7 = (f32[4864]{0:T(1024)S(1)}, f32[4864]{0:T(1024)S(1)}, u32[]{:S(2)}, u32[]{:S(2)}) collective-permute-start(f32[4864]{0:T(1024)S(1)} %reshape.383), channel_id=1, source_target_pairs={{1,0},{2,1},{3,2},{4,3},{5,4},{6,5},{7,6},{8,7},{9,8},{10,9},{11,1... | collective-permute-start | bytes 58376 | tf_op jit(solution)/shard_map/ppermute | solution.py:27
  68.3 0.1 reshape.384
  68.4 7.6 %collective-permute-done.7 = f32[4864]{0:T(1024)S(1)} collective-permute-done((f32[4864]{0:T(1024)S(1)}, f32[4864]{0:T(1024)S(1)}, u32[]{:S(2)}, u32[]{:S(2)}) %collective-permute-start.7) | collective-permute-done | bytes 19488 | tf_op jit(solution)/shard_map/ppermute | solution.py:27
  76.0 0.1 reshape.385
  76.1 0.1 fusion.29
  76.2 0.6 copy.27
  (32 shorter events, 0.5 us)
Async XLA Ops:
  1.6 1.3 %copy-start.3 = (f32[8,2,2,2,76]{4,3,2,1,0:T(2,128)S(1)}, f32[8,2,2,2,76]{4,3,2,1,0:T(2,128)}, u32[]{:S(2)}) copy-start(f32[8,2,2,2,76]{4,3,2,1,0:T(2,128)} %param.8) | copy-start | bytes 58372
  3.0 1.0 %copy-start = (bf16[8,2,1,2,2,2850]{5,4,3,2,1,0:T(2,128)(2,1)S(1)}, bf16[8,2,1,2,2,2850]{5,4,3,2,1,0:T(2,128)(2,1)}, u32[]{:S(2)}) copy-start(bf16[8,2,1,2,2,2850]{5,4,3,2,1,0:T(2,128)(2,1)} %param.7) | copy-start | bytes 1094404
  4.5 3.2 %collective-permute-start = (f32[2,1,2,2,2850]{4,3,2,1,0:T(2,128)S(1)}, f32[2,1,2,2,2850]{4,3,2,1,0:T(2,128)S(1)}, u32[]{:S(2)}, u32[]{:S(2)}) collective-permute-start(f32[2,1,2,2,2850]{4,3,2,1,0:T(2,128)S(1)} %bitcast.64), channel_id=1, source_target_pairs={{0,128},{128,0},{256,384},{384,256},{1,129},{129,1},{257,385},{385... | collective-permute-start | bytes 273608 | tf_op jit(solution)/shard_map/ppermute | solution.py:48
  8.4 12.9 %collective-permute-start.1 = (f32[2,1,2,2,2850]{4,3,2,1,0:T(2,128)}, f32[2,1,2,2,2850]{4,3,2,1,0:T(2,128)}, u32[]{:S(2)}, u32[]{:S(2)}) collective-permute-start(f32[2,1,2,2,2850]{4,3,2,1,0:T(2,128)} %bitcast_add_fusion.1), channel_id=1, source_target_pairs={{0,256},{128,384},{256,0},{384,128},{1,257},{129,385},{257,1},{385... | collective-permute-start | bytes 273608 | tf_op jit(solution)/shard_map/ppermute | solution.py:48
  23.6 0.9 %copy-start.4 = (f32[2]{0:T(128)S(1)}, f32[2]{0:T(128)}, u32[]{:S(2)}) copy-start(f32[2]{0:T(128)} %param.9) | copy-start | bytes 28
  23.6 20.6 %copy-start.5 = (s32[2]{0:T(128)S(1)}, s32[2]{0:T(128)}, u32[]{:S(2)}) copy-start(s32[2]{0:T(128)} %param.10) | copy-start | bytes 28
  24.5 9.7 %collective-permute-start.2 = (f32[4866]{0:T(1024)S(1)}, f32[4866]{0:T(1024)S(1)}, u32[]{:S(2)}, u32[]{:S(2)}) collective-permute-start(f32[4866]{0:T(1024)S(1)} %constant_dynamic-update-slice_fusion), channel_id=1, source_target_pairs={{0,1},{1,2},{2,3},{3,4},{4,5},{5,6},{6,7},{7,8},{8,9},{9,10},{10,1... | collective-permute-start | bytes 58400 | tf_op jit(solution)/shard_map/ppermute | solution.py:27
  32.3 11.7 %collective-permute-start.3 = (f32[4866]{0:T(1024)S(1)}, f32[4866]{0:T(1024)S(1)}, u32[]{:S(2)}, u32[]{:S(2)}) collective-permute-start(f32[4866]{0:T(1024)S(1)} %constant_dynamic-update-slice_fusion), channel_id=1, source_target_pairs={{1,0},{2,1},{3,2},{4,3},{5,4},{6,5},{7,6},{8,7},{9,8},{10,9},{11,1... | collective-permute-start | bytes 58400 | tf_op jit(solution)/shard_map/ppermute | solution.py:27
  45.6 14.1 %copy-start.1 = (f32[2,1,2,2,2850]{4,3,2,1,0:T(2,128)S(1)}, f32[2,1,2,2,2850]{4,3,2,1,0:T(2,128)}, u32[]{:S(2)}) copy-start(f32[2,1,2,2,2850]{4,3,2,1,0:T(2,128)} %param.6) | copy-start | bytes 273604
  45.8 3.2 %collective-permute-start.4 = (f32[2,1,2,2,2850]{4,3,2,1,0:T(2,128)S(1)}, f32[2,1,2,2,2850]{4,3,2,1,0:T(2,128)S(1)}, u32[]{:S(2)}, u32[]{:S(2)}) collective-permute-start(f32[2,1,2,2,2850]{4,3,2,1,0:T(2,128)S(1)} %bitcast.65), channel_id=1, source_target_pairs={{0,128},{128,0},{256,384},{384,256},{1,129},{129,1},{257,385},{385... | collective-permute-start | bytes 273608 | tf_op jit(solution)/shard_map/ppermute | solution.py:48
  49.1 10.6 %collective-permute-start.5 = (f32[2,1,2,2,2850]{4,3,2,1,0:T(2,128)S(1)}, f32[2,1,2,2,2850]{4,3,2,1,0:T(2,128)S(1)}, u32[]{:S(2)}, u32[]{:S(2)}) collective-permute-start(f32[2,1,2,2,2850]{4,3,2,1,0:T(2,128)S(1)} %bitcast_add_fusion), channel_id=1, source_target_pairs={{0,256},{128,384},{256,0},{384,128},{1,257},{129,385},{257,1},{385... | collective-permute-start | bytes 273608 | tf_op jit(solution)/shard_map/ppermute | solution.py:48
  59.7 0.6 copy-start.2
  62.4 5.9 %collective-permute-start.6 = (f32[4864]{0:T(1024)S(1)}, f32[4864]{0:T(1024)S(1)}, u32[]{:S(2)}, u32[]{:S(2)}) collective-permute-start(f32[4864]{0:T(1024)S(1)} %reshape.383), channel_id=1, source_target_pairs={{0,1},{1,2},{2,3},{3,4},{4,5},{5,6},{6,7},{7,8},{8,9},{9,10},{10,1... | collective-permute-start | bytes 58376 | tf_op jit(solution)/shard_map/ppermute | solution.py:27
  64.3 11.7 %collective-permute-start.7 = (f32[4864]{0:T(1024)S(1)}, f32[4864]{0:T(1024)S(1)}, u32[]{:S(2)}, u32[]{:S(2)}) collective-permute-start(f32[4864]{0:T(1024)S(1)} %reshape.383), channel_id=1, source_target_pairs={{1,0},{2,1},{3,2},{4,3},{5,4},{6,5},{7,6},{8,7},{9,8},{10,9},{11,1... | collective-permute-start | bytes 58376 | tf_op jit(solution)/shard_map/ppermute | solution.py:27

commit v9 on v3

--- a/solution.py
+++ b/solution.py
@@ -10,7 +10,7 @@
 
 step_size = 0.6
 epsilon = 1e-06
-highest = lax.Precision.HIGHEST
+table_precision = lax.Precision.HIGH
 
 
 def extended(items, axis, width):
@@ -59,8 +59,8 @@
 
 def corrupt(gains, model, left_hot, right_hot):
     model = model.astype(jnp.float32)
-    left_gain = jnp.matmul(gains, left_hot, precision=highest)[:, None]
-    right_gain = jnp.matmul(gains, right_hot, precision=highest)[:, None]
+    left_gain = jnp.matmul(gains, left_hot, precision=table_precision)[:, None]
+    right_gain = jnp.matmul(gains, right_hot, precision=table_precision)[:, None]
     left_re, left_im = (left_gain[..., 0, :], left_gain[..., 1, :])
     right_re, right_im = (right_gain[..., 0, :], right_gain[..., 1, :])
     model_re, model_im = (model[..., 0, :], model[..., 1, :])
@@ -88,8 +88,8 @@
     right_den = power * (left_re * left_re + left_im * left_im)
     left_products = jnp.sum(jnp.stack([left_num_re, left_num_im, left_den], axis=3), axis=1)
     right_terms = jnp.sum(jnp.stack([right_num_re, right_num_im, right_den], axis=3), axis=1)
-    totals = jnp.matmul(left_products, left_hot.T, precision=highest) + jnp.matmul(
-        right_terms, right_hot.T, precision=highest
+    totals = jnp.matmul(left_products, left_hot.T, precision=table_precision) + jnp.matmul(
+        right_terms, right_hot.T, precision=table_precision
     )
     solved = totals[:, :, 0:2] / (totals[:, :, 2:3] + epsilon)
     return (1.0 - step_size) * gains + step_size * solved

time: 75.7 us -> 74.1 us (0.979)
  matrix products: 6.06 us -> 4.39 us
    dot_general x8, matrix products: 6.06 us -> 4.39 us  [the longest x2 1.69 us: corrupt(): jnp.matmul(gains, right_hot, precision=table_precision)[:, None]]
where the time goes in v9:
time: 74.1 us; the launch traced here: 73.7 us
  waiting for transfers between devices  36.3 us (49%)
  starting transfers between devices  26 us (35%)
  matrix products  4.39 us (6%)
  local copies, waits for them, and re-layouts  3.39 us (5%)
  other arithmetic  2.57 us (3%)
  between operations  1.06 us (1%)
    ppermute x4, waiting for transfers between devices, sum_over_dir(): lax.ppermute(total, 'dir', [(i, i ^ mask) for i in range(count)])  19 us
    ppermute x4, waiting for transfers between devices, send(): arrived = lax.ppermute(flat, axis, pairs)  17.2 us
    ppermute x4, starting transfers between devices, send(): arrived = lax.ppermute(flat, axis, pairs)  15.5 us
    ppermute x4, starting transfers between devices, sum_over_dir(): lax.ppermute(total, 'dir', [(i, i ^ mask) for i in range(count)])  10.5 us
    unnamed x14, local copies, waits for them, and re-layouts  1.75 us
    dot_general x2, matrix products, corrupt(): jnp.matmul(gains, right_hot, precision=table_precision)[:, None]  1.69 us
  transfers between devices with their start and end apart: 8, of which 6 were waited for; matrix products, arithmetic and copies ran while one was open for 0% of the time, Pallas kernels for 0%

profile of v9, /device:TPU:254, one launch (start us, length us, event | category | flops | bytes accessed | tf_op | source)
XLA Modules:
  0.0 73.7 jit_solution(17190736762654987902)
XLA Ops:
  0.6 0.9 %slice_reduce_fusion.1 = (s32[2850]{0:T(1024)S(1)}, s32[2850]{0:T(1024)S(1)}) fusion(s32[2,2850]{1,0:T(2,128)} %param.11), kind=kLoop, calls=%fused_computation.107 | loop fusion | bytes 45600 | tf_op jit(solution)/shard_map/slice | solution.py:55
  1.5 1.2 %convolution_bitcast_fusion.2 = f32[8,2,1,2,2,2850]{5,0,4,3,1,2:T(8,128)S(1)} fusion(s32[2850]{0:T(1024)S(1)} %get-tuple-element.7, f32[8,2,2,2,76]{4,3,2,1,0:T(2,128)} %param.8), kind=kOutput, calls=%fused_computation.2 | convolution fusion | flops 83391000 | bytes 760456 | tf_op jit(solution)/shard_map/vmap()/dot_general | solution.py:63
  2.8 0.4 convolution_bitcast_fusion.3
  3.2 0.5 copy-done
  3.8 0.1 multiply_add_fusion.9
  4.0 0.1 multiply_subtract_fusion.8
  4.1 0.2 fusion.35
  4.3 1.9 %collective-permute-start = (f32[2,1,2,2,2850]{4,3,2,1,0:T(2,128)S(1)}, f32[2,1,2,2,2850]{4,3,2,1,0:T(2,128)S(1)}, u32[]{:S(2)}, u32[]{:S(2)}) collective-permute-start(f32[2,1,2,2,2850]{4,3,2,1,0:T(2,128)S(1)} %bitcast.60), channel_id=1, source_target_pairs={{0,128},{128,0},{256,384},{384,256},{1,129},{129,1},{257,385},{385... | collective-permute-start | bytes 273608 | tf_op jit(solution)/shard_map/ppermute | solution.py:48
  6.2 1.3 %collective-permute-done = f32[2,1,2,2,2850]{4,3,2,1,0:T(2,128)S(1)} collective-permute-done((f32[2,1,2,2,2850]{4,3,2,1,0:T(2,128)S(1)}, f32[2,1,2,2,2850]{4,3,2,1,0:T(2,128)S(1)}, u32[]{:S(2)}, u32[]{:S(2)}) %collective-permute-start) | collective-permute-done | bytes 91232 | tf_op jit(solution)/shard_map/ppermute | solution.py:48
  7.5 4.7 %collective-permute-start.1 = (f32[2,1,2,2,2850]{4,3,2,1,0:T(2,128)S(1)}, f32[2,1,2,2,2850]{4,3,2,1,0:T(2,128)S(1)}, u32[]{:S(2)}, u32[]{:S(2)}) collective-permute-start(f32[2,1,2,2,2850]{4,3,2,1,0:T(2,128)S(1)} %bitcast_add_fusion.1), channel_id=1, source_target_pairs={{0,256},{128,384},{256,0},{384,128},{1,257},{129,385},{257,1},{385... | collective-permute-start | bytes 273608 | tf_op jit(solution)/shard_map/ppermute | solution.py:48
  12.3 7.9 %collective-permute-done.1 = f32[2,1,2,2,2850]{4,3,2,1,0:T(2,128)S(1)} collective-permute-done((f32[2,1,2,2,2850]{4,3,2,1,0:T(2,128)S(1)}, f32[2,1,2,2,2850]{4,3,2,1,0:T(2,128)S(1)}, u32[]{:S(2)}, u32[]{:S(2)}) %collective-permute-start.1) | collective-permute-done | bytes 91232 | tf_op jit(solution)/shard_map/ppermute | solution.py:48
  20.2 0.1 fusion.34
  20.3 0.2 multiply_add_fusion.5
  20.5 0.2 multiply_subtract_fusion.6
  20.7 0.5 fusion
  21.2 0.5 fusion.21
  21.7 0.1 reshape.379
  21.9 7.7 %collective-permute-start.2 = (f32[4866]{0:T(1024)S(1)}, f32[4866]{0:T(1024)S(1)}, u32[]{:S(2)}, u32[]{:S(2)}) collective-permute-start(f32[4866]{0:T(1024)S(1)} %constant_dynamic-update-slice_fusion), channel_id=1, source_target_pairs={{0,1},{1,2},{2,3},{3,4},{4,5},{5,6},{6,7},{7,8},{8,9},{9,10},{10,1... | collective-permute-start | bytes 58400 | tf_op jit(solution)/shard_map/ppermute | solution.py:27
  29.6 1.9 %collective-permute-start.3 = (f32[4866]{0:T(1024)S(1)}, f32[4866]{0:T(1024)S(1)}, u32[]{:S(2)}, u32[]{:S(2)}) collective-permute-start(f32[4866]{0:T(1024)S(1)} %constant_dynamic-update-slice_fusion), channel_id=1, source_target_pairs={{1,0},{2,1},{3,2},{4,3},{5,4},{6,5},{7,6},{8,7},{9,8},{10,9},{11,1... | collective-permute-start | bytes 58400 | tf_op jit(solution)/shard_map/ppermute | solution.py:27
  31.6 0.1 reshape.380
  31.7 9.6 %collective-permute-done.3 = f32[4866]{0:T(1024)S(1)} collective-permute-done((f32[4866]{0:T(1024)S(1)}, f32[4866]{0:T(1024)S(1)}, u32[]{:S(2)}, u32[]{:S(2)}) %collective-permute-start.3) | collective-permute-done | bytes 19496 | tf_op jit(solution)/shard_map/ppermute | solution.py:27
  41.3 0.1 reshape.381
  41.5 0.1 pad_maximum_fusion.7
  41.6 0.1 add_add_fusion
  41.6 0.1 fusion.56
  41.7 0.4 convolution_bitcast_fusion
  42.2 0.4 convolution_bitcast_fusion.1
  42.7 0.2 multiply_add_fusion.3
  42.8 0.1 multiply_subtract_fusion.3
  42.9 0.2 fusion.33
  43.1 1.9 %collective-permute-start.4 = (f32[2,1,2,2,2850]{4,3,2,1,0:T(2,128)S(1)}, f32[2,1,2,2,2850]{4,3,2,1,0:T(2,128)S(1)}, u32[]{:S(2)}, u32[]{:S(2)}) collective-permute-start(f32[2,1,2,2,2850]{4,3,2,1,0:T(2,128)S(1)} %bitcast.61), channel_id=1, source_target_pairs={{0,128},{128,0},{256,384},{384,256},{1,129},{129,1},{257,385},{385... | collective-permute-start | bytes 273608 | tf_op jit(solution)/shard_map/ppermute | solution.py:48
  45.1 1.3 %collective-permute-done.4 = f32[2,1,2,2,2850]{4,3,2,1,0:T(2,128)S(1)} collective-permute-done((f32[2,1,2,2,2850]{4,3,2,1,0:T(2,128)S(1)}, f32[2,1,2,2,2850]{4,3,2,1,0:T(2,128)S(1)}, u32[]{:S(2)}, u32[]{:S(2)}) %collective-permute-start.4) | collective-permute-done | bytes 91232 | tf_op jit(solution)/shard_map/ppermute | solution.py:48
  46.4 1.9 %collective-permute-start.5 = (f32[2,1,2,2,2850]{4,3,2,1,0:T(2,128)S(1)}, f32[2,1,2,2,2850]{4,3,2,1,0:T(2,128)S(1)}, u32[]{:S(2)}, u32[]{:S(2)}) collective-permute-start(f32[2,1,2,2,2850]{4,3,2,1,0:T(2,128)S(1)} %bitcast_add_fusion), channel_id=1, source_target_pairs={{0,256},{128,384},{256,0},{384,128},{1,257},{129,385},{257,1},{385... | collective-permute-start | bytes 273608 | tf_op jit(solution)/shard_map/ppermute | solution.py:48
  48.3 8.6 %collective-permute-done.5 = f32[2,1,2,2,2850]{4,3,2,1,0:T(2,128)S(1)} collective-permute-done((f32[2,1,2,2,2850]{4,3,2,1,0:T(2,128)S(1)}, f32[2,1,2,2,2850]{4,3,2,1,0:T(2,128)S(1)}, u32[]{:S(2)}, u32[]{:S(2)}) %collective-permute-start.5) | collective-permute-done | bytes 91232 | tf_op jit(solution)/shard_map/ppermute | solution.py:48
  57.0 0.1 fusion.32
  57.1 0.5 copy-done.2
  57.7 0.2 multiply_add_fusion
  57.8 0.2 multiply_subtract_fusion
  58.1 0.5 fusion.10
  58.5 0.5 fusion.20
  59.1 0.1 reshape.382
  59.2 1.9 %collective-permute-start.6 = (f32[4864]{0:T(1024)S(1)}, f32[4864]{0:T(1024)S(1)}, u32[]{:S(2)}, u32[]{:S(2)}) collective-permute-start(f32[4864]{0:T(1024)S(1)} %reshape.382), channel_id=1, source_target_pairs={{0,1},{1,2},{2,3},{3,4},{4,5},{5,6},{6,7},{7,8},{8,9},{9,10},{10,1... | collective-permute-start | bytes 58376 | tf_op jit(solution)/shard_map/ppermute | solution.py:27
  61.1 3.9 %collective-permute-start.7 = (f32[4864]{0:T(1024)S(1)}, f32[4864]{0:T(1024)S(1)}, u32[]{:S(2)}, u32[]{:S(2)}) collective-permute-start(f32[4864]{0:T(1024)S(1)} %reshape.382), channel_id=1, source_target_pairs={{1,0},{2,1},{3,2},{4,3},{5,4},{6,5},{7,6},{8,7},{9,8},{10,9},{11,1... | collective-permute-start | bytes 58376 | tf_op jit(solution)/shard_map/ppermute | solution.py:27
  65.0 0.1 reshape.383
  65.2 7.6 %collective-permute-done.7 = f32[4864]{0:T(1024)S(1)} collective-permute-done((f32[4864]{0:T(1024)S(1)}, f32[4864]{0:T(1024)S(1)}, u32[]{:S(2)}, u32[]{:S(2)}) %collective-permute-start.7) | collective-permute-done | bytes 19488 | tf_op jit(solution)/shard_map/ppermute | solution.py:27
  72.8 0.1 reshape.384
  72.9 0.1 fusion.47
  73.0 0.6 copy.27
  (32 shorter events, 0.5 us)
Async XLA Ops:
  1.5 1.3 %copy-start.3 = (f32[8,2,2,2,76]{4,3,2,1,0:T(2,128)S(1)}, f32[8,2,2,2,76]{4,3,2,1,0:T(2,128)}, u32[]{:S(2)}) copy-start(f32[8,2,2,2,76]{4,3,2,1,0:T(2,128)} %param.8) | copy-start | bytes 58372
  2.8 1.0 %copy-start = (bf16[8,2,1,2,2,2850]{5,4,3,2,1,0:T(2,128)(2,1)S(1)}, bf16[8,2,1,2,2,2850]{5,4,3,2,1,0:T(2,128)(2,1)}, u32[]{:S(2)}) copy-start(bf16[8,2,1,2,2,2850]{5,4,3,2,1,0:T(2,128)(2,1)} %param.7) | copy-start | bytes 1094404
  4.1 16.1 %copy-start.1 = (f32[2,1,2,2,2850]{4,3,2,1,0:T(2,128)S(1)}, f32[2,1,2,2,2850]{4,3,2,1,0:T(2,128)}, u32[]{:S(2)}) copy-start(f32[2,1,2,2,2850]{4,3,2,1,0:T(2,128)} %param.6) | copy-start | bytes 273604
  4.3 3.2 %collective-permute-start = (f32[2,1,2,2,2850]{4,3,2,1,0:T(2,128)S(1)}, f32[2,1,2,2,2850]{4,3,2,1,0:T(2,128)S(1)}, u32[]{:S(2)}, u32[]{:S(2)}) collective-permute-start(f32[2,1,2,2,2850]{4,3,2,1,0:T(2,128)S(1)} %bitcast.60), channel_id=1, source_target_pairs={{0,128},{128,0},{256,384},{384,256},{1,129},{129,1},{257,385},{385... | collective-permute-start | bytes 273608 | tf_op jit(solution)/shard_map/ppermute | solution.py:48
  7.5 12.6 %collective-permute-start.1 = (f32[2,1,2,2,2850]{4,3,2,1,0:T(2,128)S(1)}, f32[2,1,2,2,2850]{4,3,2,1,0:T(2,128)S(1)}, u32[]{:S(2)}, u32[]{:S(2)}) collective-permute-start(f32[2,1,2,2,2850]{4,3,2,1,0:T(2,128)S(1)} %bitcast_add_fusion.1), channel_id=1, source_target_pairs={{0,256},{128,384},{256,0},{384,128},{1,257},{129,385},{257,1},{385... | collective-permute-start | bytes 273608 | tf_op jit(solution)/shard_map/ppermute | solution.py:48
  21.2 0.7 copy-start.4
  21.2 20.4 %copy-start.5 = (s32[2]{0:T(128)S(1)}, s32[2]{0:T(128)}, u32[]{:S(2)}) copy-start(s32[2]{0:T(128)} %param.10) | copy-start | bytes 28
  21.9 9.7 %collective-permute-start.2 = (f32[4866]{0:T(1024)S(1)}, f32[4866]{0:T(1024)S(1)}, u32[]{:S(2)}, u32[]{:S(2)}) collective-permute-start(f32[4866]{0:T(1024)S(1)} %constant_dynamic-update-slice_fusion), channel_id=1, source_target_pairs={{0,1},{1,2},{2,3},{3,4},{4,5},{5,6},{6,7},{7,8},{8,9},{9,10},{10,1... | collective-permute-start | bytes 58400 | tf_op jit(solution)/shard_map/ppermute | solution.py:27
  29.6 11.7 %collective-permute-start.3 = (f32[4866]{0:T(1024)S(1)}, f32[4866]{0:T(1024)S(1)}, u32[]{:S(2)}, u32[]{:S(2)}) collective-permute-start(f32[4866]{0:T(1024)S(1)} %constant_dynamic-update-slice_fusion), channel_id=1, source_target_pairs={{1,0},{2,1},{3,2},{4,3},{5,4},{6,5},{7,6},{8,7},{9,8},{10,9},{11,1... | collective-permute-start | bytes 58400 | tf_op jit(solution)/shard_map/ppermute | solution.py:27
  43.1 3.2 %collective-permute-start.4 = (f32[2,1,2,2,2850]{4,3,2,1,0:T(2,128)S(1)}, f32[2,1,2,2,2850]{4,3,2,1,0:T(2,128)S(1)}, u32[]{:S(2)}, u32[]{:S(2)}) collective-permute-start(f32[2,1,2,2,2850]{4,3,2,1,0:T(2,128)S(1)} %bitcast.61), channel_id=1, source_target_pairs={{0,128},{128,0},{256,384},{384,256},{1,129},{129,1},{257,385},{385... | collective-permute-start | bytes 273608 | tf_op jit(solution)/shard_map/ppermute | solution.py:48
  46.4 10.6 %collective-permute-start.5 = (f32[2,1,2,2,2850]{4,3,2,1,0:T(2,128)S(1)}, f32[2,1,2,2,2850]{4,3,2,1,0:T(2,128)S(1)}, u32[]{:S(2)}, u32[]{:S(2)}) collective-permute-start(f32[2,1,2,2,2850]{4,3,2,1,0:T(2,128)S(1)} %bitcast_add_fusion), channel_id=1, source_target_pairs={{0,256},{128,384},{256,0},{384,128},{1,257},{129,385},{257,1},{385... | collective-permute-start | bytes 273608 | tf_op jit(solution)/shard_map/ppermute | solution.py:48
  57.0 0.6 copy-start.2
  59.2 5.9 %collective-permute-start.6 = (f32[4864]{0:T(1024)S(1)}, f32[4864]{0:T(1024)S(1)}, u32[]{:S(2)}, u32[]{:S(2)}) collective-permute-start(f32[4864]{0:T(1024)S(1)} %reshape.382), channel_id=1, source_target_pairs={{0,1},{1,2},{2,3},{3,4},{4,5},{5,6},{6,7},{7,8},{8,9},{9,10},{10,1... | collective-permute-start | bytes 58376 | tf_op jit(solution)/shard_map/ppermute | solution.py:27
  61.1 11.7 %collective-permute-start.7 = (f32[4864]{0:T(1024)S(1)}, f32[4864]{0:T(1024)S(1)}, u32[]{:S(2)}, u32[]{:S(2)}) collective-permute-start(f32[4864]{0:T(1024)S(1)} %reshape.382), channel_id=1, source_target_pairs={{1,0},{2,1},{3,2},{4,3},{5,4},{6,5},{7,6},{8,7},{9,8},{10,9},{11,1... | collective-permute-start | bytes 58376 | tf_op jit(solution)/shard_map/ppermute | solution.py:27

commit v10 on v9

--- a/solution.py
+++ b/solution.py
@@ -13,31 +13,20 @@
 table_precision = lax.Precision.HIGH
 
 
-def extended(items, axis, width):
+def extended(cells, axis, dim, width):
     count = lax.axis_size(axis)
     ends = count - 1
-
-    def edge(cells, dim, first):
-        size = cells.shape[dim]
-        start = 0 if first else size - width
-        return lax.slice_in_dim(cells, start, start + width, axis=dim)
-
-    def send(pieces, pairs):
-        flat = jnp.concatenate([piece.reshape(-1) for piece in pieces])
-        arrived = lax.ppermute(flat, axis, pairs)
-        out = []
-        offset = 0
-        for piece in pieces:
-            out.append(arrived[offset : offset + piece.size].reshape(piece.shape))
-            offset += piece.size
-        return out
-
-    from_left = send([edge(c, d, False) for c, d in items], [(i, i + 1) for i in range(ends)])
-    from_right = send([edge(c, d, True) for c, d in items], [(i + 1, i) for i in range(ends)])
-    return [
-        jnp.concatenate([left, cells, right], axis=dim)
-        for (cells, dim), left, right in zip(items, from_left, from_right)
-    ]
+    size = cells.shape[dim]
+    head = lax.slice_in_dim(cells, 0, width, axis=dim)
+    tail = lax.slice_in_dim(cells, size - width, size, axis=dim)
+    return jnp.concatenate(
+        [
+            lax.ppermute(tail, axis, [(i, i + 1) for i in range(ends)]),
+            cells,
+            lax.ppermute(head, axis, [(i + 1, i) for i in range(ends)]),
+        ],
+        axis=dim,
+    )
 
 
 def sum_over_dir(partial):
@@ -127,9 +116,12 @@
         residual = visibilities - total
         stepped = solve_all(current, model, corrupted_model, parts, residual, left_hot, right_hot)
         if padded_weights is None:
-            padded_gains, padded_weights = extended(((stepped, 1), (weights, 0)), "chan", SPAN)
+            column = jnp.broadcast_to(weights[None, :, None, None, None], stepped.shape[:-1] + (1,))
+            padded = extended(jnp.concatenate([stepped, column], axis=-1), "chan", 1, SPAN)
+            padded_gains = padded[..., :-1]
+            padded_weights = padded[0, :, 0, 0, -1]
         else:
-            (padded_gains,) = extended(((stepped, 1),), "chan", SPAN)
+            padded_gains = extended(stepped, "chan", 1, SPAN)
         current = smooth(padded_gains, padded_weights, widths)
     return (current, residual)
 

time: 74.1 us -> 74 us (level)
    unnamed x14 -> x13, local copies, waits for them, and re-layouts: 1.75 us -> 1.89 us
where the time goes in v10:
time: 74 us; the launch traced here: 73.5 us
  waiting for transfers between devices  36.8 us (50%)
  starting transfers between devices  26 us (35%)
  matrix products  4.39 us (6%)
  local copies, waits for them, and re-layouts  2.83 us (4%)
  other arithmetic  2.58 us (3%)
  between operations  0.96 us (1%)
    ppermute x4, waiting for transfers between devices, sum_over_dir(): lax.ppermute(total, 'dir', [(i, i ^ mask) for i in range(count)])  19 us
    ppermute x2, waiting for transfers between devices, extended(): lax.ppermute(head, axis, [(i + 1, i) for i in range(ends)])  17.8 us
    ppermute x4, starting transfers between devices, sum_over_dir(): lax.ppermute(total, 'dir', [(i, i ^ mask) for i in range(count)])  10.5 us
    ppermute x2, starting transfers between devices, extended(): lax.ppermute(tail, axis, [(i, i + 1) for i in range(ends)])  9.65 us
    ppermute x2, starting transfers between devices, extended(): lax.ppermute(head, axis, [(i + 1, i) for i in range(ends)])  5.84 us
    unnamed x13, local copies, waits for them, and re-layouts  1.89 us
    dot_general x2, matrix products, corrupt(): jnp.matmul(gains, right_hot, precision=table_precision)[:, None]  1.69 us
  transfers between devices with their start and end apart: 8, of which 6 were waited for; matrix products, arithmetic and copies ran while one was open for 0% of the time, Pallas kernels for 0%

profile of v10, /device:TPU:254, one launch (start us, length us, event | category | flops | bytes accessed | tf_op | source)
XLA Modules:
  0.0 73.5 jit_solution(7435012322662597692)
XLA Ops:
  0.6 0.9 %slice_reduce_fusion.1 = (s32[2850]{0:T(1024)S(1)}, s32[2850]{0:T(1024)S(1)}) fusion(s32[2,2850]{1,0:T(2,128)} %param.11), kind=kLoop, calls=%fused_computation.112 | loop fusion | bytes 45600 | tf_op jit(solution)/shard_map/slice | solution.py:44
  1.5 1.2 %convolution_bitcast_fusion.2 = f32[8,2,1,2,2,2850]{5,0,4,3,1,2:T(8,128)S(1)} fusion(s32[2850]{0:T(1024)S(1)} %get-tuple-element.11, f32[8,2,2,2,76]{4,3,2,1,0:T(2,128)} %param.8), kind=kOutput, calls=%fused_computation.2 | convolution fusion | flops 83391000 | bytes 760456 | tf_op jit(solution)/shard_map/vmap()/dot_general | solution.py:52
  2.8 0.4 convolution_bitcast_fusion.3
  3.2 0.5 copy-done
  3.8 0.1 copy_convert_fusion
  3.8 0.1 multiply_add_fusion.9
  4.0 0.1 multiply_subtract_fusion.8
  4.1 0.2 fusion.35
  4.3 1.9 %collective-permute-start = (f32[2,1,2,2,2850]{4,3,2,1,0:T(2,128)S(1)}, f32[2,1,2,2,2850]{4,3,2,1,0:T(2,128)S(1)}, u32[]{:S(2)}, u32[]{:S(2)}) collective-permute-start(f32[2,1,2,2,2850]{4,3,2,1,0:T(2,128)S(1)} %bitcast.58), channel_id=1, source_target_pairs={{0,128},{128,0},{256,384},{384,256},{1,129},{129,1},{257,385},{385... | collective-permute-start | bytes 273608 | tf_op jit(solution)/shard_map/ppermute | solution.py:37
  6.2 1.3 %collective-permute-done = f32[2,1,2,2,2850]{4,3,2,1,0:T(2,128)S(1)} collective-permute-done((f32[2,1,2,2,2850]{4,3,2,1,0:T(2,128)S(1)}, f32[2,1,2,2,2850]{4,3,2,1,0:T(2,128)S(1)}, u32[]{:S(2)}, u32[]{:S(2)}) %collective-permute-start) | collective-permute-done | bytes 91232 | tf_op jit(solution)/shard_map/ppermute | solution.py:37
  7.5 4.7 %collective-permute-start.1 = (f32[2,1,2,2,2850]{4,3,2,1,0:T(2,128)S(1)}, f32[2,1,2,2,2850]{4,3,2,1,0:T(2,128)S(1)}, u32[]{:S(2)}, u32[]{:S(2)}) collective-permute-start(f32[2,1,2,2,2850]{4,3,2,1,0:T(2,128)S(1)} %bitcast_add_fusion.1), channel_id=1, source_target_pairs={{0,256},{128,384},{256,0},{384,128},{1,257},{129,385},{257,1},{385... | collective-permute-start | bytes 273608 | tf_op jit(solution)/shard_map/ppermute | solution.py:37
  12.2 7.9 %collective-permute-done.1 = f32[2,1,2,2,2850]{4,3,2,1,0:T(2,128)S(1)} collective-permute-done((f32[2,1,2,2,2850]{4,3,2,1,0:T(2,128)S(1)}, f32[2,1,2,2,2850]{4,3,2,1,0:T(2,128)S(1)}, u32[]{:S(2)}, u32[]{:S(2)}) %collective-permute-start.1) | collective-permute-done | bytes 91232 | tf_op jit(solution)/shard_map/ppermute | solution.py:37
  20.1 0.1 subtract_bitcast_fusion
  20.2 0.1 fusion.34
  20.3 0.2 multiply_add_fusion.5
  20.5 0.2 multiply_subtract_fusion.6
  20.7 0.5 fusion
  21.2 0.5 fusion.21
  21.7 0.1 copy-done.4
  21.8 0.1 broadcast_in_dim.12
  21.9 0.1 pad_maximum_fusion.8
  22.0 7.7 %collective-permute-start.2 = (f32[8,2,2,2,77]{4,0,3,2,1:T(8,128)S(1)}, f32[8,2,2,2,77]{4,0,3,2,1:T(8,128)S(1)}, u32[]{:S(2)}, u32[]{:S(2)}) collective-permute-start(f32[8,2,2,2,77]{4,0,3,2,1:T(8,128)S(1)} %pad_maximum_fusion.8), channel_id=1, source_target_pairs={{0,1},{1,2},{2,3},{3,4},{4,5},{5,6},{6,7},{7,8},{8,9},{9,10},{10,1... | collective-permute-start | bytes 59144 | tf_op jit(solution)/shard_map/ppermute | solution.py:24
  29.7 1.9 %collective-permute-start.3 = (f32[8,2,2,2,77]{4,0,3,2,1:T(8,128)S(1)}, f32[8,2,2,2,77]{4,0,3,2,1:T(8,128)S(1)}, u32[]{:S(2)}, u32[]{:S(2)}) collective-permute-start(f32[8,2,2,2,77]{4,0,3,2,1:T(8,128)S(1)} %pad_maximum_fusion.8), channel_id=1, source_target_pairs={{1,0},{2,1},{3,2},{4,3},{5,4},{6,5},{7,6},{8,7},{9,8},{10,9},{11,1... | collective-permute-start | bytes 59144 | tf_op jit(solution)/shard_map/ppermute | solution.py:26
  31.7 9.9 %collective-permute-done.3 = f32[8,2,2,2,77]{4,0,3,2,1:T(8,128)S(1)} collective-permute-done((f32[8,2,2,2,77]{4,0,3,2,1:T(8,128)S(1)}, f32[8,2,2,2,77]{4,0,3,2,1:T(8,128)S(1)}, u32[]{:S(2)}, u32[]{:S(2)}) %collective-permute-start.3) | collective-permute-done | bytes 19744 | tf_op jit(solution)/shard_map/ppermute | solution.py:26
  41.5 0.2 maximum_reduce_fusion.1
  41.8 0.1 fusion.54
  41.9 0.4 convolution_bitcast_fusion
  42.3 0.4 convolution_bitcast_fusion.1
  42.8 0.1 multiply_add_fusion.3
  42.9 0.1 multiply_subtract_fusion.3
  43.0 0.2 fusion.33
  43.2 1.9 %collective-permute-start.4 = (f32[2,1,2,2,2850]{4,3,2,1,0:T(2,128)S(1)}, f32[2,1,2,2,2850]{4,3,2,1,0:T(2,128)S(1)}, u32[]{:S(2)}, u32[]{:S(2)}) collective-permute-start(f32[2,1,2,2,2850]{4,3,2,1,0:T(2,128)S(1)} %bitcast.59), channel_id=1, source_target_pairs={{0,128},{128,0},{256,384},{384,256},{1,129},{129,1},{257,385},{385... | collective-permute-start | bytes 273608 | tf_op jit(solution)/shard_map/ppermute | solution.py:37
  45.1 1.3 %collective-permute-done.4 = f32[2,1,2,2,2850]{4,3,2,1,0:T(2,128)S(1)} collective-permute-done((f32[2,1,2,2,2850]{4,3,2,1,0:T(2,128)S(1)}, f32[2,1,2,2,2850]{4,3,2,1,0:T(2,128)S(1)}, u32[]{:S(2)}, u32[]{:S(2)}) %collective-permute-start.4) | collective-permute-done | bytes 91232 | tf_op jit(solution)/shard_map/ppermute | solution.py:37
  46.4 0.1 bitcast_add_fusion
  46.4 1.9 %collective-permute-start.5 = (f32[2,1,2,2,2850]{4,3,2,1,0:T(2,128)S(1)}, f32[2,1,2,2,2850]{4,3,2,1,0:T(2,128)S(1)}, u32[]{:S(2)}, u32[]{:S(2)}) collective-permute-start(f32[2,1,2,2,2850]{4,3,2,1,0:T(2,128)S(1)} %bitcast_add_fusion), channel_id=1, source_target_pairs={{0,256},{128,384},{256,0},{384,128},{1,257},{129,385},{257,1},{385... | collective-permute-start | bytes 273608 | tf_op jit(solution)/shard_map/ppermute | solution.py:37
  48.4 8.6 %collective-permute-done.5 = f32[2,1,2,2,2850]{4,3,2,1,0:T(2,128)S(1)} collective-permute-done((f32[2,1,2,2,2850]{4,3,2,1,0:T(2,128)S(1)}, f32[2,1,2,2,2850]{4,3,2,1,0:T(2,128)S(1)}, u32[]{:S(2)}, u32[]{:S(2)}) %collective-permute-start.5) | collective-permute-done | bytes 91232 | tf_op jit(solution)/shard_map/ppermute | solution.py:37
  57.0 0.1 add_subtract_fusion
  57.1 0.1 fusion.32
  57.2 0.5 copy-done.2
  57.7 0.1 multiply_add_fusion
  57.8 0.2 multiply_subtract_fusion
  58.1 0.5 fusion.10
  58.6 0.5 fusion.20
  59.0 1.9 %collective-permute-start.6 = (f32[8,2,2,2,76]{4,0,3,2,1:T(8,128)S(1)}, f32[8,2,2,2,76]{4,0,3,2,1:T(8,128)S(1)}, u32[]{:S(2)}, u32[]{:S(2)}) collective-permute-start(f32[8,2,2,2,76]{4,0,3,2,1:T(8,128)S(1)} %fusion.52), channel_id=1, source_target_pairs={{0,1},{1,2},{2,3},{3,4},{4,5},{5,6},{6,7},{7,8},{8,9},{9,10},{10,1... | collective-permute-start | bytes 58376 | tf_op jit(solution)/shard_map/ppermute | solution.py:24
  61.0 3.9 %collective-permute-start.7 = (f32[8,2,2,2,76]{4,0,3,2,1:T(8,128)S(1)}, f32[8,2,2,2,76]{4,0,3,2,1:T(8,128)S(1)}, u32[]{:S(2)}, u32[]{:S(2)}) collective-permute-start(f32[8,2,2,2,76]{4,0,3,2,1:T(8,128)S(1)} %fusion.52), channel_id=1, source_target_pairs={{1,0},{2,1},{3,2},{4,3},{5,4},{6,5},{7,6},{8,7},{9,8},{10,9},{11,1... | collective-permute-start | bytes 58376 | tf_op jit(solution)/shard_map/ppermute | solution.py:26
  64.9 7.9 %collective-permute-done.7 = f32[8,2,2,2,76]{4,0,3,2,1:T(8,128)S(1)} collective-permute-done((f32[8,2,2,2,76]{4,0,3,2,1:T(8,128)S(1)}, f32[8,2,2,2,76]{4,0,3,2,1:T(8,128)S(1)}, u32[]{:S(2)}, u32[]{:S(2)}) %collective-permute-start.7) | collective-permute-done | bytes 19488 | tf_op jit(solution)/shard_map/ppermute | solution.py:26
  72.8 0.1 fusion.47
  72.9 0.6 copy.17
  (17 shorter events, 0.1 us)
Async XLA Ops:
  1.5 1.3 %copy-start.3 = (f32[8,2,2,2,76]{4,3,2,1,0:T(2,128)S(1)}, f32[8,2,2,2,76]{4,3,2,1,0:T(2,128)}, u32[]{:S(2)}) copy-start(f32[8,2,2,2,76]{4,3,2,1,0:T(2,128)} %param.8) | copy-start | bytes 58372
  2.8 1.0 %copy-start = (bf16[8,2,1,2,2,2850]{5,4,3,2,1,0:T(2,128)(2,1)S(1)}, bf16[8,2,1,2,2,2850]{5,4,3,2,1,0:T(2,128)(2,1)}, u32[]{:S(2)}) copy-start(bf16[8,2,1,2,2,2850]{5,4,3,2,1,0:T(2,128)(2,1)} %param.7) | copy-start | bytes 1094404
  4.0 16.1 %copy-start.1 = (f32[2,1,2,2,2850]{4,3,2,1,0:T(2,128)S(1)}, f32[2,1,2,2,2850]{4,3,2,1,0:T(2,128)}, u32[]{:S(2)}) copy-start(f32[2,1,2,2,2850]{4,3,2,1,0:T(2,128)} %param.6) | copy-start | bytes 273604
  4.3 3.2 %collective-permute-start = (f32[2,1,2,2,2850]{4,3,2,1,0:T(2,128)S(1)}, f32[2,1,2,2,2850]{4,3,2,1,0:T(2,128)S(1)}, u32[]{:S(2)}, u32[]{:S(2)}) collective-permute-start(f32[2,1,2,2,2850]{4,3,2,1,0:T(2,128)S(1)} %bitcast.58), channel_id=1, source_target_pairs={{0,128},{128,0},{256,384},{384,256},{1,129},{129,1},{257,385},{385... | collective-permute-start | bytes 273608 | tf_op jit(solution)/shard_map/ppermute | solution.py:37
  7.5 12.6 %collective-permute-start.1 = (f32[2,1,2,2,2850]{4,3,2,1,0:T(2,128)S(1)}, f32[2,1,2,2,2850]{4,3,2,1,0:T(2,128)S(1)}, u32[]{:S(2)}, u32[]{:S(2)}) collective-permute-start(f32[2,1,2,2,2850]{4,3,2,1,0:T(2,128)S(1)} %bitcast_add_fusion.1), channel_id=1, source_target_pairs={{0,256},{128,384},{256,0},{384,128},{1,257},{129,385},{257,1},{385... | collective-permute-start | bytes 273608 | tf_op jit(solution)/shard_map/ppermute | solution.py:37
  21.2 0.7 copy-start.4
  21.2 20.5 %copy-start.5 = (s32[2]{0:T(128)S(1)}, s32[2]{0:T(128)}, u32[]{:S(2)}) copy-start(s32[2]{0:T(128)} %param.10) | copy-start | bytes 28
  22.0 9.7 %collective-permute-start.2 = (f32[8,2,2,2,77]{4,0,3,2,1:T(8,128)S(1)}, f32[8,2,2,2,77]{4,0,3,2,1:T(8,128)S(1)}, u32[]{:S(2)}, u32[]{:S(2)}) collective-permute-start(f32[8,2,2,2,77]{4,0,3,2,1:T(8,128)S(1)} %pad_maximum_fusion.8), channel_id=1, source_target_pairs={{0,1},{1,2},{2,3},{3,4},{4,5},{5,6},{6,7},{7,8},{8,9},{9,10},{10,1... | collective-permute-start | bytes 59144 | tf_op jit(solution)/shard_map/ppermute | solution.py:24
  29.7 11.8 %collective-permute-start.3 = (f32[8,2,2,2,77]{4,0,3,2,1:T(8,128)S(1)}, f32[8,2,2,2,77]{4,0,3,2,1:T(8,128)S(1)}, u32[]{:S(2)}, u32[]{:S(2)}) collective-permute-start(f32[8,2,2,2,77]{4,0,3,2,1:T(8,128)S(1)} %pad_maximum_fusion.8), channel_id=1, source_target_pairs={{1,0},{2,1},{3,2},{4,3},{5,4},{6,5},{7,6},{8,7},{9,8},{10,9},{11,1... | collective-permute-start | bytes 59144 | tf_op jit(solution)/shard_map/ppermute | solution.py:26
  43.2 3.2 %collective-permute-start.4 = (f32[2,1,2,2,2850]{4,3,2,1,0:T(2,128)S(1)}, f32[2,1,2,2,2850]{4,3,2,1,0:T(2,128)S(1)}, u32[]{:S(2)}, u32[]{:S(2)}) collective-permute-start(f32[2,1,2,2,2850]{4,3,2,1,0:T(2,128)S(1)} %bitcast.59), channel_id=1, source_target_pairs={{0,128},{128,0},{256,384},{384,256},{1,129},{129,1},{257,385},{385... | collective-permute-start | bytes 273608 | tf_op jit(solution)/shard_map/ppermute | solution.py:37
  46.4 10.6 %collective-permute-start.5 = (f32[2,1,2,2,2850]{4,3,2,1,0:T(2,128)S(1)}, f32[2,1,2,2,2850]{4,3,2,1,0:T(2,128)S(1)}, u32[]{:S(2)}, u32[]{:S(2)}) collective-permute-start(f32[2,1,2,2,2850]{4,3,2,1,0:T(2,128)S(1)} %bitcast_add_fusion), channel_id=1, source_target_pairs={{0,256},{128,384},{256,0},{384,128},{1,257},{129,385},{257,1},{385... | collective-permute-start | bytes 273608 | tf_op jit(solution)/shard_map/ppermute | solution.py:37
  57.1 0.6 copy-start.2
  59.0 5.9 %collective-permute-start.6 = (f32[8,2,2,2,76]{4,0,3,2,1:T(8,128)S(1)}, f32[8,2,2,2,76]{4,0,3,2,1:T(8,128)S(1)}, u32[]{:S(2)}, u32[]{:S(2)}) collective-permute-start(f32[8,2,2,2,76]{4,0,3,2,1:T(8,128)S(1)} %fusion.52), channel_id=1, source_target_pairs={{0,1},{1,2},{2,3},{3,4},{4,5},{5,6},{6,7},{7,8},{8,9},{9,10},{10,1... | collective-permute-start | bytes 58376 | tf_op jit(solution)/shard_map/ppermute | solution.py:24
  61.0 11.8 %collective-permute-start.7 = (f32[8,2,2,2,76]{4,0,3,2,1:T(8,128)S(1)}, f32[8,2,2,2,76]{4,0,3,2,1:T(8,128)S(1)}, u32[]{:S(2)}, u32[]{:S(2)}) collective-permute-start(f32[8,2,2,2,76]{4,0,3,2,1:T(8,128)S(1)} %fusion.52), channel_id=1, source_target_pairs={{1,0},{2,1},{3,2},{4,3},{5,4},{6,5},{7,6},{8,7},{9,8},{10,9},{11,1... | collective-permute-start | bytes 58376 | tf_op jit(solution)/shard_map/ppermute | solution.py:26

commit v11 on v10

--- a/solution.py
+++ b/solution.py
@@ -60,10 +60,10 @@
     return (jnp.stack([outer_re, outer_im], axis=-2), (left_re, left_im, right_re, right_im))
 
 
-def solve(gains, model, corrupted_model, parts, residual, left_hot, right_hot):
+def solve(gains, model, corrupted_model, parts, visibilities, total, left_hot, right_hot):
     model = model.astype(jnp.float32)
     left_re, left_im, right_re, right_im = parts
-    target = residual + corrupted_model
+    target = visibilities + (corrupted_model - total)
     target_re, target_im = (target[..., 0, :], target[..., 1, :])
     model_re, model_im = (model[..., 0, :], model[..., 1, :])
     weighted_re = target_re * model_re + target_im * model_im
@@ -108,13 +108,13 @@
     current = gains
     residual = visibilities
     corrupt_all = jax.vmap(corrupt, in_axes=(0, 0, None, None))
-    solve_all = jax.vmap(solve, in_axes=(0, 0, 0, 0, None, None, None))
+    solve_all = jax.vmap(solve, in_axes=(0, 0, 0, 0, None, None, None, None))
     for sweep in range(ITERS):
         corrupted_model, parts = corrupt_all(current, model, left_hot, right_hot)
         partial_total = jnp.sum(corrupted_model, axis=0)
         total = sum_over_dir(partial_total)
         residual = visibilities - total
-        stepped = solve_all(current, model, corrupted_model, parts, residual, left_hot, right_hot)
+        stepped = solve_all(current, model, corrupted_model, parts, visibilities, total, left_hot, right_hot)
         if padded_weights is None:
             column = jnp.broadcast_to(weights[None, :, None, None, None], stepped.shape[:-1] + (1,))
             padded = extended(jnp.concatenate([stepped, column], axis=-1), "chan", 1, SPAN)

time: 74 us -> 74.2 us (level)
    unnamed x13 -> x11, local copies, waits for them, and re-layouts: 1.89 us -> 1.35 us
where the time goes in v11:
time: 74.2 us; the launch traced here: 73.7 us
  waiting for transfers between devices  36.8 us (50%)
  starting transfers between devices  26 us (35%)
  matrix products  4.41 us (6%)
  other arithmetic  3.29 us (4%)
  local copies, waits for them, and re-layouts  2.29 us (3%)
  between operations  0.96 us (1%)
    ppermute x4, waiting for transfers between devices, sum_over_dir(): lax.ppermute(total, 'dir', [(i, i ^ mask) for i in range(count)])  19 us
    ppermute x2, waiting for transfers between devices, extended(): lax.ppermute(head, axis, [(i + 1, i) for i in range(ends)])  17.8 us
    ppermute x4, starting transfers between devices, sum_over_dir(): lax.ppermute(total, 'dir', [(i, i ^ mask) for i in range(count)])  10.5 us
    ppermute x2, starting transfers between devices, extended(): lax.ppermute(tail, axis, [(i, i + 1) for i in range(ends)])  9.65 us
    ppermute x2, starting transfers between devices, extended(): lax.ppermute(head, axis, [(i + 1, i) for i in range(ends)])  5.84 us
    dot_general x2, matrix products, corrupt(): jnp.matmul(gains, right_hot, precision=table_precision)[:, None]  1.69 us
  transfers between devices with their start and end apart: 8, of which 6 were waited for; matrix products, arithmetic and copies ran while one was open for 0% of the time, Pallas kernels for 0%

profile of v11, /device:TPU:254, one launch (start us, length us, event | category | flops | bytes accessed | tf_op | source)
XLA Modules:
  0.0 73.7 jit_solution(15564899336138259047)
XLA Ops:
  0.6 0.9 %slice_reduce_fusion.1 = (s32[2850]{0:T(1024)S(1)}, s32[2850]{0:T(1024)S(1)}) fusion(s32[2,2850]{1,0:T(2,128)} %param.11), kind=kLoop, calls=%fused_computation.113 | loop fusion | bytes 45600 | tf_op jit(solution)/shard_map/slice | solution.py:44
  1.5 1.2 %convolution_bitcast_fusion.2 = f32[8,2,1,2,2,2850]{5,0,4,3,1,2:T(8,128)S(1)} fusion(s32[2850]{0:T(1024)S(1)} %get-tuple-element.11, f32[8,2,2,2,76]{4,3,2,1,0:T(2,128)} %param.8), kind=kOutput, calls=%fused_computation.2 | convolution fusion | flops 83391000 | bytes 760456 | tf_op jit(solution)/shard_map/vmap()/dot_general | solution.py:52
  2.8 0.4 convolution_bitcast_fusion.3
  3.2 0.5 copy-done.1
  3.8 0.1 copy_convert_fusion
  3.8 0.1 multiply_add_fusion.9
  4.0 0.1 multiply_subtract_fusion.8
  4.1 0.2 fusion.33
  4.3 1.9 %collective-permute-start = (f32[2,1,2,2,2850]{4,3,2,0,1:T(2,128)S(1)}, f32[2,1,2,2,2850]{4,3,2,0,1:T(2,128)S(1)}, u32[]{:S(2)}, u32[]{:S(2)}) collective-permute-start(f32[2,1,2,2,2850]{4,3,2,0,1:T(2,128)S(1)} %bitcast.61), channel_id=1, source_target_pairs={{0,128},{128,0},{256,384},{384,256},{1,129},{129,1},{257,385},{385... | collective-permute-start | bytes 273608 | tf_op jit(solution)/shard_map/ppermute | solution.py:37
  6.2 1.3 %collective-permute-done = f32[2,1,2,2,2850]{4,3,2,0,1:T(2,128)S(1)} collective-permute-done((f32[2,1,2,2,2850]{4,3,2,0,1:T(2,128)S(1)}, f32[2,1,2,2,2850]{4,3,2,0,1:T(2,128)S(1)}, u32[]{:S(2)}, u32[]{:S(2)}) %collective-permute-start) | collective-permute-done | bytes 91232 | tf_op jit(solution)/shard_map/ppermute | solution.py:37
  7.5 0.1 bitcast_add_fusion.1
  7.5 4.7 %collective-permute-start.1 = (f32[2,1,2,2,2850]{4,3,2,0,1:T(2,128)S(1)}, f32[2,1,2,2,2850]{4,3,2,0,1:T(2,128)S(1)}, u32[]{:S(2)}, u32[]{:S(2)}) collective-permute-start(f32[2,1,2,2,2850]{4,3,2,0,1:T(2,128)S(1)} %bitcast_add_fusion.1), channel_id=1, source_target_pairs={{0,256},{128,384},{256,0},{384,128},{1,257},{129,385},{257,1},{385... | collective-permute-start | bytes 273608 | tf_op jit(solution)/shard_map/ppermute | solution.py:37
  12.2 7.9 %collective-permute-done.1 = f32[2,1,2,2,2850]{4,3,2,0,1:T(2,128)S(1)} collective-permute-done((f32[2,1,2,2,2850]{4,3,2,0,1:T(2,128)S(1)}, f32[2,1,2,2,2850]{4,3,2,0,1:T(2,128)S(1)}, u32[]{:S(2)}, u32[]{:S(2)}) %collective-permute-start.1) | collective-permute-done | bytes 91232 | tf_op jit(solution)/shard_map/ppermute | solution.py:37
  20.1 0.1 add_bitcast_fusion
  20.2 0.1 subtract_add_fusion.1
  20.3 0.2 multiply_add_fusion.5
  20.5 0.2 multiply_subtract_fusion.6
  20.7 0.5 fusion
  21.2 0.5 fusion.21
  21.7 0.1 copy-done.3
  21.9 0.1 broadcast_in_dim.12
  21.9 0.1 pad_maximum_fusion.8
  22.0 7.7 %collective-permute-start.2 = (f32[8,2,2,2,77]{4,0,3,2,1:T(8,128)S(1)}, f32[8,2,2,2,77]{4,0,3,2,1:T(8,128)S(1)}, u32[]{:S(2)}, u32[]{:S(2)}) collective-permute-start(f32[8,2,2,2,77]{4,0,3,2,1:T(8,128)S(1)} %pad_maximum_fusion.8), channel_id=1, source_target_pairs={{0,1},{1,2},{2,3},{3,4},{4,5},{5,6},{6,7},{7,8},{8,9},{9,10},{10,1... | collective-permute-start | bytes 59144 | tf_op jit(solution)/shard_map/ppermute | solution.py:24
  29.7 1.9 %collective-permute-start.3 = (f32[8,2,2,2,77]{4,0,3,2,1:T(8,128)S(1)}, f32[8,2,2,2,77]{4,0,3,2,1:T(8,128)S(1)}, u32[]{:S(2)}, u32[]{:S(2)}) collective-permute-start(f32[8,2,2,2,77]{4,0,3,2,1:T(8,128)S(1)} %pad_maximum_fusion.8), channel_id=1, source_target_pairs={{1,0},{2,1},{3,2},{4,3},{5,4},{6,5},{7,6},{8,7},{9,8},{10,9},{11,1... | collective-permute-start | bytes 59144 | tf_op jit(solution)/shard_map/ppermute | solution.py:26
  31.7 9.9 %collective-permute-done.3 = f32[8,2,2,2,77]{4,0,3,2,1:T(8,128)S(1)} collective-permute-done((f32[8,2,2,2,77]{4,0,3,2,1:T(8,128)S(1)}, f32[8,2,2,2,77]{4,0,3,2,1:T(8,128)S(1)}, u32[]{:S(2)}, u32[]{:S(2)}) %collective-permute-start.3) | collective-permute-done | bytes 19744 | tf_op jit(solution)/shard_map/ppermute | solution.py:26
  41.6 0.2 maximum_reduce_fusion.1
  41.8 0.1 fusion.52
  41.9 0.4 convolution_bitcast_fusion
  42.3 0.4 convolution_bitcast_fusion.1
  42.8 0.1 multiply_add_fusion.3
  42.9 0.1 multiply_subtract_fusion.3
  43.0 0.2 fusion.32
  43.2 1.9 %collective-permute-start.4 = (f32[2,1,2,2,2850]{4,3,2,1,0:T(2,128)S(1)}, f32[2,1,2,2,2850]{4,3,2,1,0:T(2,128)S(1)}, u32[]{:S(2)}, u32[]{:S(2)}) collective-permute-start(f32[2,1,2,2,2850]{4,3,2,1,0:T(2,128)S(1)} %bitcast.62), channel_id=1, source_target_pairs={{0,128},{128,0},{256,384},{384,256},{1,129},{129,1},{257,385},{385... | collective-permute-start | bytes 273608 | tf_op jit(solution)/shard_map/ppermute | solution.py:37
  45.2 1.3 %collective-permute-done.4 = f32[2,1,2,2,2850]{4,3,2,1,0:T(2,128)S(1)} collective-permute-done((f32[2,1,2,2,2850]{4,3,2,1,0:T(2,128)S(1)}, f32[2,1,2,2,2850]{4,3,2,1,0:T(2,128)S(1)}, u32[]{:S(2)}, u32[]{:S(2)}) %collective-permute-start.4) | collective-permute-done | bytes 91232 | tf_op jit(solution)/shard_map/ppermute | solution.py:37
  46.4 0.1 bitcast_add_fusion
  46.5 1.9 %collective-permute-start.5 = (f32[2,1,2,2,2850]{4,3,2,1,0:T(2,128)S(1)}, f32[2,1,2,2,2850]{4,3,2,1,0:T(2,128)S(1)}, u32[]{:S(2)}, u32[]{:S(2)}) collective-permute-start(f32[2,1,2,2,2850]{4,3,2,1,0:T(2,128)S(1)} %bitcast_add_fusion), channel_id=1, source_target_pairs={{0,256},{128,384},{256,0},{384,128},{1,257},{129,385},{257,1},{385... | collective-permute-start | bytes 273608 | tf_op jit(solution)/shard_map/ppermute | solution.py:37
  48.4 8.6 %collective-permute-done.5 = f32[2,1,2,2,2850]{4,3,2,1,0:T(2,128)S(1)} collective-permute-done((f32[2,1,2,2,2850]{4,3,2,1,0:T(2,128)S(1)}, f32[2,1,2,2,2850]{4,3,2,1,0:T(2,128)S(1)}, u32[]{:S(2)}, u32[]{:S(2)}) %collective-permute-start.5) | collective-permute-done | bytes 91232 | tf_op jit(solution)/shard_map/ppermute | solution.py:37
  57.0 0.7 add_subtract_fusion
  57.8 0.1 subtract_add_fusion
  57.9 0.1 multiply_add_fusion
  58.0 0.2 multiply_subtract_fusion
  58.3 0.5 fusion.10
  58.7 0.5 fusion.20
  59.2 1.9 %collective-permute-start.6 = (f32[8,2,2,2,76]{4,0,3,2,1:T(8,128)S(1)}, f32[8,2,2,2,76]{4,0,3,2,1:T(8,128)S(1)}, u32[]{:S(2)}, u32[]{:S(2)}) collective-permute-start(f32[8,2,2,2,76]{4,0,3,2,1:T(8,128)S(1)} %fusion.50), channel_id=1, source_target_pairs={{0,1},{1,2},{2,3},{3,4},{4,5},{5,6},{6,7},{7,8},{8,9},{9,10},{10,1... | collective-permute-start | bytes 58376 | tf_op jit(solution)/shard_map/ppermute | solution.py:24
  61.2 3.9 %collective-permute-start.7 = (f32[8,2,2,2,76]{4,0,3,2,1:T(8,128)S(1)}, f32[8,2,2,2,76]{4,0,3,2,1:T(8,128)S(1)}, u32[]{:S(2)}, u32[]{:S(2)}) collective-permute-start(f32[8,2,2,2,76]{4,0,3,2,1:T(8,128)S(1)} %fusion.50), channel_id=1, source_target_pairs={{1,0},{2,1},{3,2},{4,3},{5,4},{6,5},{7,6},{8,7},{9,8},{10,9},{11,1... | collective-permute-start | bytes 58376 | tf_op jit(solution)/shard_map/ppermute | solution.py:26
  65.1 7.9 %collective-permute-done.7 = f32[8,2,2,2,76]{4,0,3,2,1:T(8,128)S(1)} collective-permute-done((f32[8,2,2,2,76]{4,0,3,2,1:T(8,128)S(1)}, f32[8,2,2,2,76]{4,0,3,2,1:T(8,128)S(1)}, u32[]{:S(2)}, u32[]{:S(2)}) %collective-permute-start.7) | collective-permute-done | bytes 19488 | tf_op jit(solution)/shard_map/ppermute | solution.py:26
  73.0 0.1 fusion.45
  73.1 0.6 copy.17
  (15 shorter events, 0.1 us)
Async XLA Ops:
  1.5 1.3 %copy-start.2 = (f32[8,2,2,2,76]{4,3,2,1,0:T(2,128)S(1)}, f32[8,2,2,2,76]{4,3,2,1,0:T(2,128)}, u32[]{:S(2)}) copy-start(f32[8,2,2,2,76]{4,3,2,1,0:T(2,128)} %param.8) | copy-start | bytes 58372
  2.8 1.0 %copy-start.1 = (bf16[8,2,1,2,2,2850]{5,4,3,2,1,0:T(2,128)(2,1)S(1)}, bf16[8,2,1,2,2,2850]{5,4,3,2,1,0:T(2,128)(2,1)}, u32[]{:S(2)}) copy-start(bf16[8,2,1,2,2,2850]{5,4,3,2,1,0:T(2,128)(2,1)} %param.7) | copy-start | bytes 1094404
  4.0 16.1 %copy-start = (f32[2,1,2,2,2850]{4,3,2,1,0:T(2,128)S(1)}, f32[2,1,2,2,2850]{4,3,2,1,0:T(2,128)}, u32[]{:S(2)}) copy-start(f32[2,1,2,2,2850]{4,3,2,1,0:T(2,128)} %param.6) | copy-start | bytes 273604
  4.3 3.2 %collective-permute-start = (f32[2,1,2,2,2850]{4,3,2,0,1:T(2,128)S(1)}, f32[2,1,2,2,2850]{4,3,2,0,1:T(2,128)S(1)}, u32[]{:S(2)}, u32[]{:S(2)}) collective-permute-start(f32[2,1,2,2,2850]{4,3,2,0,1:T(2,128)S(1)} %bitcast.61), channel_id=1, source_target_pairs={{0,128},{128,0},{256,384},{384,256},{1,129},{129,1},{257,385},{385... | collective-permute-start | bytes 273608 | tf_op jit(solution)/shard_map/ppermute | solution.py:37
  7.5 12.6 %collective-permute-start.1 = (f32[2,1,2,2,2850]{4,3,2,0,1:T(2,128)S(1)}, f32[2,1,2,2,2850]{4,3,2,0,1:T(2,128)S(1)}, u32[]{:S(2)}, u32[]{:S(2)}) collective-permute-start(f32[2,1,2,2,2850]{4,3,2,0,1:T(2,128)S(1)} %bitcast_add_fusion.1), channel_id=1, source_target_pairs={{0,256},{128,384},{256,0},{384,128},{1,257},{129,385},{257,1},{385... | collective-permute-start | bytes 273608 | tf_op jit(solution)/shard_map/ppermute | solution.py:37
  21.2 0.7 copy-start.3
  21.2 20.5 %copy-start.4 = (s32[2]{0:T(128)S(1)}, s32[2]{0:T(128)}, u32[]{:S(2)}) copy-start(s32[2]{0:T(128)} %param.10) | copy-start | bytes 28
  22.0 9.7 %collective-permute-start.2 = (f32[8,2,2,2,77]{4,0,3,2,1:T(8,128)S(1)}, f32[8,2,2,2,77]{4,0,3,2,1:T(8,128)S(1)}, u32[]{:S(2)}, u32[]{:S(2)}) collective-permute-start(f32[8,2,2,2,77]{4,0,3,2,1:T(8,128)S(1)} %pad_maximum_fusion.8), channel_id=1, source_target_pairs={{0,1},{1,2},{2,3},{3,4},{4,5},{5,6},{6,7},{7,8},{8,9},{9,10},{10,1... | collective-permute-start | bytes 59144 | tf_op jit(solution)/shard_map/ppermute | solution.py:24
  29.7 11.8 %collective-permute-start.3 = (f32[8,2,2,2,77]{4,0,3,2,1:T(8,128)S(1)}, f32[8,2,2,2,77]{4,0,3,2,1:T(8,128)S(1)}, u32[]{:S(2)}, u32[]{:S(2)}) collective-permute-start(f32[8,2,2,2,77]{4,0,3,2,1:T(8,128)S(1)} %pad_maximum_fusion.8), channel_id=1, source_target_pairs={{1,0},{2,1},{3,2},{4,3},{5,4},{6,5},{7,6},{8,7},{9,8},{10,9},{11,1... | collective-permute-start | bytes 59144 | tf_op jit(solution)/shard_map/ppermute | solution.py:26
  43.2 3.2 %collective-permute-start.4 = (f32[2,1,2,2,2850]{4,3,2,1,0:T(2,128)S(1)}, f32[2,1,2,2,2850]{4,3,2,1,0:T(2,128)S(1)}, u32[]{:S(2)}, u32[]{:S(2)}) collective-permute-start(f32[2,1,2,2,2850]{4,3,2,1,0:T(2,128)S(1)} %bitcast.62), channel_id=1, source_target_pairs={{0,128},{128,0},{256,384},{384,256},{1,129},{129,1},{257,385},{385... | collective-permute-start | bytes 273608 | tf_op jit(solution)/shard_map/ppermute | solution.py:37
  46.5 10.6 %collective-permute-start.5 = (f32[2,1,2,2,2850]{4,3,2,1,0:T(2,128)S(1)}, f32[2,1,2,2,2850]{4,3,2,1,0:T(2,128)S(1)}, u32[]{:S(2)}, u32[]{:S(2)}) collective-permute-start(f32[2,1,2,2,2850]{4,3,2,1,0:T(2,128)S(1)} %bitcast_add_fusion), channel_id=1, source_target_pairs={{0,256},{128,384},{256,0},{384,128},{1,257},{129,385},{257,1},{385... | collective-permute-start | bytes 273608 | tf_op jit(solution)/shard_map/ppermute | solution.py:37
  59.2 5.9 %collective-permute-start.6 = (f32[8,2,2,2,76]{4,0,3,2,1:T(8,128)S(1)}, f32[8,2,2,2,76]{4,0,3,2,1:T(8,128)S(1)}, u32[]{:S(2)}, u32[]{:S(2)}) collective-permute-start(f32[8,2,2,2,76]{4,0,3,2,1:T(8,128)S(1)} %fusion.50), channel_id=1, source_target_pairs={{0,1},{1,2},{2,3},{3,4},{4,5},{5,6},{6,7},{7,8},{8,9},{9,10},{10,1... | collective-permute-start | bytes 58376 | tf_op jit(solution)/shard_map/ppermute | solution.py:24
  61.2 11.8 %collective-permute-start.7 = (f32[8,2,2,2,76]{4,0,3,2,1:T(8,128)S(1)}, f32[8,2,2,2,76]{4,0,3,2,1:T(8,128)S(1)}, u32[]{:S(2)}, u32[]{:S(2)}) collective-permute-start(f32[8,2,2,2,76]{4,0,3,2,1:T(8,128)S(1)} %fusion.50), channel_id=1, source_target_pairs={{1,0},{2,1},{3,2},{4,3},{5,4},{6,5},{7,6},{8,7},{9,8},{10,9},{11,1... | collective-permute-start | bytes 58376 | tf_op jit(solution)/shard_map/ppermute | solution.py:26

commit v12 on v10

--- a/solution.py
+++ b/solution.py
@@ -10,7 +10,7 @@
 
 step_size = 0.6
 epsilon = 1e-06
-table_precision = lax.Precision.HIGH
+table_precision = lax.Precision.HIGHEST
 
 
 def extended(cells, axis, dim, width):

time: 74 us -> 75.5 us (1.020)
  matrix products: 4.39 us -> 6.07 us
where the time goes in v12:
time: 75.5 us; the launch traced here: 75 us
  waiting for transfers between devices  36.8 us (49%)
  starting transfers between devices  26 us (34%)
  matrix products  6.07 us (8%)
  local copies, waits for them, and re-layouts  2.58 us (3%)
  other arithmetic  2.58 us (3%)
  between operations  0.96 us (1%)
    ppermute x4, waiting for transfers between devices, sum_over_dir(): lax.ppermute(total, 'dir', [(i, i ^ mask) for i in range(count)])  19 us
    ppermute x2, waiting for transfers between devices, extended(): lax.ppermute(head, axis, [(i + 1, i) for i in range(ends)])  17.8 us
    ppermute x4, starting transfers between devices, sum_over_dir(): lax.ppermute(total, 'dir', [(i, i ^ mask) for i in range(count)])  10.5 us
    ppermute x2, starting transfers between devices, extended(): lax.ppermute(tail, axis, [(i, i + 1) for i in range(ends)])  9.66 us
    ppermute x2, starting transfers between devices, extended(): lax.ppermute(head, axis, [(i + 1, i) for i in range(ends)])  5.84 us
    dot_general x2, matrix products, corrupt(): jnp.matmul(gains, right_hot, precision=table_precision)[:, None]  1.89 us
    unnamed x13, local copies, waits for them, and re-layouts  1.64 us
    dot_general x2, matrix products, solve(): jnp.matmul(right_terms, right_hot.T, precision=table_precision)  1.55 us
  transfers between devices with their start and end apart: 8, of which 6 were waited for; matrix products, arithmetic and copies ran while one was open for 0% of the time, Pallas kernels for 0%

profile of v12, /device:TPU:254, one launch (start us, length us, event | category | flops | bytes accessed | tf_op | source)
XLA Modules:
  0.0 75.0 jit_solution(6053887993073468209)
XLA Ops:
  0.6 0.9 %slice_reduce_fusion.1 = (s32[2850]{0:T(1024)S(1)}, s32[2850]{0:T(1024)S(1)}) fusion(s32[2,2850]{1,0:T(2,128)} %param.11), kind=kLoop, calls=%fused_computation.112 | loop fusion | bytes 45600 | tf_op jit(solution)/shard_map/slice | solution.py:44
  1.5 1.3 %convolution_bitcast_fusion.2 = f32[8,2,1,2,2,2850]{5,0,4,3,1,2:T(8,128)S(1)} fusion(s32[2850]{0:T(1024)S(1)} %get-tuple-element.11, f32[8,2,2,2,76]{4,3,2,1,0:T(2,128)} %param.8), kind=kOutput, calls=%fused_computation.2 | convolution fusion | flops 166565408 | bytes 760456 | tf_op jit(solution)/shard_map/vmap()/dot_general | solution.py:52
  2.9 0.5 convolution_bitcast_fusion.3
  3.4 0.4 copy-done
  3.9 0.1 copy_convert_fusion
  3.9 0.1 multiply_add_fusion.9
  4.1 0.1 multiply_subtract_fusion.8
  4.2 0.2 fusion.35
  4.4 1.9 %collective-permute-start = (f32[2,1,2,2,2850]{4,3,2,1,0:T(2,128)S(1)}, f32[2,1,2,2,2850]{4,3,2,1,0:T(2,128)S(1)}, u32[]{:S(2)}, u32[]{:S(2)}) collective-permute-start(f32[2,1,2,2,2850]{4,3,2,1,0:T(2,128)S(1)} %bitcast.58), channel_id=1, source_target_pairs={{0,128},{128,0},{256,384},{384,256},{1,129},{129,1},{257,385},{385... | collective-permute-start | bytes 273608 | tf_op jit(solution)/shard_map/ppermute | solution.py:37
  6.3 1.3 %collective-permute-done = f32[2,1,2,2,2850]{4,3,2,1,0:T(2,128)S(1)} collective-permute-done((f32[2,1,2,2,2850]{4,3,2,1,0:T(2,128)S(1)}, f32[2,1,2,2,2850]{4,3,2,1,0:T(2,128)S(1)}, u32[]{:S(2)}, u32[]{:S(2)}) %collective-permute-start) | collective-permute-done | bytes 91232 | tf_op jit(solution)/shard_map/ppermute | solution.py:37
  7.6 0.1 bitcast_add_fusion.1
  7.6 4.7 %collective-permute-start.1 = (f32[2,1,2,2,2850]{4,3,2,1,0:T(2,128)S(1)}, f32[2,1,2,2,2850]{4,3,2,1,0:T(2,128)S(1)}, u32[]{:S(2)}, u32[]{:S(2)}) collective-permute-start(f32[2,1,2,2,2850]{4,3,2,1,0:T(2,128)S(1)} %bitcast_add_fusion.1), channel_id=1, source_target_pairs={{0,256},{128,384},{256,0},{384,128},{1,257},{129,385},{257,1},{385... | collective-permute-start | bytes 273608 | tf_op jit(solution)/shard_map/ppermute | solution.py:37
  12.3 7.9 %collective-permute-done.1 = f32[2,1,2,2,2850]{4,3,2,1,0:T(2,128)S(1)} collective-permute-done((f32[2,1,2,2,2850]{4,3,2,1,0:T(2,128)S(1)}, f32[2,1,2,2,2850]{4,3,2,1,0:T(2,128)S(1)}, u32[]{:S(2)}, u32[]{:S(2)}) %collective-permute-start.1) | collective-permute-done | bytes 91232 | tf_op jit(solution)/shard_map/ppermute | solution.py:37
  20.2 0.1 subtract_bitcast_fusion
  20.3 0.1 fusion.34
  20.4 0.2 multiply_add_fusion.5
  20.6 0.2 multiply_subtract_fusion.6
  20.8 0.8 %fusion = f32[8,2,2,3,76]{4,0,3,2,1:T(8,128)S(1)} fusion(f32[8,2,1,2,1,2850]{5,0,4,3,1,2:T(8,128)S(1)} %get-tuple-element.44, f32[8,2,1,2,1,2850]{5,0,4,3,1,2:T(8,128)S(1)} %get-tuple-element.35, f32[8,2,1,2,1,2850]{5,0,4,3,1,2:T(8,128)S(1)} %get-tuple-element.34, s32[2850]{0:T(1024)S(1)} %get-tuple-element.10), kind=kOutput, calls=%fused_computation.5 | convolution fusion | flops 250287008 | bytes 1134984 | tf_op jit(solution)/shard_map/vmap()/dot_general | solution.py:80
  21.6 0.8 %fusion.21 = f32[8,2,2,3,76]{4,0,3,2,1:T(8,128)S(1)} fusion(f32[8,2,2,3,76]{4,0,3,2,1:T(8,128)S(1)} %fusion, f32[8,2,1,2,1,2850]{5,0,4,3,1,2:T(8,128)S(1)} %get-tuple-element.36, f32[8,2,1,2,1,2850]{5,0,4,3,1,2:T(8,128)S(1)} %get-tuple-element.43, f32[8,2,1,2,1,2850]{5,0,4,3,1,2:T(8,128)S(1)} %get-tuple-element.24, s32[2850]{0:T(1024)S(1)} %get-tuple-element.11), kind=kOutput, calls=%fused_computation.29 | convolution fusion | flops 250294304 | bytes 1164168 | tf_op jit(solution)/shard_map/vmap()/dot_general | solution.py:80
  22.4 0.1 broadcast_in_dim.12
  22.5 0.1 pad_maximum_fusion.8
  22.6 7.7 %collective-permute-start.2 = (f32[8,2,2,2,77]{4,0,3,2,1:T(8,128)S(1)}, f32[8,2,2,2,77]{4,0,3,2,1:T(8,128)S(1)}, u32[]{:S(2)}, u32[]{:S(2)}) collective-permute-start(f32[8,2,2,2,77]{4,0,3,2,1:T(8,128)S(1)} %pad_maximum_fusion.8), channel_id=1, source_target_pairs={{0,1},{1,2},{2,3},{3,4},{4,5},{5,6},{6,7},{7,8},{8,9},{9,10},{10,1... | collective-permute-start | bytes 59144 | tf_op jit(solution)/shard_map/ppermute | solution.py:24
  30.3 1.9 %collective-permute-start.3 = (f32[8,2,2,2,77]{4,0,3,2,1:T(8,128)S(1)}, f32[8,2,2,2,77]{4,0,3,2,1:T(8,128)S(1)}, u32[]{:S(2)}, u32[]{:S(2)}) collective-permute-start(f32[8,2,2,2,77]{4,0,3,2,1:T(8,128)S(1)} %pad_maximum_fusion.8), channel_id=1, source_target_pairs={{1,0},{2,1},{3,2},{4,3},{5,4},{6,5},{7,6},{8,7},{9,8},{10,9},{11,1... | collective-permute-start | bytes 59144 | tf_op jit(solution)/shard_map/ppermute | solution.py:26
  32.3 9.9 %collective-permute-done.3 = f32[8,2,2,2,77]{4,0,3,2,1:T(8,128)S(1)} collective-permute-done((f32[8,2,2,2,77]{4,0,3,2,1:T(8,128)S(1)}, f32[8,2,2,2,77]{4,0,3,2,1:T(8,128)S(1)}, u32[]{:S(2)}, u32[]{:S(2)}) %collective-permute-start.3) | collective-permute-done | bytes 19744 | tf_op jit(solution)/shard_map/ppermute | solution.py:26
  42.2 0.2 maximum_reduce_fusion.1
  42.4 0.1 fusion.54
  42.5 0.5 convolution_bitcast_fusion
  43.0 0.5 convolution_bitcast_fusion.1
  43.6 0.1 multiply_add_fusion.3
  43.7 0.1 multiply_subtract_fusion.3
  43.8 0.2 fusion.33
  44.0 1.9 %collective-permute-start.4 = (f32[2,1,2,2,2850]{4,3,2,1,0:T(2,128)S(1)}, f32[2,1,2,2,2850]{4,3,2,1,0:T(2,128)S(1)}, u32[]{:S(2)}, u32[]{:S(2)}) collective-permute-start(f32[2,1,2,2,2850]{4,3,2,1,0:T(2,128)S(1)} %bitcast.59), channel_id=1, source_target_pairs={{0,128},{128,0},{256,384},{384,256},{1,129},{129,1},{257,385},{385... | collective-permute-start | bytes 273608 | tf_op jit(solution)/shard_map/ppermute | solution.py:37
  46.0 1.3 %collective-permute-done.4 = f32[2,1,2,2,2850]{4,3,2,1,0:T(2,128)S(1)} collective-permute-done((f32[2,1,2,2,2850]{4,3,2,1,0:T(2,128)S(1)}, f32[2,1,2,2,2850]{4,3,2,1,0:T(2,128)S(1)}, u32[]{:S(2)}, u32[]{:S(2)}) %collective-permute-start.4) | collective-permute-done | bytes 91232 | tf_op jit(solution)/shard_map/ppermute | solution.py:37
  47.2 0.1 bitcast_add_fusion
  47.3 1.9 %collective-permute-start.5 = (f32[2,1,2,2,2850]{4,3,2,1,0:T(2,128)S(1)}, f32[2,1,2,2,2850]{4,3,2,1,0:T(2,128)S(1)}, u32[]{:S(2)}, u32[]{:S(2)}) collective-permute-start(f32[2,1,2,2,2850]{4,3,2,1,0:T(2,128)S(1)} %bitcast_add_fusion), channel_id=1, source_target_pairs={{0,256},{128,384},{256,0},{384,128},{1,257},{129,385},{257,1},{385... | collective-permute-start | bytes 273608 | tf_op jit(solution)/shard_map/ppermute | solution.py:37
  49.2 8.6 %collective-permute-done.5 = f32[2,1,2,2,2850]{4,3,2,1,0:T(2,128)S(1)} collective-permute-done((f32[2,1,2,2,2850]{4,3,2,1,0:T(2,128)S(1)}, f32[2,1,2,2,2850]{4,3,2,1,0:T(2,128)S(1)}, u32[]{:S(2)}, u32[]{:S(2)}) %collective-permute-start.5) | collective-permute-done | bytes 91232 | tf_op jit(solution)/shard_map/ppermute | solution.py:37
  57.8 0.1 add_subtract_fusion
  57.9 0.1 fusion.32
  58.0 0.5 copy-done.2
  58.5 0.1 multiply_add_fusion
  58.7 0.2 multiply_subtract_fusion
  58.9 0.8 %fusion.10 = f32[8,2,2,3,76]{4,0,3,2,1:T(8,128)S(1)} fusion(f32[8,2,1,2,1,2850]{5,0,4,3,1,2:T(8,128)S(1)} %get-tuple-element.42, f32[8,2,1,2,1,2850]{5,0,4,3,1,2:T(8,128)S(1)} %get-tuple-element.40, f32[8,2,1,2,1,2850]{5,0,4,3,1,2:T(8,128)S(1)} %get-tuple-element.41, s32[2850]{0:T(1024)S(1)} %get-tuple-element.10), kind=kOutput, calls=%fused_computation.17 | convolution fusion | flops 250287008 | bytes 1134984 | tf_op jit(solution)/shard_map/vmap()/dot_general | solution.py:80
  59.7 0.8 %fusion.20 = f32[8,2,2,3,76]{4,0,3,2,1:T(8,128)S(1)} fusion(f32[8,2,2,3,76]{4,0,3,2,1:T(8,128)S(1)} %fusion.10, f32[8,2,1,2,1,2850]{5,0,4,3,1,2:T(8,128)S(1)} %get-tuple-element.39, f32[8,2,1,2,1,2850]{5,0,4,3,1,2:T(8,128)S(1)} %get-tuple-element.38, f32[8,2,1,2,1,2850]{5,0,4,3,1,2:T(8,128)S(1)} %get-tuple-element.12, s32[2850]{0:T(1024)S(1)} %get-tuple-element.11), kind=kOutput, calls=%fused_computation.28 | convolution fusion | flops 250294304 | bytes 1164168 | tf_op jit(solution)/shard_map/vmap()/dot_general | solution.py:80
  60.5 1.9 %collective-permute-start.6 = (f32[8,2,2,2,76]{4,0,3,2,1:T(8,128)S(1)}, f32[8,2,2,2,76]{4,0,3,2,1:T(8,128)S(1)}, u32[]{:S(2)}, u32[]{:S(2)}) collective-permute-start(f32[8,2,2,2,76]{4,0,3,2,1:T(8,128)S(1)} %fusion.52), channel_id=1, source_target_pairs={{0,1},{1,2},{2,3},{3,4},{4,5},{5,6},{6,7},{7,8},{8,9},{9,10},{10,1... | collective-permute-start | bytes 58376 | tf_op jit(solution)/shard_map/ppermute | solution.py:24
  62.4 3.9 %collective-permute-start.7 = (f32[8,2,2,2,76]{4,0,3,2,1:T(8,128)S(1)}, f32[8,2,2,2,76]{4,0,3,2,1:T(8,128)S(1)}, u32[]{:S(2)}, u32[]{:S(2)}) collective-permute-start(f32[8,2,2,2,76]{4,0,3,2,1:T(8,128)S(1)} %fusion.52), channel_id=1, source_target_pairs={{1,0},{2,1},{3,2},{4,3},{5,4},{6,5},{7,6},{8,7},{9,8},{10,9},{11,1... | collective-permute-start | bytes 58376 | tf_op jit(solution)/shard_map/ppermute | solution.py:26
  66.4 7.9 %collective-permute-done.7 = f32[8,2,2,2,76]{4,0,3,2,1:T(8,128)S(1)} collective-permute-done((f32[8,2,2,2,76]{4,0,3,2,1:T(8,128)S(1)}, f32[8,2,2,2,76]{4,0,3,2,1:T(8,128)S(1)}, u32[]{:S(2)}, u32[]{:S(2)}) %collective-permute-start.7) | collective-permute-done | bytes 19488 | tf_op jit(solution)/shard_map/ppermute | solution.py:26
  74.3 0.1 fusion.47
  74.3 0.6 copy.17
  (17 shorter events, 0.1 us)
Async XLA Ops:
  1.5 1.4 %copy-start.3 = (f32[8,2,2,2,76]{4,3,2,1,0:T(2,128)S(1)}, f32[8,2,2,2,76]{4,3,2,1,0:T(2,128)}, u32[]{:S(2)}) copy-start(f32[8,2,2,2,76]{4,3,2,1,0:T(2,128)} %param.8) | copy-start | bytes 58372
  2.9 1.0 %copy-start = (bf16[8,2,1,2,2,2850]{5,4,3,2,1,0:T(2,128)(2,1)S(1)}, bf16[8,2,1,2,2,2850]{5,4,3,2,1,0:T(2,128)(2,1)}, u32[]{:S(2)}) copy-start(bf16[8,2,1,2,2,2850]{5,4,3,2,1,0:T(2,128)(2,1)} %param.7) | copy-start | bytes 1094404
  4.1 16.1 %copy-start.1 = (f32[2,1,2,2,2850]{4,3,2,1,0:T(2,128)S(1)}, f32[2,1,2,2,2850]{4,3,2,1,0:T(2,128)}, u32[]{:S(2)}) copy-start(f32[2,1,2,2,2850]{4,3,2,1,0:T(2,128)} %param.6) | copy-start | bytes 273604
  4.4 3.2 %collective-permute-start = (f32[2,1,2,2,2850]{4,3,2,1,0:T(2,128)S(1)}, f32[2,1,2,2,2850]{4,3,2,1,0:T(2,128)S(1)}, u32[]{:S(2)}, u32[]{:S(2)}) collective-permute-start(f32[2,1,2,2,2850]{4,3,2,1,0:T(2,128)S(1)} %bitcast.58), channel_id=1, source_target_pairs={{0,128},{128,0},{256,384},{384,256},{1,129},{129,1},{257,385},{385... | collective-permute-start | bytes 273608 | tf_op jit(solution)/shard_map/ppermute | solution.py:37
  7.6 12.6 %collective-permute-start.1 = (f32[2,1,2,2,2850]{4,3,2,1,0:T(2,128)S(1)}, f32[2,1,2,2,2850]{4,3,2,1,0:T(2,128)S(1)}, u32[]{:S(2)}, u32[]{:S(2)}) collective-permute-start(f32[2,1,2,2,2850]{4,3,2,1,0:T(2,128)S(1)} %bitcast_add_fusion.1), channel_id=1, source_target_pairs={{0,256},{128,384},{256,0},{384,128},{1,257},{129,385},{257,1},{385... | collective-permute-start | bytes 273608 | tf_op jit(solution)/shard_map/ppermute | solution.py:37
  21.6 0.8 %copy-start.4 = (f32[2]{0:T(128)S(1)}, f32[2]{0:T(128)}, u32[]{:S(2)}) copy-start(f32[2]{0:T(128)} %param.9) | copy-start | bytes 28
  21.6 20.7 %copy-start.5 = (s32[2]{0:T(128)S(1)}, s32[2]{0:T(128)}, u32[]{:S(2)}) copy-start(s32[2]{0:T(128)} %param.10) | copy-start | bytes 28
  22.6 9.7 %collective-permute-start.2 = (f32[8,2,2,2,77]{4,0,3,2,1:T(8,128)S(1)}, f32[8,2,2,2,77]{4,0,3,2,1:T(8,128)S(1)}, u32[]{:S(2)}, u32[]{:S(2)}) collective-permute-start(f32[8,2,2,2,77]{4,0,3,2,1:T(8,128)S(1)} %pad_maximum_fusion.8), channel_id=1, source_target_pairs={{0,1},{1,2},{2,3},{3,4},{4,5},{5,6},{6,7},{7,8},{8,9},{9,10},{10,1... | collective-permute-start | bytes 59144 | tf_op jit(solution)/shard_map/ppermute | solution.py:24
  30.3 11.8 %collective-permute-start.3 = (f32[8,2,2,2,77]{4,0,3,2,1:T(8,128)S(1)}, f32[8,2,2,2,77]{4,0,3,2,1:T(8,128)S(1)}, u32[]{:S(2)}, u32[]{:S(2)}) collective-permute-start(f32[8,2,2,2,77]{4,0,3,2,1:T(8,128)S(1)} %pad_maximum_fusion.8), channel_id=1, source_target_pairs={{1,0},{2,1},{3,2},{4,3},{5,4},{6,5},{7,6},{8,7},{9,8},{10,9},{11,1... | collective-permute-start | bytes 59144 | tf_op jit(solution)/shard_map/ppermute | solution.py:26
  44.0 3.2 %collective-permute-start.4 = (f32[2,1,2,2,2850]{4,3,2,1,0:T(2,128)S(1)}, f32[2,1,2,2,2850]{4,3,2,1,0:T(2,128)S(1)}, u32[]{:S(2)}, u32[]{:S(2)}) collective-permute-start(f32[2,1,2,2,2850]{4,3,2,1,0:T(2,128)S(1)} %bitcast.59), channel_id=1, source_target_pairs={{0,128},{128,0},{256,384},{384,256},{1,129},{129,1},{257,385},{385... | collective-permute-start | bytes 273608 | tf_op jit(solution)/shard_map/ppermute | solution.py:37
  47.3 10.6 %collective-permute-start.5 = (f32[2,1,2,2,2850]{4,3,2,1,0:T(2,128)S(1)}, f32[2,1,2,2,2850]{4,3,2,1,0:T(2,128)S(1)}, u32[]{:S(2)}, u32[]{:S(2)}) collective-permute-start(f32[2,1,2,2,2850]{4,3,2,1,0:T(2,128)S(1)} %bitcast_add_fusion), channel_id=1, source_target_pairs={{0,256},{128,384},{256,0},{384,128},{1,257},{129,385},{257,1},{385... | collective-permute-start | bytes 273608 | tf_op jit(solution)/shard_map/ppermute | solution.py:37
  57.9 0.6 copy-start.2
  60.5 5.9 %collective-permute-start.6 = (f32[8,2,2,2,76]{4,0,3,2,1:T(8,128)S(1)}, f32[8,2,2,2,76]{4,0,3,2,1:T(8,128)S(1)}, u32[]{:S(2)}, u32[]{:S(2)}) collective-permute-start(f32[8,2,2,2,76]{4,0,3,2,1:T(8,128)S(1)} %fusion.52), channel_id=1, source_target_pairs={{0,1},{1,2},{2,3},{3,4},{4,5},{5,6},{6,7},{7,8},{8,9},{9,10},{10,1... | collective-permute-start | bytes 58376 | tf_op jit(solution)/shard_map/ppermute | solution.py:24
  62.4 11.8 %collective-permute-start.7 = (f32[8,2,2,2,76]{4,0,3,2,1:T(8,128)S(1)}, f32[8,2,2,2,76]{4,0,3,2,1:T(8,128)S(1)}, u32[]{:S(2)}, u32[]{:S(2)}) collective-permute-start(f32[8,2,2,2,76]{4,0,3,2,1:T(8,128)S(1)} %fusion.52), channel_id=1, source_target_pairs={{1,0},{2,1},{3,2},{4,3},{5,4},{6,5},{7,6},{8,7},{9,8},{10,9},{11,1... | collective-permute-start | bytes 58376 | tf_op jit(solution)/shard_map/ppermute | solution.py:26

commit v13 on v12

--- a/solution.py
+++ b/solution.py
@@ -10,7 +10,6 @@
 
 step_size = 0.6
 epsilon = 1e-06
-table_precision = lax.Precision.HIGHEST
 
 
 def extended(cells, axis, dim, width):
@@ -39,6 +38,13 @@
     return total
 
 
+def table_dot(values, table):
+    high = lax.reduce_precision(values, exponent_bits=8, mantissa_bits=7)
+    parts = jnp.stack([high, values - high])
+    out = jnp.matmul(parts, table, precision=lax.Precision.HIGH)
+    return out[0] + out[1]
+
+
 def station_tables(baseline_table):
     column = jnp.arange(STATIONS, dtype=jnp.int32)[:, None]
     left_hot = (baseline_table[0][None, :] == column).astype(jnp.float32)
@@ -48,8 +54,8 @@
 
 def corrupt(gains, model, left_hot, right_hot):
     model = model.astype(jnp.float32)
-    left_gain = jnp.matmul(gains, left_hot, precision=table_precision)[:, None]
-    right_gain = jnp.matmul(gains, right_hot, precision=table_precision)[:, None]
+    left_gain = table_dot(gains, left_hot)[:, None]
+    right_gain = table_dot(gains, right_hot)[:, None]
     left_re, left_im = (left_gain[..., 0, :], left_gain[..., 1, :])
     right_re, right_im = (right_gain[..., 0, :], right_gain[..., 1, :])
     model_re, model_im = (model[..., 0, :], model[..., 1, :])
@@ -77,9 +83,7 @@
     right_den = power * (left_re * left_re + left_im * left_im)
     left_products = jnp.sum(jnp.stack([left_num_re, left_num_im, left_den], axis=3), axis=1)
     right_terms = jnp.sum(jnp.stack([right_num_re, right_num_im, right_den], axis=3), axis=1)
-    totals = jnp.matmul(left_products, left_hot.T, precision=table_precision) + jnp.matmul(
-        right_terms, right_hot.T, precision=table_precision
-    )
+    totals = table_dot(left_products, left_hot.T) + table_dot(right_terms, right_hot.T)
     solved = totals[:, :, 0:2] / (totals[:, :, 2:3] + epsilon)
     return (1.0 - step_size) * gains + step_size * solved
 

time: 75.5 us -> 76.3 us (1.011)
  other arithmetic: 2.58 us -> 4.32 us
  matrix products: 6.07 us -> 5.22 us
    another operation x0 -> x3, other arithmetic: none -> 0.87 us  [table_dot(): parts = jnp.stack([high, values - high])]
    dot_general x8, matrix products: 6.07 us -> 5.22 us  [table_dot(): out = jnp.matmul(parts, table, precision=lax.Precision.HIGH)]
where the time goes in v13:
time: 76.3 us; the launch traced here: 75.8 us
  waiting for transfers between devices  36.8 us (48%)
  starting transfers between devices  26 us (34%)
  matrix products  5.22 us (7%)
  other arithmetic  4.32 us (6%)
  local copies, waits for them, and re-layouts  2.41 us (3%)
  between operations  1.05 us (1%)
    ppermute x4, waiting for transfers between devices, sum_over_dir(): lax.ppermute(total, 'dir', [(i, i ^ mask) for i in range(count)])  19 us
    ppermute x2, waiting for transfers between devices, extended(): lax.ppermute(head, axis, [(i + 1, i) for i in range(ends)])  17.8 us
    ppermute x4, starting transfers between devices, sum_over_dir(): lax.ppermute(total, 'dir', [(i, i ^ mask) for i in range(count)])  10.5 us
    ppermute x2, starting transfers between devices, extended(): lax.ppermute(tail, axis, [(i, i + 1) for i in range(ends)])  9.66 us
    ppermute x2, starting transfers between devices, extended(): lax.ppermute(head, axis, [(i + 1, i) for i in range(ends)])  5.84 us
    dot_general x8, matrix products, table_dot(): out = jnp.matmul(parts, table, precision=lax.Precision.HIGH)  5.22 us
  transfers between devices with their start and end apart: 8, of which 6 were waited for; matrix products, arithmetic and copies ran while one was open for 0% of the time, Pallas kernels for 0%

profile of v13, /device:TPU:254, one launch (start us, length us, event | category | flops | bytes accessed | tf_op | source)
XLA Modules:
  0.0 75.8 jit_solution(12702506220531412612)
XLA Ops:
  0.6 0.9 %slice_reduce_fusion = (s32[2850]{0:T(1024)S(1)}, s32[2850]{0:T(1024)S(1)}) fusion(s32[2,2850]{1,0:T(2,128)} %param.11), kind=kLoop, calls=%fused_computation.135 | loop fusion | bytes 45600 | tf_op jit(solution)/shard_map/slice | solution.py:51
  1.5 0.8 %reduce-precision_bitcast_fusion.1 = (f32[1,8,2,2,2,76]{5,1,4,3,2,0:T(8,128)S(1)}, f32[1,8,2,2,2,76]{5,1,4,3,2,0:T(8,128)S(1)}) fusion(f32[8,2,2,2,76]{4,3,2,1,0:T(2,128)} %param.8), kind=kLoop, calls=%fused_computation.99 | loop fusion | flops 9728 | bytes 58368 | tf_op jit(solution)/shard_map/vmap()/stack | solution.py:43
  2.3 0.6 fusion.21
  2.9 0.6 fusion.28
  3.4 0.4 copy-done
  3.9 0.2 fusion.40
  4.1 0.1 multiply_add_fusion.9
  4.3 0.2 fusion.45
  4.5 1.9 %collective-permute-start = (f32[2,1,2,2,2850]{4,3,2,1,0:T(2,128)S(1)}, f32[2,1,2,2,2850]{4,3,2,1,0:T(2,128)S(1)}, u32[]{:S(2)}, u32[]{:S(2)}) collective-permute-start(f32[2,1,2,2,2850]{4,3,2,1,0:T(2,128)S(1)} %bitcast.80), channel_id=1, source_target_pairs={{0,128},{128,0},{256,384},{384,256},{1,129},{129,1},{257,385},{385... | collective-permute-start | bytes 273608 | tf_op jit(solution)/shard_map/ppermute | solution.py:36
  6.4 1.3 %collective-permute-done = f32[2,1,2,2,2850]{4,3,2,1,0:T(2,128)S(1)} collective-permute-done((f32[2,1,2,2,2850]{4,3,2,1,0:T(2,128)S(1)}, f32[2,1,2,2,2850]{4,3,2,1,0:T(2,128)S(1)}, u32[]{:S(2)}, u32[]{:S(2)}) %collective-permute-start) | collective-permute-done | bytes 91232 | tf_op jit(solution)/shard_map/ppermute | solution.py:36
  7.7 4.7 %collective-permute-start.1 = (f32[2,1,2,2,2850]{4,3,2,1,0:T(2,128)S(1)}, f32[2,1,2,2,2850]{4,3,2,1,0:T(2,128)S(1)}, u32[]{:S(2)}, u32[]{:S(2)}) collective-permute-start(f32[2,1,2,2,2850]{4,3,2,1,0:T(2,128)S(1)} %bitcast_add_fusion.1), channel_id=1, source_target_pairs={{0,256},{128,384},{256,0},{384,128},{1,257},{129,385},{257,1},{385... | collective-permute-start | bytes 273608 | tf_op jit(solution)/shard_map/ppermute | solution.py:36
  12.5 7.9 %collective-permute-done.1 = f32[2,1,2,2,2850]{4,3,2,1,0:T(2,128)S(1)} collective-permute-done((f32[2,1,2,2,2850]{4,3,2,1,0:T(2,128)S(1)}, f32[2,1,2,2,2850]{4,3,2,1,0:T(2,128)S(1)}, u32[]{:S(2)}, u32[]{:S(2)}) %collective-permute-start.1) | collective-permute-done | bytes 91232 | tf_op jit(solution)/shard_map/ppermute | solution.py:36
  20.4 0.1 fusion.44
  20.5 0.2 multiply_subtract_fusion.6
  20.7 0.2 multiply_add_fusion.5
  20.9 0.1 fusion.37
  21.1 0.7 fusion
  21.8 0.1 fusion.35
  22.0 0.8 fusion.4
  22.9 0.1 pad_maximum_fusion.14
  23.0 7.7 %collective-permute-start.2 = (f32[8,2,2,2,77]{4,0,3,2,1:T(8,128)S(1)}, f32[8,2,2,2,77]{4,0,3,2,1:T(8,128)S(1)}, u32[]{:S(2)}, u32[]{:S(2)}) collective-permute-start(f32[8,2,2,2,77]{4,0,3,2,1:T(8,128)S(1)} %pad_maximum_fusion.14), channel_id=1, source_target_pairs={{0,1},{1,2},{2,3},{3,4},{4,5},{5,6},{6,7},{7,8},{8,9},{9,10},{10,1... | collective-permute-start | bytes 59144 | tf_op jit(solution)/shard_map/ppermute | solution.py:23
  30.8 1.9 %collective-permute-start.3 = (f32[8,2,2,2,77]{4,0,3,2,1:T(8,128)S(1)}, f32[8,2,2,2,77]{4,0,3,2,1:T(8,128)S(1)}, u32[]{:S(2)}, u32[]{:S(2)}) collective-permute-start(f32[8,2,2,2,77]{4,0,3,2,1:T(8,128)S(1)} %pad_maximum_fusion.14), channel_id=1, source_target_pairs={{1,0},{2,1},{3,2},{4,3},{5,4},{6,5},{7,6},{8,7},{9,8},{10,9},{11,1... | collective-permute-start | bytes 59144 | tf_op jit(solution)/shard_map/ppermute | solution.py:25
  32.7 9.9 %collective-permute-done.3 = f32[8,2,2,2,77]{4,0,3,2,1:T(8,128)S(1)} collective-permute-done((f32[8,2,2,2,77]{4,0,3,2,1:T(8,128)S(1)}, f32[8,2,2,2,77]{4,0,3,2,1:T(8,128)S(1)}, u32[]{:S(2)}, u32[]{:S(2)}) %collective-permute-start.3) | collective-permute-done | bytes 19744 | tf_op jit(solution)/shard_map/ppermute | solution.py:25
  42.6 0.2 maximum_reduce_fusion.1
  42.8 0.1 reduce-precision_bitcast_fusion
  42.9 0.6 fusion.18
  43.5 0.6 fusion.25
  44.1 0.1 fusion.39
  44.1 0.1 fusion.38
  44.2 0.1 multiply_add_fusion.3
  44.4 0.2 fusion.43
  44.7 1.9 %collective-permute-start.4 = (f32[2,1,2,2,2850]{4,3,2,1,0:T(2,128)S(1)}, f32[2,1,2,2,2850]{4,3,2,1,0:T(2,128)S(1)}, u32[]{:S(2)}, u32[]{:S(2)}) collective-permute-start(f32[2,1,2,2,2850]{4,3,2,1,0:T(2,128)S(1)} %bitcast.81), channel_id=1, source_target_pairs={{0,128},{128,0},{256,384},{384,256},{1,129},{129,1},{257,385},{385... | collective-permute-start | bytes 273608 | tf_op jit(solution)/shard_map/ppermute | solution.py:36
  46.6 1.3 %collective-permute-done.4 = f32[2,1,2,2,2850]{4,3,2,1,0:T(2,128)S(1)} collective-permute-done((f32[2,1,2,2,2850]{4,3,2,1,0:T(2,128)S(1)}, f32[2,1,2,2,2850]{4,3,2,1,0:T(2,128)S(1)}, u32[]{:S(2)}, u32[]{:S(2)}) %collective-permute-start.4) | collective-permute-done | bytes 91232 | tf_op jit(solution)/shard_map/ppermute | solution.py:36
  47.9 1.9 %collective-permute-start.5 = (f32[2,1,2,2,2850]{4,3,2,1,0:T(2,128)S(1)}, f32[2,1,2,2,2850]{4,3,2,1,0:T(2,128)S(1)}, u32[]{:S(2)}, u32[]{:S(2)}) collective-permute-start(f32[2,1,2,2,2850]{4,3,2,1,0:T(2,128)S(1)} %bitcast_add_fusion), channel_id=1, source_target_pairs={{0,256},{128,384},{256,0},{384,128},{1,257},{129,385},{257,1},{385... | collective-permute-start | bytes 273608 | tf_op jit(solution)/shard_map/ppermute | solution.py:36
  49.8 8.6 %collective-permute-done.5 = f32[2,1,2,2,2850]{4,3,2,1,0:T(2,128)S(1)} collective-permute-done((f32[2,1,2,2,2850]{4,3,2,1,0:T(2,128)S(1)}, f32[2,1,2,2,2850]{4,3,2,1,0:T(2,128)S(1)}, u32[]{:S(2)}, u32[]{:S(2)}) %collective-permute-start.5) | collective-permute-done | bytes 91232 | tf_op jit(solution)/shard_map/ppermute | solution.py:36
  58.6 0.1 fusion.42
  58.7 0.1 multiply_subtract_fusion.1
  58.8 0.4 copy-done.2
  59.2 0.2 multiply_add_fusion.1
  59.4 0.1 fusion.33
  59.6 0.7 fusion.8
  60.3 0.1 fusion.31
  60.5 0.7 fusion.12
  61.3 1.9 %collective-permute-start.6 = (f32[8,2,2,2,76]{4,0,3,2,1:T(8,128)S(1)}, f32[8,2,2,2,76]{4,0,3,2,1:T(8,128)S(1)}, u32[]{:S(2)}, u32[]{:S(2)}) collective-permute-start(f32[8,2,2,2,76]{4,0,3,2,1:T(8,128)S(1)} %fusion.68), channel_id=1, source_target_pairs={{0,1},{1,2},{2,3},{3,4},{4,5},{5,6},{6,7},{7,8},{8,9},{9,10},{10,1... | collective-permute-start | bytes 58376 | tf_op jit(solution)/shard_map/ppermute | solution.py:23
  63.2 3.9 %collective-permute-start.7 = (f32[8,2,2,2,76]{4,0,3,2,1:T(8,128)S(1)}, f32[8,2,2,2,76]{4,0,3,2,1:T(8,128)S(1)}, u32[]{:S(2)}, u32[]{:S(2)}) collective-permute-start(f32[8,2,2,2,76]{4,0,3,2,1:T(8,128)S(1)} %fusion.68), channel_id=1, source_target_pairs={{1,0},{2,1},{3,2},{4,3},{5,4},{6,5},{7,6},{8,7},{9,8},{10,9},{11,1... | collective-permute-start | bytes 58376 | tf_op jit(solution)/shard_map/ppermute | solution.py:25
  67.2 7.9 %collective-permute-done.7 = f32[8,2,2,2,76]{4,0,3,2,1:T(8,128)S(1)} collective-permute-done((f32[8,2,2,2,76]{4,0,3,2,1:T(8,128)S(1)}, f32[8,2,2,2,76]{4,0,3,2,1:T(8,128)S(1)}, u32[]{:S(2)}, u32[]{:S(2)}) %collective-permute-start.7) | collective-permute-done | bytes 19488 | tf_op jit(solution)/shard_map/ppermute | solution.py:25
  75.1 0.1 fusion.63
  75.1 0.6 copy.17
  (28 shorter events, 0.6 us)
Async XLA Ops:
  2.8 1.0 %copy-start = (bf16[8,2,1,2,2,2850]{5,4,3,2,1,0:T(2,128)(2,1)S(1)}, bf16[8,2,1,2,2,2850]{5,4,3,2,1,0:T(2,128)(2,1)}, u32[]{:S(2)}) copy-start(bf16[8,2,1,2,2,2850]{5,4,3,2,1,0:T(2,128)(2,1)} %param.7) | copy-start | bytes 1094404
  4.2 16.2 %copy-start.1 = (f32[2,1,2,2,2850]{4,3,2,1,0:T(2,128)S(1)}, f32[2,1,2,2,2850]{4,3,2,1,0:T(2,128)}, u32[]{:S(2)}) copy-start(f32[2,1,2,2,2850]{4,3,2,1,0:T(2,128)} %param.6) | copy-start | bytes 273604
  4.5 3.2 %collective-permute-start = (f32[2,1,2,2,2850]{4,3,2,1,0:T(2,128)S(1)}, f32[2,1,2,2,2850]{4,3,2,1,0:T(2,128)S(1)}, u32[]{:S(2)}, u32[]{:S(2)}) collective-permute-start(f32[2,1,2,2,2850]{4,3,2,1,0:T(2,128)S(1)} %bitcast.80), channel_id=1, source_target_pairs={{0,128},{128,0},{256,384},{384,256},{1,129},{129,1},{257,385},{385... | collective-permute-start | bytes 273608 | tf_op jit(solution)/shard_map/ppermute | solution.py:36
  7.7 12.6 %collective-permute-start.1 = (f32[2,1,2,2,2850]{4,3,2,1,0:T(2,128)S(1)}, f32[2,1,2,2,2850]{4,3,2,1,0:T(2,128)S(1)}, u32[]{:S(2)}, u32[]{:S(2)}) collective-permute-start(f32[2,1,2,2,2850]{4,3,2,1,0:T(2,128)S(1)} %bitcast_add_fusion.1), channel_id=1, source_target_pairs={{0,256},{128,384},{256,0},{384,128},{1,257},{129,385},{257,1},{385... | collective-permute-start | bytes 273608 | tf_op jit(solution)/shard_map/ppermute | solution.py:36
  22.0 0.8 %copy-start.3 = (f32[8,2,2,2,76]{4,3,2,1,0:T(2,128)S(1)}, f32[8,2,2,2,76]{4,3,2,1,0:T(2,128)}, u32[]{:S(2)}) copy-start(f32[8,2,2,2,76]{4,3,2,1,0:T(2,128)} %param.8) | copy-start | bytes 58372
  22.0 0.9 %copy-start.4 = (f32[2]{0:T(128)S(1)}, f32[2]{0:T(128)}, u32[]{:S(2)}) copy-start(f32[2]{0:T(128)} %param.9) | copy-start | bytes 28
  22.0 20.8 %copy-start.5 = (s32[2]{0:T(128)S(1)}, s32[2]{0:T(128)}, u32[]{:S(2)}) copy-start(s32[2]{0:T(128)} %param.10) | copy-start | bytes 28
  23.0 9.7 %collective-permute-start.2 = (f32[8,2,2,2,77]{4,0,3,2,1:T(8,128)S(1)}, f32[8,2,2,2,77]{4,0,3,2,1:T(8,128)S(1)}, u32[]{:S(2)}, u32[]{:S(2)}) collective-permute-start(f32[8,2,2,2,77]{4,0,3,2,1:T(8,128)S(1)} %pad_maximum_fusion.14), channel_id=1, source_target_pairs={{0,1},{1,2},{2,3},{3,4},{4,5},{5,6},{6,7},{7,8},{8,9},{9,10},{10,1... | collective-permute-start | bytes 59144 | tf_op jit(solution)/shard_map/ppermute | solution.py:23
  30.8 11.8 %collective-permute-start.3 = (f32[8,2,2,2,77]{4,0,3,2,1:T(8,128)S(1)}, f32[8,2,2,2,77]{4,0,3,2,1:T(8,128)S(1)}, u32[]{:S(2)}, u32[]{:S(2)}) collective-permute-start(f32[8,2,2,2,77]{4,0,3,2,1:T(8,128)S(1)} %pad_maximum_fusion.14), channel_id=1, source_target_pairs={{1,0},{2,1},{3,2},{4,3},{5,4},{6,5},{7,6},{8,7},{9,8},{10,9},{11,1... | collective-permute-start | bytes 59144 | tf_op jit(solution)/shard_map/ppermute | solution.py:25
  44.7 3.2 %collective-permute-start.4 = (f32[2,1,2,2,2850]{4,3,2,1,0:T(2,128)S(1)}, f32[2,1,2,2,2850]{4,3,2,1,0:T(2,128)S(1)}, u32[]{:S(2)}, u32[]{:S(2)}) collective-permute-start(f32[2,1,2,2,2850]{4,3,2,1,0:T(2,128)S(1)} %bitcast.81), channel_id=1, source_target_pairs={{0,128},{128,0},{256,384},{384,256},{1,129},{129,1},{257,385},{385... | collective-permute-start | bytes 273608 | tf_op jit(solution)/shard_map/ppermute | solution.py:36
  47.9 10.6 %collective-permute-start.5 = (f32[2,1,2,2,2850]{4,3,2,1,0:T(2,128)S(1)}, f32[2,1,2,2,2850]{4,3,2,1,0:T(2,128)S(1)}, u32[]{:S(2)}, u32[]{:S(2)}) collective-permute-start(f32[2,1,2,2,2850]{4,3,2,1,0:T(2,128)S(1)} %bitcast_add_fusion), channel_id=1, source_target_pairs={{0,256},{128,384},{256,0},{384,128},{1,257},{129,385},{257,1},{385... | collective-permute-start | bytes 273608 | tf_op jit(solution)/shard_map/ppermute | solution.py:36
  58.6 0.6 copy-start.2
  61.3 5.9 %collective-permute-start.6 = (f32[8,2,2,2,76]{4,0,3,2,1:T(8,128)S(1)}, f32[8,2,2,2,76]{4,0,3,2,1:T(8,128)S(1)}, u32[]{:S(2)}, u32[]{:S(2)}) collective-permute-start(f32[8,2,2,2,76]{4,0,3,2,1:T(8,128)S(1)} %fusion.68), channel_id=1, source_target_pairs={{0,1},{1,2},{2,3},{3,4},{4,5},{5,6},{6,7},{7,8},{8,9},{9,10},{10,1... | collective-permute-start | bytes 58376 | tf_op jit(solution)/shard_map/ppermute | solution.py:23
  63.2 11.8 %collective-permute-start.7 = (f32[8,2,2,2,76]{4,0,3,2,1:T(8,128)S(1)}, f32[8,2,2,2,76]{4,0,3,2,1:T(8,128)S(1)}, u32[]{:S(2)}, u32[]{:S(2)}) collective-permute-start(f32[8,2,2,2,76]{4,0,3,2,1:T(8,128)S(1)} %fusion.68), channel_id=1, source_target_pairs={{1,0},{2,1},{3,2},{4,3},{5,4},{6,5},{7,6},{8,7},{9,8},{10,9},{11,1... | collective-permute-start | bytes 58376 | tf_op jit(solution)/shard_map/ppermute | solution.py:25

commit v14 on v12

--- a/solution.py
+++ b/solution.py
@@ -115,6 +115,7 @@
         total = sum_over_dir(partial_total)
         residual = visibilities - total
         stepped = solve_all(current, model, corrupted_model, parts, residual, left_hot, right_hot)
+        residual = -(total - visibilities)
         if padded_weights is None:
             column = jnp.broadcast_to(weights[None, :, None, None, None], stepped.shape[:-1] + (1,))
             padded = extended(jnp.concatenate([stepped, column], axis=-1), "chan", 1, SPAN)

time: 75.5 us -> 75.6 us (level)
    unnamed x13 -> x11, local copies, waits for them, and re-layouts: 1.64 us -> 1.1 us
where the time goes in v14:
time: 75.6 us; the launch traced here: 75.1 us
  waiting for transfers between devices  36.8 us (49%)
  starting transfers between devices  26 us (34%)
  matrix products  6.07 us (8%)
  other arithmetic  3.25 us (4%)
  local copies, waits for them, and re-layouts  2.05 us (3%)
  between operations  0.96 us (1%)
    ppermute x4, waiting for transfers between devices, sum_over_dir(): lax.ppermute(total, 'dir', [(i, i ^ mask) for i in range(count)])  19 us
    ppermute x2, waiting for transfers between devices, extended(): lax.ppermute(head, axis, [(i + 1, i) for i in range(ends)])  17.8 us
    ppermute x4, starting transfers between devices, sum_over_dir(): lax.ppermute(total, 'dir', [(i, i ^ mask) for i in range(count)])  10.5 us
    ppermute x2, starting transfers between devices, extended(): lax.ppermute(tail, axis, [(i, i + 1) for i in range(ends)])  9.66 us
    ppermute x2, starting transfers between devices, extended(): lax.ppermute(head, axis, [(i + 1, i) for i in range(ends)])  5.84 us
    dot_general x2, matrix products, corrupt(): jnp.matmul(gains, right_hot, precision=table_precision)[:, None]  1.89 us
    dot_general x2, matrix products, solve(): jnp.matmul(right_terms, right_hot.T, precision=table_precision)  1.55 us
    dot_general x2, matrix products, solve(): jnp.matmul(left_products, left_hot.T, precision=table_precision)  1.55 us
  transfers between devices with their start and end apart: 8, of which 6 were waited for; matrix products, arithmetic and copies ran while one was open for 0% of the time, Pallas kernels for 0%

profile of v14, /device:TPU:254, one launch (start us, length us, event | category | flops | bytes accessed | tf_op | source)
XLA Modules:
  0.0 75.1 jit_solution(16252313831187648442)
XLA Ops:
  0.6 0.9 %slice_reduce_fusion.1 = (s32[2850]{0:T(1024)S(1)}, s32[2850]{0:T(1024)S(1)}) fusion(s32[2,2850]{1,0:T(2,128)} %param.11), kind=kLoop, calls=%fused_computation.113 | loop fusion | bytes 45600 | tf_op jit(solution)/shard_map/slice | solution.py:44
  1.5 0.0 copy-start.2
  1.5 1.3 %convolution_bitcast_fusion.2 = f32[8,2,1,2,2,2850]{5,0,4,3,1,2:T(8,128)S(1)} fusion(s32[2850]{0:T(1024)S(1)} %get-tuple-element.11, f32[8,2,2,2,76]{4,3,2,1,0:T(2,128)} %param.8), kind=kOutput, calls=%fused_computation.2 | convolution fusion | flops 166565408 | bytes 760456 | tf_op jit(solution)/shard_map/vmap()/dot_general | solution.py:52
  2.9 0.5 convolution_bitcast_fusion.3
  3.4 0.4 copy-done.1
  3.9 0.1 copy_convert_fusion
  3.9 0.1 multiply_add_fusion.9
  4.1 0.1 multiply_subtract_fusion.8
  4.2 0.2 fusion.35
  4.4 1.9 %collective-permute-start = (f32[2,1,2,2,2850]{4,3,2,1,0:T(2,128)S(1)}, f32[2,1,2,2,2850]{4,3,2,1,0:T(2,128)S(1)}, u32[]{:S(2)}, u32[]{:S(2)}) collective-permute-start(f32[2,1,2,2,2850]{4,3,2,1,0:T(2,128)S(1)} %bitcast.58), channel_id=1, source_target_pairs={{0,128},{128,0},{256,384},{384,256},{1,129},{129,1},{257,385},{385... | collective-permute-start | bytes 273608 | tf_op jit(solution)/shard_map/ppermute | solution.py:37
  6.3 1.3 %collective-permute-done = f32[2,1,2,2,2850]{4,3,2,1,0:T(2,128)S(1)} collective-permute-done((f32[2,1,2,2,2850]{4,3,2,1,0:T(2,128)S(1)}, f32[2,1,2,2,2850]{4,3,2,1,0:T(2,128)S(1)}, u32[]{:S(2)}, u32[]{:S(2)}) %collective-permute-start) | collective-permute-done | bytes 91232 | tf_op jit(solution)/shard_map/ppermute | solution.py:37
  7.6 0.1 bitcast_add_fusion.1
  7.6 4.7 %collective-permute-start.1 = (f32[2,1,2,2,2850]{4,3,2,1,0:T(2,128)S(1)}, f32[2,1,2,2,2850]{4,3,2,1,0:T(2,128)S(1)}, u32[]{:S(2)}, u32[]{:S(2)}) collective-permute-start(f32[2,1,2,2,2850]{4,3,2,1,0:T(2,128)S(1)} %bitcast_add_fusion.1), channel_id=1, source_target_pairs={{0,256},{128,384},{256,0},{384,128},{1,257},{129,385},{257,1},{385... | collective-permute-start | bytes 273608 | tf_op jit(solution)/shard_map/ppermute | solution.py:37
  12.3 7.9 %collective-permute-done.1 = f32[2,1,2,2,2850]{4,3,2,1,0:T(2,128)S(1)} collective-permute-done((f32[2,1,2,2,2850]{4,3,2,1,0:T(2,128)S(1)}, f32[2,1,2,2,2850]{4,3,2,1,0:T(2,128)S(1)}, u32[]{:S(2)}, u32[]{:S(2)}) %collective-permute-start.1) | collective-permute-done | bytes 91232 | tf_op jit(solution)/shard_map/ppermute | solution.py:37
  20.2 0.1 subtract_bitcast_fusion.1
  20.3 0.1 fusion.34
  20.4 0.2 multiply_add_fusion.5
  20.6 0.2 multiply_subtract_fusion.6
  20.8 0.8 %fusion = f32[8,2,2,3,76]{4,0,3,2,1:T(8,128)S(1)} fusion(f32[8,2,1,2,1,2850]{5,0,4,3,1,2:T(8,128)S(1)} %get-tuple-element.44, f32[8,2,1,2,1,2850]{5,0,4,3,1,2:T(8,128)S(1)} %get-tuple-element.35, f32[8,2,1,2,1,2850]{5,0,4,3,1,2:T(8,128)S(1)} %get-tuple-element.34, s32[2850]{0:T(1024)S(1)} %get-tuple-element.10), kind=kOutput, calls=%fused_computation.5 | convolution fusion | flops 250287008 | bytes 1134984 | tf_op jit(solution)/shard_map/vmap()/dot_general | solution.py:80
  21.6 0.8 %fusion.21 = f32[8,2,2,3,76]{4,0,3,2,1:T(8,128)S(1)} fusion(f32[8,2,2,3,76]{4,0,3,2,1:T(8,128)S(1)} %fusion, f32[8,2,1,2,1,2850]{5,0,4,3,1,2:T(8,128)S(1)} %get-tuple-element.36, f32[8,2,1,2,1,2850]{5,0,4,3,1,2:T(8,128)S(1)} %get-tuple-element.43, f32[8,2,1,2,1,2850]{5,0,4,3,1,2:T(8,128)S(1)} %get-tuple-element.24, s32[2850]{0:T(1024)S(1)} %get-tuple-element.11), kind=kOutput, calls=%fused_computation.29 | convolution fusion | flops 250294304 | bytes 1164168 | tf_op jit(solution)/shard_map/vmap()/dot_general | solution.py:80
  22.4 0.1 broadcast_in_dim.12
  22.5 0.1 pad_maximum_fusion.8
  22.6 7.7 %collective-permute-start.2 = (f32[8,2,2,2,77]{4,0,3,2,1:T(8,128)S(1)}, f32[8,2,2,2,77]{4,0,3,2,1:T(8,128)S(1)}, u32[]{:S(2)}, u32[]{:S(2)}) collective-permute-start(f32[8,2,2,2,77]{4,0,3,2,1:T(8,128)S(1)} %pad_maximum_fusion.8), channel_id=1, source_target_pairs={{0,1},{1,2},{2,3},{3,4},{4,5},{5,6},{6,7},{7,8},{8,9},{9,10},{10,1... | collective-permute-start | bytes 59144 | tf_op jit(solution)/shard_map/ppermute | solution.py:24
  30.3 1.9 %collective-permute-start.3 = (f32[8,2,2,2,77]{4,0,3,2,1:T(8,128)S(1)}, f32[8,2,2,2,77]{4,0,3,2,1:T(8,128)S(1)}, u32[]{:S(2)}, u32[]{:S(2)}) collective-permute-start(f32[8,2,2,2,77]{4,0,3,2,1:T(8,128)S(1)} %pad_maximum_fusion.8), channel_id=1, source_target_pairs={{1,0},{2,1},{3,2},{4,3},{5,4},{6,5},{7,6},{8,7},{9,8},{10,9},{11,1... | collective-permute-start | bytes 59144 | tf_op jit(solution)/shard_map/ppermute | solution.py:26
  32.3 9.9 %collective-permute-done.3 = f32[8,2,2,2,77]{4,0,3,2,1:T(8,128)S(1)} collective-permute-done((f32[8,2,2,2,77]{4,0,3,2,1:T(8,128)S(1)}, f32[8,2,2,2,77]{4,0,3,2,1:T(8,128)S(1)}, u32[]{:S(2)}, u32[]{:S(2)}) %collective-permute-start.3) | collective-permute-done | bytes 19744 | tf_op jit(solution)/shard_map/ppermute | solution.py:26
  42.2 0.2 maximum_reduce_fusion.1
  42.4 0.1 fusion.54
  42.5 0.5 convolution_bitcast_fusion
  43.0 0.5 convolution_bitcast_fusion.1
  43.6 0.1 multiply_add_fusion.3
  43.7 0.1 multiply_subtract_fusion.3
  43.8 0.2 fusion.33
  44.0 1.9 %collective-permute-start.4 = (f32[2,1,2,2,2850]{4,3,2,1,0:T(2,128)S(1)}, f32[2,1,2,2,2850]{4,3,2,1,0:T(2,128)S(1)}, u32[]{:S(2)}, u32[]{:S(2)}) collective-permute-start(f32[2,1,2,2,2850]{4,3,2,1,0:T(2,128)S(1)} %bitcast.59), channel_id=1, source_target_pairs={{0,128},{128,0},{256,384},{384,256},{1,129},{129,1},{257,385},{385... | collective-permute-start | bytes 273608 | tf_op jit(solution)/shard_map/ppermute | solution.py:37
  46.0 1.3 %collective-permute-done.4 = f32[2,1,2,2,2850]{4,3,2,1,0:T(2,128)S(1)} collective-permute-done((f32[2,1,2,2,2850]{4,3,2,1,0:T(2,128)S(1)}, f32[2,1,2,2,2850]{4,3,2,1,0:T(2,128)S(1)}, u32[]{:S(2)}, u32[]{:S(2)}) %collective-permute-start.4) | collective-permute-done | bytes 91232 | tf_op jit(solution)/shard_map/ppermute | solution.py:37
  47.2 0.1 bitcast_add_fusion
  47.3 1.9 %collective-permute-start.5 = (f32[2,1,2,2,2850]{4,3,2,1,0:T(2,128)S(1)}, f32[2,1,2,2,2850]{4,3,2,1,0:T(2,128)S(1)}, u32[]{:S(2)}, u32[]{:S(2)}) collective-permute-start(f32[2,1,2,2,2850]{4,3,2,1,0:T(2,128)S(1)} %bitcast_add_fusion), channel_id=1, source_target_pairs={{0,256},{128,384},{256,0},{384,128},{1,257},{129,385},{257,1},{385... | collective-permute-start | bytes 273608 | tf_op jit(solution)/shard_map/ppermute | solution.py:37
  49.2 8.6 %collective-permute-done.5 = f32[2,1,2,2,2850]{4,3,2,1,0:T(2,128)S(1)} collective-permute-done((f32[2,1,2,2,2850]{4,3,2,1,0:T(2,128)S(1)}, f32[2,1,2,2,2850]{4,3,2,1,0:T(2,128)S(1)}, u32[]{:S(2)}, u32[]{:S(2)}) %collective-permute-start.5) | collective-permute-done | bytes 91232 | tf_op jit(solution)/shard_map/ppermute | solution.py:37
  57.8 0.7 subtract_negate_fusion
  58.6 0.1 fusion.32
  58.7 0.1 multiply_add_fusion
  58.8 0.2 multiply_subtract_fusion
  59.0 0.8 %fusion.10 = f32[8,2,2,3,76]{4,0,3,2,1:T(8,128)S(1)} fusion(f32[8,2,1,2,1,2850]{5,0,4,3,1,2:T(8,128)S(1)} %get-tuple-element.42, f32[8,2,1,2,1,2850]{5,0,4,3,1,2:T(8,128)S(1)} %get-tuple-element.40, f32[8,2,1,2,1,2850]{5,0,4,3,1,2:T(8,128)S(1)} %get-tuple-element.41, s32[2850]{0:T(1024)S(1)} %get-tuple-element.10), kind=kOutput, calls=%fused_computation.17 | convolution fusion | flops 250287008 | bytes 1134984 | tf_op jit(solution)/shard_map/vmap()/dot_general | solution.py:80
  59.8 0.8 %fusion.20 = f32[8,2,2,3,76]{4,0,3,2,1:T(8,128)S(1)} fusion(f32[8,2,2,3,76]{4,0,3,2,1:T(8,128)S(1)} %fusion.10, f32[8,2,1,2,1,2850]{5,0,4,3,1,2:T(8,128)S(1)} %get-tuple-element.39, f32[8,2,1,2,1,2850]{5,0,4,3,1,2:T(8,128)S(1)} %get-tuple-element.38, f32[8,2,1,2,1,2850]{5,0,4,3,1,2:T(8,128)S(1)} %get-tuple-element.12, s32[2850]{0:T(1024)S(1)} %get-tuple-element.11), kind=kOutput, calls=%fused_computation.28 | convolution fusion | flops 250294304 | bytes 1164168 | tf_op jit(solution)/shard_map/vmap()/dot_general | solution.py:80
  60.6 1.9 %collective-permute-start.6 = (f32[8,2,2,2,76]{4,0,3,2,1:T(8,128)S(1)}, f32[8,2,2,2,76]{4,0,3,2,1:T(8,128)S(1)}, u32[]{:S(2)}, u32[]{:S(2)}) collective-permute-start(f32[8,2,2,2,76]{4,0,3,2,1:T(8,128)S(1)} %fusion.52), channel_id=1, source_target_pairs={{0,1},{1,2},{2,3},{3,4},{4,5},{5,6},{6,7},{7,8},{8,9},{9,10},{10,1... | collective-permute-start | bytes 58376 | tf_op jit(solution)/shard_map/ppermute | solution.py:24
  62.6 3.9 %collective-permute-start.7 = (f32[8,2,2,2,76]{4,0,3,2,1:T(8,128)S(1)}, f32[8,2,2,2,76]{4,0,3,2,1:T(8,128)S(1)}, u32[]{:S(2)}, u32[]{:S(2)}) collective-permute-start(f32[8,2,2,2,76]{4,0,3,2,1:T(8,128)S(1)} %fusion.52), channel_id=1, source_target_pairs={{1,0},{2,1},{3,2},{4,3},{5,4},{6,5},{7,6},{8,7},{9,8},{10,9},{11,1... | collective-permute-start | bytes 58376 | tf_op jit(solution)/shard_map/ppermute | solution.py:26
  66.5 7.9 %collective-permute-done.7 = f32[8,2,2,2,76]{4,0,3,2,1:T(8,128)S(1)} collective-permute-done((f32[8,2,2,2,76]{4,0,3,2,1:T(8,128)S(1)}, f32[8,2,2,2,76]{4,0,3,2,1:T(8,128)S(1)}, u32[]{:S(2)}, u32[]{:S(2)}) %collective-permute-start.7) | collective-permute-done | bytes 19488 | tf_op jit(solution)/shard_map/ppermute | solution.py:26
  74.4 0.1 fusion.47
  74.5 0.6 copy.17
  (15 shorter events, 0.1 us)
Async XLA Ops:
  1.5 1.4 %copy-start.2 = (f32[8,2,2,2,76]{4,3,2,1,0:T(2,128)S(1)}, f32[8,2,2,2,76]{4,3,2,1,0:T(2,128)}, u32[]{:S(2)}) copy-start(f32[8,2,2,2,76]{4,3,2,1,0:T(2,128)} %param.8) | copy-start | bytes 58372
  2.9 1.0 %copy-start.1 = (bf16[8,2,1,2,2,2850]{5,4,3,2,1,0:T(2,128)(2,1)S(1)}, bf16[8,2,1,2,2,2850]{5,4,3,2,1,0:T(2,128)(2,1)}, u32[]{:S(2)}) copy-start(bf16[8,2,1,2,2,2850]{5,4,3,2,1,0:T(2,128)(2,1)} %param.7) | copy-start | bytes 1094404
  4.1 16.1 %copy-start = (f32[2,1,2,2,2850]{4,3,2,1,0:T(2,128)S(1)}, f32[2,1,2,2,2850]{4,3,2,1,0:T(2,128)}, u32[]{:S(2)}) copy-start(f32[2,1,2,2,2850]{4,3,2,1,0:T(2,128)} %param.6) | copy-start | bytes 273604
  4.4 3.2 %collective-permute-start = (f32[2,1,2,2,2850]{4,3,2,1,0:T(2,128)S(1)}, f32[2,1,2,2,2850]{4,3,2,1,0:T(2,128)S(1)}, u32[]{:S(2)}, u32[]{:S(2)}) collective-permute-start(f32[2,1,2,2,2850]{4,3,2,1,0:T(2,128)S(1)} %bitcast.58), channel_id=1, source_target_pairs={{0,128},{128,0},{256,384},{384,256},{1,129},{129,1},{257,385},{385... | collective-permute-start | bytes 273608 | tf_op jit(solution)/shard_map/ppermute | solution.py:37
  7.6 12.6 %collective-permute-start.1 = (f32[2,1,2,2,2850]{4,3,2,1,0:T(2,128)S(1)}, f32[2,1,2,2,2850]{4,3,2,1,0:T(2,128)S(1)}, u32[]{:S(2)}, u32[]{:S(2)}) collective-permute-start(f32[2,1,2,2,2850]{4,3,2,1,0:T(2,128)S(1)} %bitcast_add_fusion.1), channel_id=1, source_target_pairs={{0,256},{128,384},{256,0},{384,128},{1,257},{129,385},{257,1},{385... | collective-permute-start | bytes 273608 | tf_op jit(solution)/shard_map/ppermute | solution.py:37
  21.6 0.8 %copy-start.3 = (f32[2]{0:T(128)S(1)}, f32[2]{0:T(128)}, u32[]{:S(2)}) copy-start(f32[2]{0:T(128)} %param.9) | copy-start | bytes 28
  21.6 20.7 %copy-start.4 = (s32[2]{0:T(128)S(1)}, s32[2]{0:T(128)}, u32[]{:S(2)}) copy-start(s32[2]{0:T(128)} %param.10) | copy-start | bytes 28
  22.6 9.7 %collective-permute-start.2 = (f32[8,2,2,2,77]{4,0,3,2,1:T(8,128)S(1)}, f32[8,2,2,2,77]{4,0,3,2,1:T(8,128)S(1)}, u32[]{:S(2)}, u32[]{:S(2)}) collective-permute-start(f32[8,2,2,2,77]{4,0,3,2,1:T(8,128)S(1)} %pad_maximum_fusion.8), channel_id=1, source_target_pairs={{0,1},{1,2},{2,3},{3,4},{4,5},{5,6},{6,7},{7,8},{8,9},{9,10},{10,1... | collective-permute-start | bytes 59144 | tf_op jit(solution)/shard_map/ppermute | solution.py:24
  30.3 11.8 %collective-permute-start.3 = (f32[8,2,2,2,77]{4,0,3,2,1:T(8,128)S(1)}, f32[8,2,2,2,77]{4,0,3,2,1:T(8,128)S(1)}, u32[]{:S(2)}, u32[]{:S(2)}) collective-permute-start(f32[8,2,2,2,77]{4,0,3,2,1:T(8,128)S(1)} %pad_maximum_fusion.8), channel_id=1, source_target_pairs={{1,0},{2,1},{3,2},{4,3},{5,4},{6,5},{7,6},{8,7},{9,8},{10,9},{11,1... | collective-permute-start | bytes 59144 | tf_op jit(solution)/shard_map/ppermute | solution.py:26
  44.0 3.2 %collective-permute-start.4 = (f32[2,1,2,2,2850]{4,3,2,1,0:T(2,128)S(1)}, f32[2,1,2,2,2850]{4,3,2,1,0:T(2,128)S(1)}, u32[]{:S(2)}, u32[]{:S(2)}) collective-permute-start(f32[2,1,2,2,2850]{4,3,2,1,0:T(2,128)S(1)} %bitcast.59), channel_id=1, source_target_pairs={{0,128},{128,0},{256,384},{384,256},{1,129},{129,1},{257,385},{385... | collective-permute-start | bytes 273608 | tf_op jit(solution)/shard_map/ppermute | solution.py:37
  47.3 10.6 %collective-permute-start.5 = (f32[2,1,2,2,2850]{4,3,2,1,0:T(2,128)S(1)}, f32[2,1,2,2,2850]{4,3,2,1,0:T(2,128)S(1)}, u32[]{:S(2)}, u32[]{:S(2)}) collective-permute-start(f32[2,1,2,2,2850]{4,3,2,1,0:T(2,128)S(1)} %bitcast_add_fusion), channel_id=1, source_target_pairs={{0,256},{128,384},{256,0},{384,128},{1,257},{129,385},{257,1},{385... | collective-permute-start | bytes 273608 | tf_op jit(solution)/shard_map/ppermute | solution.py:37
  60.6 5.9 %collective-permute-start.6 = (f32[8,2,2,2,76]{4,0,3,2,1:T(8,128)S(1)}, f32[8,2,2,2,76]{4,0,3,2,1:T(8,128)S(1)}, u32[]{:S(2)}, u32[]{:S(2)}) collective-permute-start(f32[8,2,2,2,76]{4,0,3,2,1:T(8,128)S(1)} %fusion.52), channel_id=1, source_target_pairs={{0,1},{1,2},{2,3},{3,4},{4,5},{5,6},{6,7},{7,8},{8,9},{9,10},{10,1... | collective-permute-start | bytes 58376 | tf_op jit(solution)/shard_map/ppermute | solution.py:24
  62.6 11.8 %collective-permute-start.7 = (f32[8,2,2,2,76]{4,0,3,2,1:T(8,128)S(1)}, f32[8,2,2,2,76]{4,0,3,2,1:T(8,128)S(1)}, u32[]{:S(2)}, u32[]{:S(2)}) collective-permute-start(f32[8,2,2,2,76]{4,0,3,2,1:T(8,128)S(1)} %fusion.52), channel_id=1, source_target_pairs={{1,0},{2,1},{3,2},{4,3},{5,4},{6,5},{7,6},{8,7},{9,8},{10,9},{11,1... | collective-permute-start | bytes 58376 | tf_op jit(solution)/shard_map/ppermute | solution.py:26

commit v15 on v12

--- a/solution.py
+++ b/solution.py
@@ -75,12 +75,17 @@
     power = model_re * model_re + model_im * model_im
     left_den = power * (right_re * right_re + right_im * right_im)
     right_den = power * (left_re * left_re + left_im * left_im)
-    left_products = jnp.sum(jnp.stack([left_num_re, left_num_im, left_den], axis=3), axis=1)
-    right_terms = jnp.sum(jnp.stack([right_num_re, right_num_im, right_den], axis=3), axis=1)
-    totals = jnp.matmul(left_products, left_hot.T, precision=table_precision) + jnp.matmul(
+    left_products = jnp.sum(jnp.stack([left_num_re, left_num_im], axis=3), axis=1)
+    right_terms = jnp.sum(jnp.stack([right_num_re, right_num_im], axis=3), axis=1)
+    left_power = jnp.sum(left_den[:, :, :, None], axis=1)
+    right_power = jnp.sum(right_den[:, :, :, None], axis=1)
+    numer = jnp.matmul(left_products, left_hot.T, precision=table_precision) + jnp.matmul(
         right_terms, right_hot.T, precision=table_precision
     )
-    solved = totals[:, :, 0:2] / (totals[:, :, 2:3] + epsilon)
+    denom = jnp.matmul(left_power, left_hot.T, precision=table_precision) + jnp.matmul(
+        right_power, right_hot.T, precision=table_precision
+    )
+    solved = numer / (denom + epsilon)
     return (1.0 - step_size) * gains + step_size * solved
 
 

time: 75.5 us -> 75.9 us (level)
  waiting for transfers between devices: 36.8 us -> 35.5 us
  matrix products: 6.07 us -> 7.32 us
    dot_general x0 -> x4, matrix products: none -> 2.52 us  [the longest x2 1.27 us: solve(): jnp.matmul(right_power, right_hot.T, precision=table_precision)]
    ppermute x4, waiting for transfers between devices: 19 us -> 17.8 us  [sum_over_dir(): lax.ppermute(total, 'dir', [(i, i ^ mask) for i in range(count)])]
    dot_general x2, matrix products: 1.89 us -> 1.08 us  [corrupt(): jnp.matmul(gains, right_hot, precision=table_precision)[:, None]]
  transfers between devices with their start and end apart: 8 -> 8, of which waited for: 6 -> 6; matrix products, arithmetic and copies ran while one was open for 0% -> 2% of each run, Pallas kernels for 0% -> 0%
where the time goes in v15:
time: 75.9 us; the launch traced here: 75.5 us
  waiting for transfers between devices  35.5 us (47%)
  starting transfers between devices  26.1 us (34%)
  matrix products  7.32 us (10%)
  local copies, waits for them, and re-layouts  3.23 us (4%)
  other arithmetic  2.32 us (3%)
  between operations  0.95 us (1%)
    ppermute x2, waiting for transfers between devices, extended(): lax.ppermute(head, axis, [(i + 1, i) for i in range(ends)])  17.8 us
    ppermute x4, waiting for transfers between devices, sum_over_dir(): lax.ppermute(total, 'dir', [(i, i ^ mask) for i in range(count)])  17.8 us
    ppermute x4, starting transfers between devices, sum_over_dir(): lax.ppermute(total, 'dir', [(i, i ^ mask) for i in range(count)])  10.6 us
    ppermute x2, starting transfers between devices, extended(): lax.ppermute(tail, axis, [(i, i + 1) for i in range(ends)])  9.66 us
    ppermute x2, starting transfers between devices, extended(): lax.ppermute(head, axis, [(i + 1, i) for i in range(ends)])  5.84 us
    unnamed x13, local copies, waits for them, and re-layouts  2.29 us
  transfers between devices with their start and end apart: 8, of which 6 were waited for; matrix products, arithmetic and copies ran while one was open for 2% of the time, Pallas kernels for 0%

profile of v15, /device:TPU:254, one launch (start us, length us, event | category | flops | bytes accessed | tf_op | source)
XLA Modules:
  0.0 75.5 jit_solution(18177283773974827567)
XLA Ops:
  0.6 0.9 %slice_reduce_fusion = (s32[2850]{0:T(1024)S(1)}, s32[2850]{0:T(1024)S(1)}) fusion(s32[2,2850]{1,0:T(2,128)} %param.11), kind=kLoop, calls=%fused_computation.133 | loop fusion | bytes 45600 | tf_op jit(solution)/shard_map/slice | solution.py:45
  1.5 0.5 convolution_bitcast_fusion.2
  2.1 0.5 convolution_bitcast_fusion.3
  2.6 0.4 copy-done
  3.1 0.1 multiply_add_fusion.9
  3.2 0.1 multiply_subtract_fusion.8
  3.3 0.2 fusion.38
  3.6 2.1 %collective-permute-start = (f32[2,1,2,2,2850]{4,3,2,1,0:T(2,128)S(1)}, f32[2,1,2,2,2850]{4,3,2,1,0:T(2,128)S(1)}, u32[]{:S(2)}, u32[]{:S(2)}) collective-permute-start(f32[2,1,2,2,2850]{4,3,2,1,0:T(2,128)S(1)} %bitcast.79), channel_id=1, source_target_pairs={{0,128},{128,0},{256,384},{384,256},{1,129},{129,1},{257,385},{385... | collective-permute-start | bytes 273608 | tf_op jit(solution)/shard_map/ppermute | solution.py:37
  5.6 1.3 %collective-permute-done = f32[2,1,2,2,2850]{4,3,2,1,0:T(2,128)S(1)} collective-permute-done((f32[2,1,2,2,2850]{4,3,2,1,0:T(2,128)S(1)}, f32[2,1,2,2,2850]{4,3,2,1,0:T(2,128)S(1)}, u32[]{:S(2)}, u32[]{:S(2)}) %collective-permute-start) | collective-permute-done | bytes 91232 | tf_op jit(solution)/shard_map/ppermute | solution.py:37
  6.9 4.7 %collective-permute-start.1 = (f32[2,1,2,2,2850]{4,3,2,1,0:T(2,128)S(1)}, f32[2,1,2,2,2850]{4,3,2,1,0:T(2,128)S(1)}, u32[]{:S(2)}, u32[]{:S(2)}) collective-permute-start(f32[2,1,2,2,2850]{4,3,2,1,0:T(2,128)S(1)} %bitcast_add_fusion.1), channel_id=1, source_target_pairs={{0,256},{128,384},{256,0},{384,128},{1,257},{129,385},{257,1},{385... | collective-permute-start | bytes 273608 | tf_op jit(solution)/shard_map/ppermute | solution.py:37
  11.7 7.9 %collective-permute-done.1 = f32[2,1,2,2,2850]{4,3,2,1,0:T(2,128)S(1)} collective-permute-done((f32[2,1,2,2,2850]{4,3,2,1,0:T(2,128)S(1)}, f32[2,1,2,2,2850]{4,3,2,1,0:T(2,128)S(1)}, u32[]{:S(2)}, u32[]{:S(2)}) %collective-permute-start.1) | collective-permute-done | bytes 91232 | tf_op jit(solution)/shard_map/ppermute | solution.py:37
  19.6 0.1 fusion.37
  19.7 0.2 multiply_add_fusion.6
  19.9 0.6 fusion.25
  20.5 0.6 fusion.6
  21.1 0.1 multiply_subtract_fusion.6
  21.3 0.7 fusion.20
  22.0 0.7 fusion.4
  22.7 0.1 pad_maximum_fusion.8
  22.8 7.7 %collective-permute-start.2 = (f32[8,2,2,2,77]{4,0,3,2,1:T(8,128)S(1)}, f32[8,2,2,2,77]{4,0,3,2,1:T(8,128)S(1)}, u32[]{:S(2)}, u32[]{:S(2)}) collective-permute-start(f32[8,2,2,2,77]{4,0,3,2,1:T(8,128)S(1)} %pad_maximum_fusion.8), channel_id=1, source_target_pairs={{0,1},{1,2},{2,3},{3,4},{4,5},{5,6},{6,7},{7,8},{8,9},{9,10},{10,1... | collective-permute-start | bytes 59144 | tf_op jit(solution)/shard_map/ppermute | solution.py:24
  30.5 1.9 %collective-permute-start.3 = (f32[8,2,2,2,77]{4,0,3,2,1:T(8,128)S(1)}, f32[8,2,2,2,77]{4,0,3,2,1:T(8,128)S(1)}, u32[]{:S(2)}, u32[]{:S(2)}) collective-permute-start(f32[8,2,2,2,77]{4,0,3,2,1:T(8,128)S(1)} %pad_maximum_fusion.8), channel_id=1, source_target_pairs={{1,0},{2,1},{3,2},{4,3},{5,4},{6,5},{7,6},{8,7},{9,8},{10,9},{11,1... | collective-permute-start | bytes 59144 | tf_op jit(solution)/shard_map/ppermute | solution.py:26
  32.5 9.9 %collective-permute-done.3 = f32[8,2,2,2,77]{4,0,3,2,1:T(8,128)S(1)} collective-permute-done((f32[8,2,2,2,77]{4,0,3,2,1:T(8,128)S(1)}, f32[8,2,2,2,77]{4,0,3,2,1:T(8,128)S(1)}, u32[]{:S(2)}, u32[]{:S(2)}) %collective-permute-start.3) | collective-permute-done | bytes 19744 | tf_op jit(solution)/shard_map/ppermute | solution.py:26
  42.4 0.2 maximum_reduce_fusion.1
  42.5 0.7 copy-done.4
  43.2 0.1 fusion.87
  43.3 0.5 convolution_bitcast_fusion.1
  43.9 0.5 convolution_bitcast_fusion
  44.4 0.1 multiply_add_fusion.3
  44.6 0.1 multiply_subtract_fusion.3
  44.6 0.2 fusion.36
  44.9 1.9 %collective-permute-start.4 = (f32[2,1,2,2,2850]{4,3,2,1,0:T(2,128)S(1)}, f32[2,1,2,2,2850]{4,3,2,1,0:T(2,128)S(1)}, u32[]{:S(2)}, u32[]{:S(2)}) collective-permute-start(f32[2,1,2,2,2850]{4,3,2,1,0:T(2,128)S(1)} %bitcast.78), channel_id=1, source_target_pairs={{0,128},{128,0},{256,384},{384,256},{1,129},{129,1},{257,385},{385... | collective-permute-start | bytes 273608 | tf_op jit(solution)/shard_map/ppermute | solution.py:37
  46.8 0.6 fusion.23
  47.4 0.6 collective-permute-done.4
  48.1 1.9 %collective-permute-start.5 = (f32[2,1,2,2,2850]{4,3,2,1,0:T(2,128)S(1)}, f32[2,1,2,2,2850]{4,3,2,1,0:T(2,128)S(1)}, u32[]{:S(2)}, u32[]{:S(2)}) collective-permute-start(f32[2,1,2,2,2850]{4,3,2,1,0:T(2,128)S(1)} %bitcast_add_fusion), channel_id=1, source_target_pairs={{0,256},{128,384},{256,0},{384,128},{1,257},{129,385},{257,1},{385... | collective-permute-start | bytes 273608 | tf_op jit(solution)/shard_map/ppermute | solution.py:37
  50.0 0.6 fusion.5
  50.7 8.0 %collective-permute-done.5 = f32[2,1,2,2,2850]{4,3,2,1,0:T(2,128)S(1)} collective-permute-done((f32[2,1,2,2,2850]{4,3,2,1,0:T(2,128)S(1)}, f32[2,1,2,2,2850]{4,3,2,1,0:T(2,128)S(1)}, u32[]{:S(2)}, u32[]{:S(2)}) %collective-permute-start.5) | collective-permute-done | bytes 91232 | tf_op jit(solution)/shard_map/ppermute | solution.py:37
  58.7 0.1 add_subtract_fusion
  58.8 0.1 fusion.35
  58.9 0.5 copy-done.2
  59.4 0.1 multiply_add_fusion
  59.5 0.1 multiply_subtract_fusion.1
  59.7 0.7 fusion.17
  60.3 0.7 multiply_add_fusion.11
  61.0 1.9 %collective-permute-start.6 = (f32[8,2,2,2,76]{4,0,3,2,1:T(8,128)S(1)}, f32[8,2,2,2,76]{4,0,3,2,1:T(8,128)S(1)}, u32[]{:S(2)}, u32[]{:S(2)}) collective-permute-start(f32[8,2,2,2,76]{4,0,3,2,1:T(8,128)S(1)} %multiply_add_fusion.11), channel_id=1, source_target_pairs={{0,1},{1,2},{2,3},{3,4},{4,5},{5,6},{6,7},{7,8},{8,9},{9,10},{10,1... | collective-permute-start | bytes 58376 | tf_op jit(solution)/shard_map/ppermute | solution.py:24
  62.9 3.9 %collective-permute-start.7 = (f32[8,2,2,2,76]{4,0,3,2,1:T(8,128)S(1)}, f32[8,2,2,2,76]{4,0,3,2,1:T(8,128)S(1)}, u32[]{:S(2)}, u32[]{:S(2)}) collective-permute-start(f32[8,2,2,2,76]{4,0,3,2,1:T(8,128)S(1)} %multiply_add_fusion.11), channel_id=1, source_target_pairs={{1,0},{2,1},{3,2},{4,3},{5,4},{6,5},{7,6},{8,7},{9,8},{10,9},{11,1... | collective-permute-start | bytes 58376 | tf_op jit(solution)/shard_map/ppermute | solution.py:26
  66.9 7.9 %collective-permute-done.7 = f32[8,2,2,2,76]{4,0,3,2,1:T(8,128)S(1)} collective-permute-done((f32[8,2,2,2,76]{4,0,3,2,1:T(8,128)S(1)}, f32[8,2,2,2,76]{4,0,3,2,1:T(8,128)S(1)}, u32[]{:S(2)}, u32[]{:S(2)}) %collective-permute-start.7) | collective-permute-done | bytes 19488 | tf_op jit(solution)/shard_map/ppermute | solution.py:26
  74.7 0.1 fusion.82
  74.8 0.6 copy.17
  (17 shorter events, 0.3 us)
Async XLA Ops:
  0.6 0.9 %copy-start.5 = (f32[8,2,2,2,76]{4,3,2,1,0:T(2,128)S(1)}, f32[8,2,2,2,76]{4,3,2,1,0:T(2,128)}, u32[]{:S(2)}) copy-start(f32[8,2,2,2,76]{4,3,2,1,0:T(2,128)} %param.8) | copy-start | bytes 58372
  2.1 1.0 %copy-start = (bf16[8,2,1,2,2,2850]{5,4,3,2,1,0:T(2,128)(2,1)S(1)}, bf16[8,2,1,2,2,2850]{5,4,3,2,1,0:T(2,128)(2,1)}, u32[]{:S(2)}) copy-start(bf16[8,2,1,2,2,2850]{5,4,3,2,1,0:T(2,128)(2,1)} %param.7) | copy-start | bytes 1094404
  3.6 16.0 %copy-start.1 = (f32[2,1,2,2,2850]{4,3,2,1,0:T(2,128)S(1)}, f32[2,1,2,2,2850]{4,3,2,1,0:T(2,128)}, u32[]{:S(2)}) copy-start(f32[2,1,2,2,2850]{4,3,2,1,0:T(2,128)} %param.6) | copy-start | bytes 273604
  3.6 3.3 %collective-permute-start = (f32[2,1,2,2,2850]{4,3,2,1,0:T(2,128)S(1)}, f32[2,1,2,2,2850]{4,3,2,1,0:T(2,128)S(1)}, u32[]{:S(2)}, u32[]{:S(2)}) collective-permute-start(f32[2,1,2,2,2850]{4,3,2,1,0:T(2,128)S(1)} %bitcast.79), channel_id=1, source_target_pairs={{0,128},{128,0},{256,384},{384,256},{1,129},{129,1},{257,385},{385... | collective-permute-start | bytes 273608 | tf_op jit(solution)/shard_map/ppermute | solution.py:37
  6.9 12.6 %collective-permute-start.1 = (f32[2,1,2,2,2850]{4,3,2,1,0:T(2,128)S(1)}, f32[2,1,2,2,2850]{4,3,2,1,0:T(2,128)S(1)}, u32[]{:S(2)}, u32[]{:S(2)}) collective-permute-start(f32[2,1,2,2,2850]{4,3,2,1,0:T(2,128)S(1)} %bitcast_add_fusion.1), channel_id=1, source_target_pairs={{0,256},{128,384},{256,0},{384,128},{1,257},{129,385},{257,1},{385... | collective-permute-start | bytes 273608 | tf_op jit(solution)/shard_map/ppermute | solution.py:37
  21.9 0.7 copy-start.3
  22.8 9.7 %collective-permute-start.2 = (f32[8,2,2,2,77]{4,0,3,2,1:T(8,128)S(1)}, f32[8,2,2,2,77]{4,0,3,2,1:T(8,128)S(1)}, u32[]{:S(2)}, u32[]{:S(2)}) collective-permute-start(f32[8,2,2,2,77]{4,0,3,2,1:T(8,128)S(1)} %pad_maximum_fusion.8), channel_id=1, source_target_pairs={{0,1},{1,2},{2,3},{3,4},{4,5},{5,6},{6,7},{7,8},{8,9},{9,10},{10,1... | collective-permute-start | bytes 59144 | tf_op jit(solution)/shard_map/ppermute | solution.py:24
  30.5 11.8 %collective-permute-start.3 = (f32[8,2,2,2,77]{4,0,3,2,1:T(8,128)S(1)}, f32[8,2,2,2,77]{4,0,3,2,1:T(8,128)S(1)}, u32[]{:S(2)}, u32[]{:S(2)}) collective-permute-start(f32[8,2,2,2,77]{4,0,3,2,1:T(8,128)S(1)} %pad_maximum_fusion.8), channel_id=1, source_target_pairs={{1,0},{2,1},{3,2},{4,3},{5,4},{6,5},{7,6},{8,7},{9,8},{10,9},{11,1... | collective-permute-start | bytes 59144 | tf_op jit(solution)/shard_map/ppermute | solution.py:26
  42.5 0.7 copy-start.4
  44.9 3.2 %collective-permute-start.4 = (f32[2,1,2,2,2850]{4,3,2,1,0:T(2,128)S(1)}, f32[2,1,2,2,2850]{4,3,2,1,0:T(2,128)S(1)}, u32[]{:S(2)}, u32[]{:S(2)}) collective-permute-start(f32[2,1,2,2,2850]{4,3,2,1,0:T(2,128)S(1)} %bitcast.78), channel_id=1, source_target_pairs={{0,128},{128,0},{256,384},{384,256},{1,129},{129,1},{257,385},{385... | collective-permute-start | bytes 273608 | tf_op jit(solution)/shard_map/ppermute | solution.py:37
  48.1 10.6 %collective-permute-start.5 = (f32[2,1,2,2,2850]{4,3,2,1,0:T(2,128)S(1)}, f32[2,1,2,2,2850]{4,3,2,1,0:T(2,128)S(1)}, u32[]{:S(2)}, u32[]{:S(2)}) collective-permute-start(f32[2,1,2,2,2850]{4,3,2,1,0:T(2,128)S(1)} %bitcast_add_fusion), channel_id=1, source_target_pairs={{0,256},{128,384},{256,0},{384,128},{1,257},{129,385},{257,1},{385... | collective-permute-start | bytes 273608 | tf_op jit(solution)/shard_map/ppermute | solution.py:37
  58.8 0.6 copy-start.2
  61.0 5.9 %collective-permute-start.6 = (f32[8,2,2,2,76]{4,0,3,2,1:T(8,128)S(1)}, f32[8,2,2,2,76]{4,0,3,2,1:T(8,128)S(1)}, u32[]{:S(2)}, u32[]{:S(2)}) collective-permute-start(f32[8,2,2,2,76]{4,0,3,2,1:T(8,128)S(1)} %multiply_add_fusion.11), channel_id=1, source_target_pairs={{0,1},{1,2},{2,3},{3,4},{4,5},{5,6},{6,7},{7,8},{8,9},{9,10},{10,1... | collective-permute-start | bytes 58376 | tf_op jit(solution)/shard_map/ppermute | solution.py:24
  62.9 11.8 %collective-permute-start.7 = (f32[8,2,2,2,76]{4,0,3,2,1:T(8,128)S(1)}, f32[8,2,2,2,76]{4,0,3,2,1:T(8,128)S(1)}, u32[]{:S(2)}, u32[]{:S(2)}) collective-permute-start(f32[8,2,2,2,76]{4,0,3,2,1:T(8,128)S(1)} %multiply_add_fusion.11), channel_id=1, source_target_pairs={{1,0},{2,1},{3,2},{4,3},{5,4},{6,5},{7,6},{8,7},{9,8},{10,9},{11,1... | collective-permute-start | bytes 58376 | tf_op jit(solution)/shard_map/ppermute | solution.py:26
